TPU v7x, 128 devices: a whole 4x4x4 slice. The times are simulated.
128 devices in a mesh: visit: 8 (over y, core), patch: 16 (over x, z).
Axes of the slice: x: 4, y: 4, z: 4, core: 2. Of those that a mesh axis runs over, the one named last changes fastest.
Arguments:
- pieces: float32 [1024, 512, 512], P(('visit', 'patch')), may hold values from -60 to 60
- ref_patch: float32 [16, 512, 512], P('patch', 'visit'), may hold values from -6 to 6
- piece_patch: int32 [1024], P(('visit', 'patch')), may hold values from 0 to 15, as said below
- piece_visit: int32 [1024], P(('visit', 'patch')), may hold values from 0 to 3, as said below
- anchors: int32 [1024, 2], P(('visit', 'patch')), may hold values from 0 to 3584
- shifts: int32 [1024, 2], P(('visit', 'patch')), may hold values from -2 to 2
- phases: float32 [1024, 2], P(('visit', 'patch')), may hold values from 0 to 1
Outputs:
- matched: float32 [1024, 512, 512], P(('visit', 'patch'))
- coefficients: float32 [32, 17, 17], P('visit')
Inputs may be any that keep to these rules, and one draw needn't show every extreme that they name: `piece_patch`: among the 8 pieces of one device at most 2 name the same patch; for each index of the visit axis one patch, drawn from the seed, is named by exactly 2 pieces of every device of that index. `piece_visit`: among the 8 pieces of one device each value occurs exactly 8 / 4 times.
All inputs are finite; a program needn't handle non-finite values.
Results may differ from a plain program's by a relative error of at most 0.0003.
Values sent between devices are 32-bit elements; how exact they have to be, the bound alone decides.
No kernel may reach another device: no remote copies, remote signals or barrier semaphores. Data moves between devices by JAX's collectives and lax.ppermute only.
A program may use at most 192 MiB of HBM per device.

v0:
```python
import jax
import jax.numpy as jnp
from jax import lax
from jax.sharding import PartitionSpec as P

VIS_DEV = 4
TERMS = 17
TILE = 4096


exact_mode = lax.Precision.HIGHEST


def lanczos_batch(band_shift, sub_phase, side_len):
    positions = jnp.arange(side_len, dtype=jnp.int32)
    whole = positions[None, :, None] + band_shift[:, None, None] - positions[None, None, :]
    offset = whole.astype(sub_phase.dtype) + sub_phase[:, None, None]
    weight = jnp.sinc(offset) * jnp.sinc(offset / 3.0)
    return jnp.where(jnp.abs(offset) < 3.0, weight, jnp.zeros_like(weight))


def warp_batch(slab_images, row_shift, col_shift, row_phase, col_phase):
    side_len = slab_images.shape[1]
    left_matrix = lanczos_batch(row_shift, row_phase, side_len)
    middle = jnp.einsum("kia,kab->kib", left_matrix, slab_images, precision=exact_mode)
    right_matrix = lanczos_batch(col_shift, col_phase, side_len)
    return jnp.einsum("kib,kjb->kij", middle, right_matrix, precision=exact_mode)


def chebyshev_rows(first_pixel, side_len):
    pixels = (first_pixel + jnp.arange(side_len, dtype=jnp.int32)).astype(jnp.float32)
    coordinate = (2.0 * pixels + 1.0) / TILE - 1.0
    orders = jnp.arange(TERMS, dtype=jnp.int32).astype(jnp.float32)
    return jnp.cos(orders[:, None] * jnp.arccos(coordinate)[None, :])


def basis_pair(anchor_pairs, side_len):
    row_basis = jax.vmap(lambda first_pixel: chebyshev_rows(first_pixel, side_len))(
        anchor_pairs[:, 0]
    )
    col_basis = jax.vmap(lambda first_pixel: chebyshev_rows(first_pixel, side_len))(
        anchor_pairs[:, 1]
    )
    return (row_basis, col_basis)


def project_terms(differences, anchor_pairs):
    row_basis, col_basis = basis_pair(anchor_pairs, differences.shape[1])
    middle = jnp.einsum("mtp,mpq->mtq", row_basis, differences, precision=exact_mode)
    return jnp.einsum("mtq,muq->mtu", middle, col_basis, precision=exact_mode)


def body(pieces, ref_patch, piece_patch, piece_visit, anchors, shifts, phases):
    piece_count = pieces.shape[0]
    side_len = pieces.shape[1]
    patch_count = lax.axis_size("patch")
    full_ref = lax.all_gather(ref_patch, "visit", axis=1, tiled=True)
    visit_slots = jnp.arange(VIS_DEV, dtype=jnp.int32)
    own_onehot = (piece_visit[:, None] == visit_slots[None, :]).astype(jnp.float32)
    warped_all = warp_batch(pieces, shifts[:, 0], shifts[:, 1], phases[:, 0], phases[:, 1])
    ref_block = lax.all_gather(full_ref, "patch", axis=0, tiled=True)
    block_count = ref_block.shape[0]
    match_table = (
        piece_patch[:, None] == jnp.arange(block_count, dtype=jnp.int32)[None, :]
    ).astype(jnp.float32)
    own_diffs = warped_all - jnp.einsum("kb,bij->kij", match_table, ref_block, precision=exact_mode)
    partial_value = project_terms(own_diffs, anchors)
    local_sums = jnp.einsum("kv,ktu->vtu", own_onehot, partial_value, precision=exact_mode)
    totals = lax.psum(local_sums, "patch")
    coefficients = totals / float(patch_count * (piece_count // VIS_DEV) * side_len * side_len)
    row_basis, col_basis = basis_pair(anchors, side_len)
    chosen = jnp.einsum("kv,vtu->ktu", own_onehot, coefficients, precision=exact_mode)
    middle = jnp.einsum("ktp,ktu->kpu", row_basis, chosen, precision=exact_mode)
    fitted = jnp.einsum("kpu,kuq->kpq", middle, col_basis, precision=exact_mode)
    return (own_diffs - fitted, coefficients)


def solution(mesh):
    return jax.shard_map(
        body,
        mesh=mesh,
        in_specs=(
            P(("visit", "patch"), None, None),
            P("patch", "visit", None),
            P(("visit", "patch")),
            P(("visit", "patch")),
            P(("visit", "patch"), None),
            P(("visit", "patch"), None),
            P(("visit", "patch"), None),
        ),
        out_specs=(P(("visit", "patch"), None, None), P("visit", None, None)),
        check_vma=False,
    )
```

profile of v0, /device:TPU:0, one launch (start us, length us, event | category | flops | bytes accessed | tf_op | source)
XLA Modules:
  0.0 283.2 jit_solution(9602985950847562917)
XLA Ops:
  7.2 0.0 all-gather.3.cloned.1.call-start
  7.2 1.7 copy.11
  8.9 0.0 all-gather.3.cloned.1.call-update
  8.9 0.0 all-gather.5.cloned.1.call-start
  9.0 27.1 %all-gather.3.cloned.1.call-done = f32[1,512,512]{2,0,1:T(1,128)} async-done(((f32[1,64,512]{2,0,1:T(1,128)}), f32[1,512,512]{2,0,1:T(1,128)}) %all-gather.3.cloned.1.call-update) | async-done | bytes 1048592 | tf_op jit(solution)/shard_map/all_gather | solution.py:57
  36.0 2.3 copy.12
  38.3 0.0 all-gather.5.cloned.1.call-update
  38.3 0.8 slice_bitcast_fusion
  39.1 0.8 slice_bitcast_fusion.3
  39.9 0.8 slice_bitcast_fusion.2
  40.6 0.1 iota_add_fusion
  40.7 0.1 iota_add_fusion.1
  40.8 0.7 sqrt_atan2_fusion
  41.5 37.1 %fusion.64 = f32[8,512,512]{2,1,0:T(8,128)S(1)} fusion(f32[8,512,512]{2,1,0:T(8,128)} %param.8, f32[8]{0:T(128)S(1)} %get-tuple-element.8, s32[8,512]{1,0:T(8,128)S(1)} %iota_add_fusion.1), kind=kOutput, calls=%fused_computation.110 | convolution fusion | flops 13037993984 | bytes 16793632 | tf_op jit(solution)/shard_map/kia,kab->kib/dot_general | solution.py:25
  78.6 0.0 copy-start.5
  78.7 39.2 %fusion.59 = f32[8,512,512]{2,1,0:T(8,128)} fusion(f32[8,512,512]{2,1,0:T(8,128)S(1)} %fusion.64, f32[8]{0:T(128)S(1)} %get-tuple-element.7, s32[8,512]{1,0:T(8,128)S(1)} %iota_add_fusion), kind=kOutput, calls=%fused_computation.105 | convolution fusion | flops 13037993984 | bytes 16793632 | tf_op jit(solution)/shard_map/kib,kjb->kij/dot_general | solution.py:27
  117.9 31.9 %all-gather.5.cloned.1.call-done = f32[16,512,512]{2,1,0:T(8,128)} async-done(((f32[1,512,512]{2,1,0:T(8,128)}), f32[16,512,512]{2,1,0:T(8,128)}) %all-gather.5.cloned.1.call-update) | async-done | bytes 16777232 | tf_op jit(solution)/shard_map/all_gather | solution.py:61
  149.8 0.0 copy-done.5
  149.8 0.0 copy-start.1
  149.8 22.9 %fusion = f32[8,512,512]{2,0,1:T(8,128)S(1)} fusion(f32[16,512,512]{2,1,0:T(8,128)} %all-gather.5.cloned.1.call-done, s32[8]{0:T(128)S(1)} %copy-done.5), kind=kOutput, calls=%fused_computation | convolution fusion | flops 402653312 | bytes 25165856 | tf_op jit(solution)/shard_map/kb,bij->kij/dot_general | solution.py:66
  172.7 0.0 copy-start
  172.7 0.0 copy-done.1
  172.7 0.0 copy-start.2
  172.7 0.0 copy-start.4
  172.7 9.3 %fusion.100 = f32[8,17,512]{2,1,0:T(8,128)S(1)} fusion(f32[8,512,512]{2,1,0:T(8,128)S(1)} %copy-done.1, f32[8,512,512]{2,0,1:T(8,128)S(1)} %fusion, f32[8,512]{1,0:T(8,128)S(1)} %get-tuple-element.10, f32[17]{0:T(128)S(1)} %iota_convert_fusion), kind=kOutput, calls=%fused_computation.142 | convolution fusion | flops 429985792 | bytes 17072196 | tf_op jit(solution)/shard_map/mtp,mpq->mtq/dot_general | solution.py:49
  182.1 0.0 copy-done
  182.1 0.0 copy-done.2
  182.1 1.8 fusion.101
  183.9 0.0 copy-done.4
  183.9 0.2 fusion.112
  184.1 72.7 %psum.7 = f32[4,17,17]{2,0,1:T(4,128)S(1)} all-reduce(f32[4,17,17]{2,0,1:T(4,128)S(1)} %fusion.112), channel_id=1, replica_groups=mesh['visit'=8,'patch'=16] {'patch'}, use_global_device_ids=true, to_apply=%region_0.2 | all-reduce | flops 1156 | bytes 9248 | tf_op jit(solution)/shard_map/psum | solution.py:69
  256.8 0.0 copy-start.3
  256.8 0.2 fusion.118
  257.0 2.3 fusion.102
  259.4 16.8 %convolution_subtract_fusion = f32[8,512,512]{2,1,0:T(8,128)} fusion(f32[8,512,17]{1,2,0:T(8,128)S(1)} %fusion.102, f32[8,512,512]{2,1,0:T(8,128)} %fusion.59, f32[8,512,512]{2,0,1:T(8,128)} %copy-done, f32[8,512]{1,0:T(8,128)S(1)} %copy-done.2, f32[17]{0:T(128)S(1)} %iota_convert_fusion), kind=kOutput, calls=%fused_computation.141 | convolution fusion | flops 432082944 | bytes 25460804 | tf_op jit(solution)/shard_map/kpu,kuq->kpq/dot_general | solution.py:74
  276.2 0.0 copy-done.3
  (2 shorter events, 0.0 us)
Async XLA Ops:
  7.2 28.9 %all-gather.3.cloned.1.call-start = ((), (), s32[]{:S(2)}) async-start(), calls=%async_computation | async-start | bytes 1179648 | tf_op jit(solution)/shard_map/all_gather | solution.py:57
  8.9 140.9 %all-gather.5.cloned.1.call-start = ((), (), s32[]{:S(2)}) async-start(), calls=%async_computation.1 | async-start | bytes 17825792 | tf_op jit(solution)/shard_map/all_gather | solution.py:61
  78.6 71.2 %copy-start.5 = (s32[8]{0:T(128)S(1)}, s32[8]{0:T(128)}, u32[]{:S(2)}) copy-start(s32[8]{0:T(128)} %param.10) | copy-start | bytes 100
  149.8 22.9 %copy-start.1 = (f32[8,512,512]{2,1,0:T(8,128)S(1)}, f32[8,512,512]{2,1,0:T(8,128)}, u32[]{:S(2)}) copy-start(f32[8,512,512]{2,1,0:T(8,128)} %fusion.59) | copy-start | bytes 25165828
  172.7 9.4 %copy-start = (f32[8,512,512]{2,0,1:T(8,128)}, f32[8,512,512]{2,0,1:T(8,128)S(1)}, u32[]{:S(2)}) copy-start(f32[8,512,512]{2,0,1:T(8,128)S(1)} %fusion) | copy-start | bytes 25165828
  172.7 9.4 %copy-start.2 = (f32[8,512]{1,0:T(8,128)S(1)}, f32[8,512]{1,0:T(8,128)}, u32[]{:S(2)}) copy-start(f32[8,512]{1,0:T(8,128)} %get-tuple-element.9) | copy-start | bytes 49156
  172.7 11.2 %copy-start.4 = (s32[8]{0:T(128)S(1)}, s32[8]{0:T(128)}, u32[]{:S(2)}) copy-start(s32[8]{0:T(128)} %param.11) | copy-start | bytes 100
  256.8 19.4 %copy-start.3 = (f32[4,17,17]{2,0,1:T(4,128)}, f32[4,17,17]{2,0,1:T(4,128)S(1)}, u32[]{:S(2)}) copy-start(f32[4,17,17]{2,0,1:T(4,128)S(1)} %broadcast_multiply_fusion) | copy-start | bytes 13876
Sparse Core Ops, SparseCore 0:
  10.3 25.7 all-gather.2
  38.5 111.2 all-gather.4
where the time goes:
time: 289 us; the launch traced here: 283 us
  matrix products  130 us (45%)
  blocking collectives  72.7 us (25%)
  waiting for transfers between devices  59 us (20%)
  between operations  14.4 us (5%)
  local copies, waits for them, and re-layouts  6.27 us (2%)
    psum x1, blocking collectives, body(): totals = lax.psum(local_sums, 'patch')  72.7 us
    dot_general x1, matrix products, warp_batch(): jnp.einsum('kib,kjb->kij', middle, right_matrix, precision=exact_mode)  39.2 us
    dot_general x1, matrix products, warp_batch(): jnp.einsum('kia,kab->kib', left_matrix, slab_images, precision=exact_mode)  37.1 us
    all_gather x1, waiting for transfers between devices, body(): ref_block = lax.all_gather(full_ref, 'patch', axis=0, tiled=True)  31.9 us
    all_gather x1, waiting for transfers between devices, body(): full_ref = lax.all_gather(ref_patch, 'visit', axis=1, tiled=True)  27.1 us
    dot_general x1, matrix products, body(): jnp.einsum('kb,bij->kij', match_table, ref_block, precision=exact_mode)  22.9 us
    dot_general x1, matrix products, body(): fitted = jnp.einsum('kpu,kuq->kpq', middle, col_basis, precision=exact_mode)  16.8 us
    dot_general x1, matrix products, project_terms(): jnp.einsum('mtp,mpq->mtq', row_basis, differences, precision=exact_mode)  9.34 us
  transfers between devices with their start and end apart: 2, of which 2 were waited for; matrix products, arithmetic and copies ran while one was open for 28% of the time, Pallas kernels for 0%

commit v1 on v0

v1 whole, which is shorter than its diff:
```python
import jax
import jax.numpy as jnp
from jax import lax
from jax.sharding import PartitionSpec as P

VIS_DEV = 4
TERMS = 17
TILE = 4096
TAPS = 6


exact_mode = lax.Precision.HIGHEST
warp_mode = lax.Precision.HIGH


def tap_weights(sub_phase):
    distance = jnp.arange(-3, 3, dtype=jnp.int32)
    offset = distance.astype(sub_phase.dtype)[None, :] + sub_phase[:, None]
    weight = jnp.sinc(offset) * jnp.sinc(offset / 3.0)
    return jnp.where(jnp.abs(offset) < 3.0, weight, jnp.zeros_like(weight))


def lanczos_batch(band_shift, sub_phase, side_len):
    positions = jnp.arange(side_len, dtype=jnp.int32)
    whole = positions[None, :, None] + band_shift[:, None, None] - positions[None, None, :]
    weights = tap_weights(sub_phase)
    matrix = jnp.zeros(whole.shape, sub_phase.dtype)
    for tap in range(TAPS):
        matrix = jnp.where(whole == tap - 3, weights[:, tap][:, None, None], matrix)
    return matrix


def warp_batch(slab_images, row_shift, col_shift, row_phase, col_phase):
    side_len = slab_images.shape[1]
    left_matrix = lanczos_batch(row_shift, row_phase, side_len)
    middle = jnp.einsum("kia,kab->kib", left_matrix, slab_images, precision=warp_mode)
    right_matrix = lanczos_batch(col_shift, col_phase, side_len)
    return jnp.einsum("kib,kjb->kij", middle, right_matrix, precision=warp_mode)


def chebyshev_rows(first_pixel, side_len):
    pixels = (first_pixel + jnp.arange(side_len, dtype=jnp.int32)).astype(jnp.float32)
    coordinate = (2.0 * pixels + 1.0) / TILE - 1.0
    orders = jnp.arange(TERMS, dtype=jnp.int32).astype(jnp.float32)
    return jnp.cos(orders[:, None] * jnp.arccos(coordinate)[None, :])


def basis_pair(anchor_pairs, side_len):
    row_basis = jax.vmap(lambda first_pixel: chebyshev_rows(first_pixel, side_len))(
        anchor_pairs[:, 0]
    )
    col_basis = jax.vmap(lambda first_pixel: chebyshev_rows(first_pixel, side_len))(
        anchor_pairs[:, 1]
    )
    return (row_basis, col_basis)


def project_terms(differences, row_basis, col_basis):
    middle = jnp.einsum("mtp,mpq->mtq", row_basis, differences, precision=exact_mode)
    return jnp.einsum("mtq,muq->mtu", middle, col_basis, precision=exact_mode)


def butterfly_sum(value, axis_name):
    count = lax.axis_size(axis_name)
    stride = 1
    while stride < count:
        pairs = [(i, i ^ stride) for i in range(count)]
        value = value + lax.ppermute(value, axis_name, pairs)
        stride *= 2
    return value


def body(pieces, ref_patch, piece_patch, piece_visit, anchors, shifts, phases):
    piece_count = pieces.shape[0]
    side_len = pieces.shape[1]
    patch_count = lax.axis_size("patch")
    gathered = lax.all_gather(ref_patch, ("patch", "visit"), axis=0, tiled=True)
    ref_block = gathered.reshape(patch_count, side_len, side_len)
    visit_slots = jnp.arange(VIS_DEV, dtype=jnp.int32)
    own_onehot = (piece_visit[:, None] == visit_slots[None, :]).astype(jnp.float32)
    warped_all = warp_batch(pieces, shifts[:, 0], shifts[:, 1], phases[:, 0], phases[:, 1])
    own_diffs = warped_all - jnp.take(ref_block, piece_patch, axis=0)
    row_basis, col_basis = basis_pair(anchors, side_len)
    partial_value = project_terms(own_diffs, row_basis, col_basis)
    local_sums = jnp.einsum("kv,ktu->vtu", own_onehot, partial_value, precision=exact_mode)
    totals = butterfly_sum(local_sums, "patch")
    coefficients = totals / float(patch_count * (piece_count // VIS_DEV) * side_len * side_len)
    chosen = jnp.take(coefficients, piece_visit, axis=0)
    middle = jnp.einsum("ktp,ktu->kpu", row_basis, chosen, precision=warp_mode)
    fitted = jnp.einsum("kpu,kuq->kpq", middle, col_basis, precision=warp_mode)
    return (own_diffs - fitted, coefficients)


def solution(mesh):
    return jax.shard_map(
        body,
        mesh=mesh,
        in_specs=(
            P(("visit", "patch"), None, None),
            P("patch", "visit", None),
            P(("visit", "patch")),
            P(("visit", "patch")),
            P(("visit", "patch"), None),
            P(("visit", "patch"), None),
            P(("visit", "patch"), None),
        ),
        out_specs=(P(("visit", "patch"), None, None), P("visit", None, None)),
        check_vma=False,
    )
```

time: 289 us -> 166 us (0.57); the launches traced: 283 us -> 166 us
  matrix products: 130 us -> 45.5 us
  blocking collectives: 72.7 us -> 0 us
  waiting for transfers between devices: 59 us -> 79.1 us
  local copies, waits for them, and re-layouts: 6.27 us -> 16.5 us
  starting transfers between devices: 0.08 us -> 8.62 us
    dot_general x6 -> x4, matrix products: 119 us -> 38.1 us  [the longest x1 13.9 us: warp_batch(): return jnp.einsum('kib,kjb->kij', middle, right_matrix, precision=warp_mode)]
    psum x1 -> x0, blocking collectives: 72.7 us -> none  [body(): totals = lax.psum(local_sums, 'patch')]
    gather x0 -> x2, local copies, waits for them, and re-layouts: none -> 10.8 us  [the longest x1 10.2 us: body(): own_diffs = warped_all - jnp.take(ref_block, piece_patch, axis=0)]
    ppermute x0 -> x4, waiting for transfers between devices: none -> 10.5 us  [butterfly_sum(): value = value + lax.ppermute(value, axis_name, pairs)]
    all_gather x2 -> x1, waiting for transfers between devices: 59 us -> 67.9 us  [body(): gathered = lax.all_gather(ref_patch, ('patch', 'visit'), axis=0, tiled=True)]
    ppermute x0 -> x4, starting transfers between devices: none -> 8.58 us  [butterfly_sum(): value = value + lax.ppermute(value, axis_name, pairs)]
    dot_general x1, matrix products: 9.34 us -> 5.33 us  [project_terms(): jnp.einsum('mtp,mpq->mtq', row_basis, differences, precision=exact_mode)]
  transfers between devices with their start and end apart: 2 -> 5, of which waited for: 2 -> 5; matrix products, arithmetic and copies ran while one was open for 28% -> 11% of each run, Pallas kernels for 0% -> 0%
where the time goes in v1:
time: 166 us
  waiting for transfers between devices  79.1 us (48%)
  matrix products  45.5 us (27%)
  local copies, waits for them, and re-layouts  16.5 us (10%)
  between operations  14.2 us (9%)
  starting transfers between devices  8.62 us (5%)
  other arithmetic  1.73 us (1%)
    all_gather x1, waiting for transfers between devices, body(): gathered = lax.all_gather(ref_patch, ('patch', 'visit'), axis=0, tiled=True)  67.9 us
    dot_general x1, matrix products, warp_batch(): return jnp.einsum('kib,kjb->kij', middle, right_matrix, precision=warp_mode)  13.9 us
    dot_general x1, matrix products, warp_batch(): jnp.einsum('kia,kab->kib', left_matrix, slab_images, precision=warp_mode)  13.8 us
    ppermute x4, waiting for transfers between devices, butterfly_sum(): value = value + lax.ppermute(value, axis_name, pairs)  10.5 us
    gather x1, local copies, waits for them, and re-layouts, body(): own_diffs = warped_all - jnp.take(ref_block, piece_patch, axis=0)  10.2 us
    dot_general x1, matrix products, body(): fitted = jnp.einsum('kpu,kuq->kpq', middle, col_basis, precision=warp_mode)  8.83 us
    ppermute x4, starting transfers between devices, butterfly_sum(): value = value + lax.ppermute(value, axis_name, pairs)  8.58 us
    dot_general x1, matrix products, project_terms(): jnp.einsum('mtp,mpq->mtq', row_basis, differences, precision=exact_mode)  5.33 us
  transfers between devices with their start and end apart: 5, of which 5 were waited for; matrix products, arithmetic and copies ran while one was open for 11% of the time, Pallas kernels for 0%

profile of v1, /device:TPU:0, one launch (start us, length us, event | category | flops | bytes accessed | tf_op | source)
XLA Modules:
  0.0 165.6 jit_solution(12295364038009174455)
XLA Ops:
  7.2 0.0 all-gather.2.cloned.1.call-start
  7.2 0.7 all-gather.2.cloned.1.call-update
  7.9 0.7 compare_select_fusion.1
  8.6 0.7 compare_and_fusion.1
  9.2 0.8 slice_bitcast_fusion.8
  10.0 0.8 slice_bitcast_fusion.9
  10.8 0.8 slice_bitcast_fusion
  11.5 0.1 fusion.119
  11.6 0.1 iota_add_fusion
  11.7 0.2 sqrt_atan2_fusion
  11.9 13.8 %fusion.13 = f32[8,512,512]{2,1,0:T(8,128)} fusion(f32[8,512,512]{2,1,0:T(8,128)} %param.8, f32[8]{0:T(128)S(1)} %get-tuple-element.10, f32[8]{0:T(128)S(1)} %get-tuple-element.11, f32[8]{0:T(128)S(1)} %get-tuple-element.12, f32[8]{0:T(128)S(1)} %get-tuple-element.13, f32[8]{0:T(128)S(1)} %get-tuple-element.14, f32[8]{0:T(128)S(1)} %get-tuple-element.9, ...), kind=kOutput, calls=%fused_computation.17 | convolution fusion | flops 6469713920 | bytes 16793792 | tf_op jit(solution)/shard_map/kia,kab->kib/dot_general | solution.py:36
  25.6 67.9 %all-gather.2.cloned.1.call-done = f32[128,64,512]{2,1,0:T(8,128)} async-done(((f32[1,64,512]{2,1,0:T(8,128)}), f32[128,64,512]{2,1,0:T(8,128)}) %all-gather.2.cloned.1.call-update) | async-done | bytes 16777232 | tf_op jit(solution)/shard_map/all_gather | solution.py:77
  93.6 10.2 %gather_fusion = f32[8,512,512]{2,1,0:T(8,128)} fusion(f32[16,512,512]{2,1,0:T(8,128)} %bitcast.45, s32[1024]{0:T(1024)S(1)} %pad_clamp_fusion.1), kind=kCustom, calls=%fused_computation | custom fusion | bytes 16777248 | tf_op jit(solution)/shard_map/jit(_take)/gather | solution.py:82
  103.8 13.9 %select_subtract_fusion = f32[8,512,512]{2,1,0:T(8,128)S(1)} fusion(f32[8,512,512]{2,1,0:T(8,128)} %gather_fusion, pred[8]{0:T(512)(128)(4,1)S(1)} %compare_and_fusion.1, f32[8,512,512]{2,1,0:T(8,128)} %fusion.13, f32[8]{0:T(128)S(1)} %get-tuple-element.4, f32[8]{0:T(128)S(1)} %get-tuple-element.5, f32[8]{0:T(128)S(1)} %get-tuple-element.6, ...), kind=kOutput, calls=%fused_computation.2 | convolution fusion | flops 6473908224 | bytes 25182408 | tf_op jit(solution)/shard_map/kib,kjb->kij/dot_general | solution.py:38
  117.7 0.0 copy-start
  117.7 0.0 copy-start.2
  117.8 3.4 %copy-done = f32[8,512,512]{2,1,0:T(8,128)} copy-done((f32[8,512,512]{2,1,0:T(8,128)}, f32[8,512,512]{2,1,0:T(8,128)S(1)}, u32[]{:S(2)}) %copy-start) | copy-done | bytes 8388632
  121.1 5.3 %fusion.70 = f32[8,17,512]{2,1,0:T(8,128)S(1)} fusion(f32[8,512,512]{2,1,0:T(8,128)S(1)} %select_subtract_fusion, f32[8,512]{1,0:T(8,128)S(1)} %get-tuple-element.26, f32[17]{0:T(128)S(1)} %iota_convert_fusion), kind=kOutput, calls=%fused_computation.64 | convolution fusion | flops 427888640 | bytes 8683588 | tf_op jit(solution)/shard_map/mtp,mpq->mtq/dot_general | solution.py:59
  126.5 1.8 %fusion.68 = f32[8,17,17]{2,1,0:T(8,128)S(1)} fusion(f32[8,17,512]{2,1,0:T(8,128)S(1)} %fusion.70, f32[8,512]{1,0:T(8,128)S(1)} %get-tuple-element.25, f32[17]{0:T(128)S(1)} %iota_convert_fusion), kind=kOutput, calls=%fused_computation.61 | convolution fusion | flops 14274560 | bytes 304228 | tf_op jit(solution)/shard_map/mtq,muq->mtu/dot_general | solution.py:60
  128.3 0.0 copy-done.2
  128.3 0.2 fusion.80
  128.5 1.2 collective-permute-start
  129.7 2.8 %collective-permute-done = f32[4,17,17]{2,0,1:T(4,128)S(1)} collective-permute-done((f32[4,17,17]{2,0,1:T(4,128)S(1)}, f32[4,17,17]{2,0,1:T(4,128)S(1)}, u32[]{:S(2)}, u32[]{:S(2)}) %collective-permute-start) | collective-permute-done | bytes 4656 | tf_op jit(solution)/shard_map/ppermute | solution.py:68
  132.5 2.8 %collective-permute-start.1 = (f32[4,17,17]{2,0,1:T(4,128)S(1)}, f32[4,17,17]{2,0,1:T(4,128)S(1)}, u32[]{:S(2)}, u32[]{:S(2)}) collective-permute-start(f32[4,17,17]{2,0,1:T(4,128)S(1)} %add.227), channel_id=1, source_target_pairs={{0,2},{1,3},{2,0},{3,1},{4,6},{5,7},{6,4},{7,5},{8,10},{9,11},{10,... | collective-permute-start | bytes 13880 | tf_op jit(solution)/shard_map/ppermute | solution.py:68
  135.3 2.8 %collective-permute-done.1 = f32[4,17,17]{2,0,1:T(4,128)S(1)} collective-permute-done((f32[4,17,17]{2,0,1:T(4,128)S(1)}, f32[4,17,17]{2,0,1:T(4,128)S(1)}, u32[]{:S(2)}, u32[]{:S(2)}) %collective-permute-start.1) | collective-permute-done | bytes 4656 | tf_op jit(solution)/shard_map/ppermute | solution.py:68
  138.1 1.6 collective-permute-start.2
  139.6 2.5 %collective-permute-done.2 = f32[4,17,17]{2,0,1:T(4,128)S(1)} collective-permute-done((f32[4,17,17]{2,0,1:T(4,128)S(1)}, f32[4,17,17]{2,0,1:T(4,128)S(1)}, u32[]{:S(2)}, u32[]{:S(2)}) %collective-permute-start.2) | collective-permute-done | bytes 4656 | tf_op jit(solution)/shard_map/ppermute | solution.py:68
  142.1 3.1 %collective-permute-start.3 = (f32[4,17,17]{2,0,1:T(4,128)S(1)}, f32[4,17,17]{2,0,1:T(4,128)S(1)}, u32[]{:S(2)}, u32[]{:S(2)}) collective-permute-start(f32[4,17,17]{2,0,1:T(4,128)S(1)} %add.229), channel_id=1, source_target_pairs={{0,8},{1,9},{2,10},{3,11},{4,12},{5,13},{6,14},{7,15},{8,0},{9,1},... | collective-permute-start | bytes 13880 | tf_op jit(solution)/shard_map/ppermute | solution.py:68
  145.2 2.4 %collective-permute-done.3 = f32[4,17,17]{2,0,1:T(4,128)S(1)} collective-permute-done((f32[4,17,17]{2,0,1:T(4,128)S(1)}, f32[4,17,17]{2,0,1:T(4,128)S(1)}, u32[]{:S(2)}, u32[]{:S(2)}) %collective-permute-start.3) | collective-permute-done | bytes 4656 | tf_op jit(solution)/shard_map/ppermute | solution.py:68
  147.6 0.0 copy-start.1
  147.7 0.6 gather_fusion.1
  148.2 1.7 %fusion.69 = f32[8,512,17]{1,2,0:T(8,128)S(1)} fusion(f32[8,512]{1,0:T(8,128)S(1)} %get-tuple-element.26, f32[17]{0:T(128)S(1)} %iota_convert_fusion, f32[8,17,17]{2,1,0:T(8,128)S(1)} %gather_fusion.1, pred[8]{0:T(512)(128)(4,1)S(1)} %compare_and_fusion), kind=kOutput, calls=%fused_computation.63 | convolution fusion | flops 7174408 | bytes 304236 | tf_op jit(solution)/shard_map/ktp,ktu->kpu/dot_general | solution.py:89
  149.9 8.8 %convolution_subtract_fusion = f32[8,512,512]{2,1,0:T(8,128)} fusion(f32[8,512,512]{2,1,0:T(8,128)} %copy-done, f32[8,512,17]{1,2,0:T(8,128)S(1)} %fusion.69, f32[8,512]{1,0:T(8,128)S(1)} %get-tuple-element.25, f32[17]{0:T(128)S(1)} %iota_convert_fusion), kind=kOutput, calls=%fused_computation.59 | convolution fusion | flops 216076288 | bytes 17072196 | tf_op jit(solution)/shard_map/kpu,kuq->kpq/dot_general | solution.py:90
  158.7 0.0 copy-done.1
  (13 shorter events, 0.1 us)
Async XLA Ops:
  7.2 86.4 %all-gather.2.cloned.1.call-start = ((), (), s32[]{:S(2)}) async-start(), calls=%async_computation | async-start | bytes 16908288 | tf_op jit(solution)/shard_map/all_gather | solution.py:77
  117.7 3.4 %copy-start = (f32[8,512,512]{2,1,0:T(8,128)}, f32[8,512,512]{2,1,0:T(8,128)S(1)}, u32[]{:S(2)}) copy-start(f32[8,512,512]{2,1,0:T(8,128)S(1)} %select_subtract_fusion) | copy-start | bytes 25165828
  117.7 10.6 %copy-start.2 = (s32[8]{0:T(128)S(1)}, s32[8]{0:T(128)}, u32[]{:S(2)}) copy-start(s32[8]{0:T(128)} %param.11) | copy-start | bytes 100
  128.5 4.0 %collective-permute-start = (f32[4,17,17]{2,0,1:T(4,128)S(1)}, f32[4,17,17]{2,0,1:T(4,128)S(1)}, u32[]{:S(2)}, u32[]{:S(2)}) collective-permute-start(f32[4,17,17]{2,0,1:T(4,128)S(1)} %fusion.80), channel_id=1, source_target_pairs={{0,1},{1,0},{2,3},{3,2},{4,5},{5,4},{6,7},{7,6},{8,9},{9,8},{10,11... | collective-permute-start | bytes 13880 | tf_op jit(solution)/shard_map/ppermute | solution.py:68
  132.5 5.5 %collective-permute-start.1 = (f32[4,17,17]{2,0,1:T(4,128)S(1)}, f32[4,17,17]{2,0,1:T(4,128)S(1)}, u32[]{:S(2)}, u32[]{:S(2)}) collective-permute-start(f32[4,17,17]{2,0,1:T(4,128)S(1)} %add.227), channel_id=1, source_target_pairs={{0,2},{1,3},{2,0},{3,1},{4,6},{5,7},{6,4},{7,5},{8,10},{9,11},{10,... | collective-permute-start | bytes 13880 | tf_op jit(solution)/shard_map/ppermute | solution.py:68
  138.1 4.0 %collective-permute-start.2 = (f32[4,17,17]{2,0,1:T(4,128)S(1)}, f32[4,17,17]{2,0,1:T(4,128)S(1)}, u32[]{:S(2)}, u32[]{:S(2)}) collective-permute-start(f32[4,17,17]{2,0,1:T(4,128)S(1)} %add.228), channel_id=1, source_target_pairs={{0,4},{1,5},{2,6},{3,7},{4,0},{5,1},{6,2},{7,3},{8,12},{9,13},{10,... | collective-permute-start | bytes 13880 | tf_op jit(solution)/shard_map/ppermute | solution.py:68
  142.1 5.5 %collective-permute-start.3 = (f32[4,17,17]{2,0,1:T(4,128)S(1)}, f32[4,17,17]{2,0,1:T(4,128)S(1)}, u32[]{:S(2)}, u32[]{:S(2)}) collective-permute-start(f32[4,17,17]{2,0,1:T(4,128)S(1)} %add.229), channel_id=1, source_target_pairs={{0,8},{1,9},{2,10},{3,11},{4,12},{5,13},{6,14},{7,15},{8,0},{9,1},... | collective-permute-start | bytes 13880 | tf_op jit(solution)/shard_map/ppermute | solution.py:68
  147.6 11.1 %copy-start.1 = (f32[4,17,17]{2,0,1:T(4,128)}, f32[4,17,17]{2,0,1:T(4,128)S(1)}, u32[]{:S(2)}) copy-start(f32[4,17,17]{2,0,1:T(4,128)S(1)} %add_multiply_fusion) | copy-start | bytes 13876
Sparse Core Ops, SparseCore 0:
  11.1 82.4 all-gather.1

commit v2 on v1

--- a/solution.py
+++ b/solution.py
@@ -1,6 +1,7 @@
 import jax
 import jax.numpy as jnp
 from jax import lax
+from jax.sharding import Mesh
 from jax.sharding import PartitionSpec as P
 
 VIS_DEV = 4
@@ -8,6 +9,9 @@
 TILE = 4096
 TAPS = 6
 
+VISIT_PARTS = ("vy", "vc")
+PATCH_PARTS = ("px", "pz")
+PIECE_AXES = VISIT_PARTS + PATCH_PARTS
 
 exact_mode = lax.Precision.HIGHEST
 warp_mode = lax.Precision.HIGH
@@ -60,30 +64,50 @@
     return jnp.einsum("mtq,muq->mtu", middle, col_basis, precision=exact_mode)
 
 
-def butterfly_sum(value, axis_name):
+def ring_sum(value, axis_name):
     count = lax.axis_size(axis_name)
-    stride = 1
-    while stride < count:
-        pairs = [(i, i ^ stride) for i in range(count)]
-        value = value + lax.ppermute(value, axis_name, pairs)
-        stride *= 2
-    return value
+    me = lax.axis_index(axis_name)
+    received = [value]
+    for step in range(1, count):
+        pairs = [(i, (i + step) % count) for i in range(count)]
+        received.append(lax.ppermute(value, axis_name, pairs))
+    stacked = jnp.stack(received)
+    total = None
+    for source in range(count):
+        term = lax.dynamic_index_in_dim(stacked, (me - source) % count, 0, keepdims=False)
+        total = term if total is None else total + term
+    return total
 
 
 def body(pieces, ref_patch, piece_patch, piece_visit, anchors, shifts, phases):
     piece_count = pieces.shape[0]
     side_len = pieces.shape[1]
-    patch_count = lax.axis_size("patch")
-    gathered = lax.all_gather(ref_patch, ("patch", "visit"), axis=0, tiled=True)
-    ref_block = gathered.reshape(patch_count, side_len, side_len)
+    patch_count = lax.axis_size(PATCH_PARTS)
+    y_count = lax.axis_size("vy")
+    core_count = lax.axis_size("vc")
+    slab_rows = ref_patch.shape[1]
+    half = lax.all_gather(ref_patch, PATCH_PARTS + ("vy",), axis=0, tiled=True)
+    other = lax.ppermute(half, "vc", [(0, 1), (1, 0)])
+    half = half.reshape(patch_count, y_count, slab_rows, side_len)
+    other = other.reshape(patch_count, y_count, slab_rows, side_len)
+    core = lax.axis_index("vc")
+
+    warped_all = warp_batch(pieces, shifts[:, 0], shifts[:, 1], phases[:, 0], phases[:, 1])
+    warped_all = lax.optimization_barrier(warped_all)
+
+    own_rows = jnp.take(half, piece_patch, axis=0)
+    other_rows = jnp.take(other, piece_patch, axis=0)
+    first = jnp.where(core == 0, own_rows, other_rows)
+    second = jnp.where(core == 0, other_rows, own_rows)
+    ref_rows = jnp.stack([first, second], axis=2).reshape(piece_count, side_len, side_len)
+    own_diffs = warped_all - ref_rows
+
+    row_basis, col_basis = basis_pair(anchors, side_len)
+    partial_value = project_terms(own_diffs, row_basis, col_basis)
     visit_slots = jnp.arange(VIS_DEV, dtype=jnp.int32)
     own_onehot = (piece_visit[:, None] == visit_slots[None, :]).astype(jnp.float32)
-    warped_all = warp_batch(pieces, shifts[:, 0], shifts[:, 1], phases[:, 0], phases[:, 1])
-    own_diffs = warped_all - jnp.take(ref_block, piece_patch, axis=0)
-    row_basis, col_basis = basis_pair(anchors, side_len)
-    partial_value = project_terms(own_diffs, row_basis, col_basis)
     local_sums = jnp.einsum("kv,ktu->vtu", own_onehot, partial_value, precision=exact_mode)
-    totals = butterfly_sum(local_sums, "patch")
+    totals = ring_sum(ring_sum(local_sums, "pz"), "px")
     coefficients = totals / float(patch_count * (piece_count // VIS_DEV) * side_len * side_len)
     chosen = jnp.take(coefficients, piece_visit, axis=0)
     middle = jnp.einsum("ktp,ktu->kpu", row_basis, chosen, precision=warp_mode)
@@ -92,18 +116,24 @@
 
 
 def solution(mesh):
+    visit_size = mesh.shape["visit"]
+    patch_size = mesh.shape["patch"]
+    fine = Mesh(
+        mesh.devices.reshape(visit_size // 2, 2, 4, patch_size // 4),
+        PIECE_AXES,
+    )
     return jax.shard_map(
         body,
-        mesh=mesh,
+        mesh=fine,
         in_specs=(
-            P(("visit", "patch"), None, None),
-            P("patch", "visit", None),
-            P(("visit", "patch")),
-            P(("visit", "patch")),
-            P(("visit", "patch"), None),
-            P(("visit", "patch"), None),
-            P(("visit", "patch"), None),
+            P(PIECE_AXES, None, None),
+            P(PATCH_PARTS, VISIT_PARTS, None),
+            P(PIECE_AXES),
+            P(PIECE_AXES),
+            P(PIECE_AXES, None),
+            P(PIECE_AXES, None),
+            P(PIECE_AXES, None),
         ),
-        out_specs=(P(("visit", "patch"), None, None), P("visit", None, None)),
+        out_specs=(P(PIECE_AXES, None, None), P(VISIT_PARTS, None, None)),
         check_vma=False,
     )

time: 166 us -> 194 us (1.17)
  other arithmetic: 1.73 us -> 20.7 us
  waiting for transfers between devices: 79.1 us -> 89.6 us
  starting transfers between devices: 8.62 us -> 10.8 us
  local copies, waits for them, and re-layouts: 16.5 us -> 14.4 us
    all_gather x1, waiting for transfers between devices: 67.9 us -> 83.9 us  [body(): half = lax.all_gather(ref_patch, PATCH_PARTS + ('vy',), axis=0, tiled=True)]
    sub x0 -> x1, other arithmetic: none -> 11.3 us  [body(): own_diffs = warped_all - ref_rows]
    another operation x0 -> x4, other arithmetic: none -> 8.97 us  [the longest x2 8.9 us: body(): jnp.stack([first, second], axis=2).reshape(piece_count, side_len, side_len)]
    ppermute x4 -> x7, waiting for transfers between devices: 10.5 us -> 5.01 us  [the longest x6 5.01 us: ring_sum(): received.append(lax.ppermute(value, axis_name, pairs))]
    unnamed x6 -> x8, local copies, waits for them, and re-layouts: 3.39 us -> 0.03 us
    dot_general x1, matrix products: 5.33 us -> 7.65 us  [project_terms(): jnp.einsum('mtp,mpq->mtq', row_basis, differences, precision=exact_mode)]
    ppermute x4 -> x7, starting transfers between devices: 8.58 us -> 10.8 us  [the longest x6 10.8 us: ring_sum(): received.append(lax.ppermute(value, axis_name, pairs))]
    dot_general x1, matrix products: 13.8 us -> 11.6 us  [warp_batch(): jnp.einsum('kia,kab->kib', left_matrix, slab_images, precision=warp_mode)]
  transfers between devices with their start and end apart: 5 -> 8, of which waited for: 5 -> 5; matrix products, arithmetic and copies ran while one was open for 11% -> 16% of each run, Pallas kernels for 0% -> 0%
where the time goes in v2:
time: 194 us; the launch traced here: 193 us
  waiting for transfers between devices  89.6 us (46%)
  matrix products  43.7 us (23%)
  other arithmetic  20.7 us (11%)
  local copies, waits for them, and re-layouts  14.4 us (7%)
  between operations  14.2 us (7%)
  starting transfers between devices  10.8 us (6%)
    all_gather x1, waiting for transfers between devices, body(): half = lax.all_gather(ref_patch, PATCH_PARTS + ('vy',), axis=0, tiled=True)  83.9 us
    dot_general x1, matrix products, warp_batch(): return jnp.einsum('kib,kjb->kij', middle, right_matrix, precision=warp_mode)  11.9 us
    dot_general x1, matrix products, warp_batch(): jnp.einsum('kia,kab->kib', left_matrix, slab_images, precision=warp_mode)  11.6 us
    sub x1, other arithmetic, body(): own_diffs = warped_all - ref_rows  11.3 us
    ppermute x6, starting transfers between devices, ring_sum(): received.append(lax.ppermute(value, axis_name, pairs))  10.8 us
    another operation x2, other arithmetic, body(): jnp.stack([first, second], axis=2).reshape(piece_count, side_len, side_len)  8.9 us
    dot_general x1, matrix products, body(): fitted = jnp.einsum('kpu,kuq->kpq', middle, col_basis, precision=warp_mode)  8.84 us
    dot_general x1, matrix products, project_terms(): jnp.einsum('mtp,mpq->mtq', row_basis, differences, precision=exact_mode)  7.65 us
  transfers between devices with their start and end apart: 8, of which 5 were waited for; matrix products, arithmetic and copies ran while one was open for 16% of the time, Pallas kernels for 0%

profile of v2, /device:TPU:0, one launch (start us, length us, event | category | flops | bytes accessed | tf_op | source)
XLA Modules:
  0.0 193.4 jit_solution(5740085992215570644)
XLA Ops:
  7.2 0.0 all-gather.2.cloned.1.call-start
  7.2 0.7 all-gather.2.cloned.1.call-update
  7.9 83.9 %all-gather.2.cloned.1.call-done = f32[64,64,512]{2,1,0:T(8,128)} async-done(((f32[1,64,512]{2,1,0:T(8,128)}), f32[64,64,512]{2,1,0:T(8,128)}) %all-gather.2.cloned.1.call-update) | async-done | bytes 8388624 | tf_op jit(solution)/shard_map/all_gather | solution.py:89
  91.8 0.0 collective-permute-start
  91.8 0.8 slice_bitcast_fusion.8
  92.5 0.8 slice_bitcast_fusion.9
  93.3 0.1 fusion.117
  93.4 0.1 iota_add_fusion
  93.5 11.6 %fusion.13 = f32[8,512,512]{2,1,0:T(8,128)S(1)} fusion(f32[8,512,512]{2,1,0:T(8,128)} %param.10, f32[8]{0:T(128)S(1)} %get-tuple-element.30, f32[8]{0:T(128)S(1)} %get-tuple-element.29, f32[8]{0:T(128)S(1)} %get-tuple-element.28, f32[8]{0:T(128)S(1)} %get-tuple-element.27, f32[8]{0:T(128)S(1)} %get-tuple-element.26, f32[8]{0:T(128)S(1)} %get-tuple-element.31, ...), kind=kOutput, calls=%fused_computation.19 | convolution fusion | flops 6469713920 | bytes 16793792 | tf_op jit(solution)/shard_map/kia,kab->kib/dot_general | solution.py:40
  105.1 0.0 copy-start.3
  105.1 0.0 copy-start.2
  105.1 0.0 copy-start.1
  105.1 11.9 %fusion = f32[8,512,512]{2,1,0:T(8,128)} fusion(f32[8,512,512]{2,1,0:T(8,128)S(1)} %fusion.13, f32[8]{0:T(128)S(1)} %get-tuple-element.7, f32[8]{0:T(128)S(1)} %get-tuple-element.8, f32[8]{0:T(128)S(1)} %get-tuple-element.9, f32[8]{0:T(128)S(1)} %get-tuple-element.10, f32[8]{0:T(128)S(1)} %get-tuple-element.11, f32[8]{0:T(128)S(1)} %get-tuple-element.6, ...), kind=kOutput, calls=%fused_computation.5 | convolution fusion | flops 6469713920 | bytes 16793792 | tf_op jit(solution)/shard_map/kib,kjb->kij/dot_general | solution.py:42
  117.0 0.0 copy-done.3
  117.0 0.0 copy-done.2
  117.1 0.0 copy-done.1
  117.1 0.2 sqrt_atan2_fusion
  117.3 6.1 %gather_fusion.1 = f32[8,4,64,512]{3,2,1,0:T(8,128)} fusion(f32[16,4,64,512]{3,2,1,0:T(8,128)} %bitcast.65, s32[1024]{0:T(1024)S(1)} %pad_clamp_fusion.1), kind=kCustom, calls=%fused_computation.clone | custom fusion | bytes 8388640 | tf_op jit(solution)/shard_map/jit(_take)/gather | solution.py:98
  123.4 0.0 collective-permute-done
  123.4 6.2 %gather_fusion.2 = f32[8,4,64,512]{3,2,1,0:T(8,128)} fusion(f32[16,4,64,512]{3,2,1,0:T(8,128)} %bitcast.17, s32[1024]{0:T(1024)S(1)} %pad_clamp_fusion.1), kind=kCustom, calls=%fused_computation.1.clone | custom fusion | bytes 8388640 | tf_op jit(solution)/shard_map/jit(_take)/gather | solution.py:99
  129.6 4.6 %select_bitcast_fusion.1 = (f32[8,4,1,64,512]{4,3,2,1,0:T(8,128)S(1)}, f32[8,4,1,64,512]{4,3,2,1,0:T(8,128)S(1)}) fusion(f32[8,4,64,512]{3,2,1,0:T(8,128)} %gather_fusion.2, f32[8,4,64,512]{3,2,1,0:T(8,128)} %gather_fusion.1, pred[8]{0:T(512)(128)(4,1)S(1)} %compare_and_fusion, pred[]{:T(512)S(6)} %eq.86), kind=kLoop, calls=%fused_computation.34 | loop fusion | flops 4194304 | bytes 16777224 | tf_op jit(solution)/shard_map/stack | solution.py:102
  134.2 4.3 %pad_maximum_fusion = f32[8,4,2,64,512]{4,3,2,1,0:T(8,128)} fusion(f32[8,4,1,64,512]{4,3,2,1,0:T(8,128)S(1)} %get-tuple-element.5, f32[8,4,1,64,512]{4,3,2,1,0:T(8,128)S(1)} %get-tuple-element.4), kind=kLoop, calls=%fused_computation.3 | loop fusion | flops 2097152 | bytes 16777216 | tf_op jit(solution)/shard_map/stack | solution.py:102
  138.5 11.3 %bitcast_subtract_fusion = f32[8,512,512]{2,1,0:T(8,128)} fusion(f32[8,512,512]{2,1,0:T(8,128)} %fusion, f32[8,4,2,64,512]{4,3,2,1,0:T(8,128)} %pad_maximum_fusion), kind=kLoop, calls=%fused_computation.4 | loop fusion | flops 2097152 | bytes 25165824 | tf_op jit(solution)/shard_map/sub | solution.py:103
  149.7 7.6 %fusion.68 = f32[8,17,512]{2,1,0:T(8,128)S(1)} fusion(f32[8,512,512]{2,1,0:T(8,128)} %bitcast_subtract_fusion, f32[8,512]{1,0:T(8,128)S(1)} %get-tuple-element.35, f32[17]{0:T(128)S(1)} %iota_convert_fusion), kind=kOutput, calls=%fused_computation.68 | convolution fusion | flops 427888640 | bytes 8683588 | tf_op jit(solution)/shard_map/mtp,mpq->mtq/dot_general | solution.py:63
  157.4 1.8 fusion.66
  159.2 0.2 fusion.78
  159.4 1.4 collective-permute-start.1
  160.8 2.9 %collective-permute-start.2 = (f32[4,17,17]{2,0,1:T(4,128)S(1)}, f32[4,17,17]{2,0,1:T(4,128)S(1)}, u32[]{:S(2)}, u32[]{:S(2)}) collective-permute-start(f32[4,17,17]{2,0,1:T(4,128)S(1)} %fusion.78), channel_id=1, source_target_pairs={{0,2},{1,3},{2,0},{3,1},{4,6},{5,7},{6,4},{7,5},{8,10},{9,11},{10,... | collective-permute-start | bytes 13880 | tf_op jit(solution)/shard_map/ppermute | solution.py:73
  163.6 1.4 collective-permute-start.3
  165.0 0.0 collective-permute-done.1
  165.0 1.2 collective-permute-done.2
  166.2 1.3 collective-permute-done.3
  167.6 1.1 collective-permute-start.4
  168.7 2.7 %collective-permute-start.5 = (f32[4,17,17]{2,0,1:T(4,128)S(1)}, f32[4,17,17]{2,0,1:T(4,128)S(1)}, u32[]{:S(2)}, u32[]{:S(2)}) collective-permute-start(f32[4,17,17]{2,0,1:T(4,128)S(1)} %fusion.195), channel_id=1, source_target_pairs={{0,8},{4,12},{8,0},{12,4},{1,9},{5,13},{9,1},{13,5},{2,10},{6,14},... | collective-permute-start | bytes 13880 | tf_op jit(solution)/shard_map/ppermute | solution.py:73
  171.4 1.5 collective-permute-start.6
  172.9 0.0 collective-permute-done.4
  172.9 1.3 collective-permute-done.5
  174.1 1.2 collective-permute-done.6
  175.4 0.0 copy-start
  175.4 0.6 gather_fusion
  176.0 1.7 fusion.67
  177.7 8.8 %convolution_subtract_fusion = f32[8,512,512]{2,1,0:T(8,128)} fusion(f32[8,512,512]{2,1,0:T(8,128)} %bitcast_subtract_fusion, f32[8,512,17]{1,2,0:T(8,128)S(1)} %fusion.67, f32[8,512]{1,0:T(8,128)S(1)} %get-tuple-element.34, f32[17]{0:T(128)S(1)} %iota_convert_fusion), kind=kOutput, calls=%fused_computation.63 | convolution fusion | flops 216076288 | bytes 17072196 | tf_op jit(solution)/shard_map/kpu,kuq->kpq/dot_general | solution.py:114
  186.5 0.0 copy-done
  (16 shorter events, 0.2 us)
Async XLA Ops:
  7.2 84.6 %all-gather.2.cloned.1.call-start = ((), (), s32[]{:S(2)}) async-start(), calls=%async_computation | async-start | bytes 8519680 | tf_op jit(solution)/shard_map/all_gather | solution.py:89
  91.8 31.7 %collective-permute-start = (f32[64,64,512]{2,1,0:T(8,128)}, f32[64,64,512]{2,1,0:T(8,128)}, u32[]{:S(2)}, u32[]{:S(2)}) collective-permute-start(f32[64,64,512]{2,1,0:T(8,128)} %all-gather.2.cloned.1.call-done), channel_id=1, source_target_pairs={{0,16},{16,0},{1,17},{17,1},{2,18},{18,2},{3,19},{19,3},{4,20},{20... | collective-permute-start | bytes 25165832 | tf_op jit(solution)/shard_map/ppermute | solution.py:90
  105.1 11.9 %copy-start.3 = (s32[8]{0:T(128)S(1)}, s32[8]{0:T(128)}, u32[]{:S(2)}) copy-start(s32[8]{0:T(128)} %param.12) | copy-start | bytes 100
  105.1 11.9 %copy-start.2 = (s32[8]{0:T(128)S(1)}, s32[8]{0:T(128)}, u32[]{:S(2)}) copy-start(s32[8]{0:T(128)} %param.13) | copy-start | bytes 100
  105.1 12.0 %copy-start.1 = (s32[8,2]{0,1:T(2,128)S(1)}, s32[8,2]{0,1:T(2,128)}, u32[]{:S(2)}) copy-start(s32[8,2]{0,1:T(2,128)} %param.14) | copy-start | bytes 196
  159.4 5.6 %collective-permute-start.1 = (f32[4,17,17]{2,0,1:T(4,128)S(1)}, f32[4,17,17]{2,0,1:T(4,128)S(1)}, u32[]{:S(2)}, u32[]{:S(2)}) collective-permute-start(f32[4,17,17]{2,0,1:T(4,128)S(1)} %fusion.78), channel_id=1, source_target_pairs={{0,1},{1,2},{2,3},{3,0},{4,5},{5,6},{6,7},{7,4},{8,9},{9,10},{10,1... | collective-permute-start | bytes 13880 | tf_op jit(solution)/shard_map/ppermute | solution.py:73
  160.8 5.4 %collective-permute-start.2 = (f32[4,17,17]{2,0,1:T(4,128)S(1)}, f32[4,17,17]{2,0,1:T(4,128)S(1)}, u32[]{:S(2)}, u32[]{:S(2)}) collective-permute-start(f32[4,17,17]{2,0,1:T(4,128)S(1)} %fusion.78), channel_id=1, source_target_pairs={{0,2},{1,3},{2,0},{3,1},{4,6},{5,7},{6,4},{7,5},{8,10},{9,11},{10,... | collective-permute-start | bytes 13880 | tf_op jit(solution)/shard_map/ppermute | solution.py:73
  163.6 3.9 %collective-permute-start.3 = (f32[4,17,17]{2,0,1:T(4,128)S(1)}, f32[4,17,17]{2,0,1:T(4,128)S(1)}, u32[]{:S(2)}, u32[]{:S(2)}) collective-permute-start(f32[4,17,17]{2,0,1:T(4,128)S(1)} %fusion.78), channel_id=1, source_target_pairs={{0,3},{1,0},{2,1},{3,2},{4,7},{5,4},{6,5},{7,6},{8,11},{9,8},{10,9... | collective-permute-start | bytes 13880 | tf_op jit(solution)/shard_map/ppermute | solution.py:73
  167.6 5.2 %collective-permute-start.4 = (f32[4,17,17]{2,0,1:T(4,128)S(1)}, f32[4,17,17]{2,0,1:T(4,128)S(1)}, u32[]{:S(2)}, u32[]{:S(2)}) collective-permute-start(f32[4,17,17]{2,0,1:T(4,128)S(1)} %fusion.195), channel_id=1, source_target_pairs={{0,4},{4,8},{8,12},{12,0},{1,5},{5,9},{9,13},{13,1},{2,6},{6,10},{... | collective-permute-start | bytes 13880 | tf_op jit(solution)/shard_map/ppermute | solution.py:73
  168.7 5.4 %collective-permute-start.5 = (f32[4,17,17]{2,0,1:T(4,128)S(1)}, f32[4,17,17]{2,0,1:T(4,128)S(1)}, u32[]{:S(2)}, u32[]{:S(2)}) collective-permute-start(f32[4,17,17]{2,0,1:T(4,128)S(1)} %fusion.195), channel_id=1, source_target_pairs={{0,8},{4,12},{8,0},{12,4},{1,9},{5,13},{9,1},{13,5},{2,10},{6,14},... | collective-permute-start | bytes 13880 | tf_op jit(solution)/shard_map/ppermute | solution.py:73
  171.4 3.9 %collective-permute-start.6 = (f32[4,17,17]{2,0,1:T(4,128)S(1)}, f32[4,17,17]{2,0,1:T(4,128)S(1)}, u32[]{:S(2)}, u32[]{:S(2)}) collective-permute-start(f32[4,17,17]{2,0,1:T(4,128)S(1)} %fusion.195), channel_id=1, source_target_pairs={{0,12},{4,0},{8,4},{12,8},{1,13},{5,1},{9,5},{13,9},{2,14},{6,2},{... | collective-permute-start | bytes 13880 | tf_op jit(solution)/shard_map/ppermute | solution.py:73
  175.4 11.1 %copy-start = (f32[4,17,17]{2,0,1:T(4,128)}, f32[4,17,17]{2,0,1:T(4,128)S(1)}, u32[]{:S(2)}) copy-start(f32[4,17,17]{2,0,1:T(4,128)S(1)} %multiply_bitcast_fusion) | copy-start | bytes 13876
Sparse Core Ops, SparseCore 0:
  10.8 80.8 all-gather.1

commit v3 on v1

--- a/solution.py
+++ b/solution.py
@@ -79,6 +79,7 @@
     visit_slots = jnp.arange(VIS_DEV, dtype=jnp.int32)
     own_onehot = (piece_visit[:, None] == visit_slots[None, :]).astype(jnp.float32)
     warped_all = warp_batch(pieces, shifts[:, 0], shifts[:, 1], phases[:, 0], phases[:, 1])
+    warped_all = lax.optimization_barrier(warped_all)
     own_diffs = warped_all - jnp.take(ref_block, piece_patch, axis=0)
     row_basis, col_basis = basis_pair(anchors, side_len)
     partial_value = project_terms(own_diffs, row_basis, col_basis)

time: 166 us -> 155 us (0.934)
  waiting for transfers between devices: 79.1 us -> 71.3 us
  local copies, waits for them, and re-layouts: 16.5 us -> 12.2 us
  matrix products: 45.5 us -> 47.9 us
    all_gather x1, waiting for transfers between devices: 67.9 us -> 60.1 us  [body(): gathered = lax.all_gather(ref_patch, ('patch', 'visit'), axis=0, tiled=True)]
    dot_general x1, matrix products: 5.33 us -> 9.57 us  [project_terms(): jnp.einsum('mtp,mpq->mtq', row_basis, differences, precision=exact_mode)]
    unnamed x6 -> x8, local copies, waits for them, and re-layouts: 3.39 us -> 0.02 us
    dot_general x1, matrix products: 8.83 us -> 11.1 us  [body(): fitted = jnp.einsum('kpu,kuq->kpq', middle, col_basis, precision=warp_mode)]
    dot_general x1, matrix products: 13.8 us -> 11.6 us  [warp_batch(): jnp.einsum('kia,kab->kib', left_matrix, slab_images, precision=warp_mode)]
    dot_general x1, matrix products: 13.9 us -> 11.9 us  [warp_batch(): return jnp.einsum('kib,kjb->kij', middle, right_matrix, precision=warp_mode)]
  transfers between devices with their start and end apart: 5 -> 5, of which waited for: 5 -> 5; matrix products, arithmetic and copies ran while one was open for 11% -> 16% of each run, Pallas kernels for 0% -> 0%
where the time goes in v3:
time: 155 us
  waiting for transfers between devices  71.3 us (46%)
  matrix products  47.9 us (31%)
  between operations  14.2 us (9%)
  local copies, waits for them, and re-layouts  12.2 us (8%)
  starting transfers between devices  8.74 us (6%)
    all_gather x1, waiting for transfers between devices, body(): gathered = lax.all_gather(ref_patch, ('patch', 'visit'), axis=0, tiled=True)  60.1 us
    dot_general x1, matrix products, warp_batch(): return jnp.einsum('kib,kjb->kij', middle, right_matrix, precision=warp_mode)  11.9 us
    dot_general x1, matrix products, warp_batch(): jnp.einsum('kia,kab->kib', left_matrix, slab_images, precision=warp_mode)  11.6 us
    dot_general x1, matrix products, body(): fitted = jnp.einsum('kpu,kuq->kpq', middle, col_basis, precision=warp_mode)  11.1 us
    ppermute x4, waiting for transfers between devices, butterfly_sum(): value = value + lax.ppermute(value, axis_name, pairs)  10.5 us
    gather x1, local copies, waits for them, and re-layouts, body(): own_diffs = warped_all - jnp.take(ref_block, piece_patch, axis=0)  10.1 us
    dot_general x1, matrix products, project_terms(): jnp.einsum('mtp,mpq->mtq', row_basis, differences, precision=exact_mode)  9.57 us
    ppermute x4, starting transfers between devices, butterfly_sum(): value = value + lax.ppermute(value, axis_name, pairs)  8.7 us
  transfers between devices with their start and end apart: 5, of which 5 were waited for; matrix products, arithmetic and copies ran while one was open for 16% of the time, Pallas kernels for 0%

profile of v3, /device:TPU:0, one launch (start us, length us, event | category | flops | bytes accessed | tf_op | source)
XLA Modules:
  0.0 154.8 jit_solution(17485878688769065173)
XLA Ops:
  7.2 0.0 all-gather.2.cloned.1.call-start
  7.2 0.7 all-gather.2.cloned.1.call-update
  7.9 0.8 slice_bitcast_fusion.9
  8.7 0.8 slice_bitcast_fusion.8
  9.4 0.1 fusion.117
  9.5 0.1 iota_add_fusion
  9.6 11.6 %fusion.13 = f32[8,512,512]{2,1,0:T(8,128)S(1)} fusion(f32[8,512,512]{2,1,0:T(8,128)} %param.8, f32[8]{0:T(128)S(1)} %get-tuple-element.27, f32[8]{0:T(128)S(1)} %get-tuple-element.26, f32[8]{0:T(128)S(1)} %get-tuple-element.25, f32[8]{0:T(128)S(1)} %get-tuple-element.24, f32[8]{0:T(128)S(1)} %get-tuple-element.23, f32[8]{0:T(128)S(1)} %get-tuple-element.28, ...), kind=kOutput, calls=%fused_computation.17 | convolution fusion | flops 6469713920 | bytes 16793792 | tf_op jit(solution)/shard_map/kia,kab->kib/dot_general | solution.py:36
  21.3 0.0 copy-start.3
  21.3 0.0 copy-start.1
  21.3 11.9 %fusion = f32[8,512,512]{2,1,0:T(8,128)} fusion(f32[8,512,512]{2,1,0:T(8,128)S(1)} %fusion.13, f32[8]{0:T(128)S(1)} %get-tuple-element.4, f32[8]{0:T(128)S(1)} %get-tuple-element.5, f32[8]{0:T(128)S(1)} %get-tuple-element.6, f32[8]{0:T(128)S(1)} %get-tuple-element.7, f32[8]{0:T(128)S(1)} %get-tuple-element.8, f32[8]{0:T(128)S(1)} %get-tuple-element.3, ...), kind=kOutput, calls=%fused_computation.3 | convolution fusion | flops 6469713920 | bytes 16793792 | tf_op jit(solution)/shard_map/kib,kjb->kij/dot_general | solution.py:38
  33.2 0.0 copy-done.3
  33.2 0.0 copy-done.1
  33.3 0.1 sqrt_atan2_fusion
  33.4 0.1 sqrt_atan2_fusion.1
  33.5 60.1 %all-gather.2.cloned.1.call-done = f32[128,64,512]{2,1,0:T(8,128)} async-done(((f32[1,64,512]{2,1,0:T(8,128)}), f32[128,64,512]{2,1,0:T(8,128)}) %all-gather.2.cloned.1.call-update) | async-done | bytes 16777232 | tf_op jit(solution)/shard_map/all_gather | solution.py:77
  93.6 10.1 %gather_fusion = f32[8,512,512]{2,1,0:T(8,128)} fusion(f32[16,512,512]{2,1,0:T(8,128)} %bitcast.44, s32[1024]{0:T(1024)S(1)} %pad_clamp_fusion.1), kind=kCustom, calls=%fused_computation | custom fusion | bytes 16777248 | tf_op jit(solution)/shard_map/jit(_take)/gather | solution.py:83
  103.7 0.0 copy-start.2
  103.7 9.6 %fusion.66 = f32[8,17,512]{2,1,0:T(8,128)S(1)} fusion(f32[8,512,512]{2,1,0:T(8,128)} %fusion, f32[8,512,512]{2,1,0:T(8,128)} %gather_fusion, pred[8]{0:T(512)(128)(4,1)S(1)} %compare_and_fusion.1, f32[8,512]{1,0:T(8,128)S(1)} %sqrt_atan2_fusion.1, f32[17]{0:T(128)S(1)} %iota_convert_fusion), kind=kOutput, calls=%fused_computation.60 | convolution fusion | flops 432082944 | bytes 17072204 | tf_op jit(solution)/shard_map/mtp,mpq->mtq/dot_general | solution.py:59
  113.3 1.8 %fusion.67 = f32[8,17,17]{2,1,0:T(8,128)S(1)} fusion(f32[8,17,512]{2,1,0:T(8,128)S(1)} %fusion.66, f32[8,512]{1,0:T(8,128)S(1)} %sqrt_atan2_fusion, f32[17]{0:T(128)S(1)} %iota_convert_fusion), kind=kOutput, calls=%fused_computation.62 | convolution fusion | flops 14274560 | bytes 304228 | tf_op jit(solution)/shard_map/mtq,muq->mtu/dot_general | solution.py:60
  115.1 0.0 copy-done.2
  115.1 0.2 fusion.78
  115.3 1.2 collective-permute-start
  116.5 2.9 %collective-permute-done = f32[4,17,17]{2,0,1:T(4,128)S(1)} collective-permute-done((f32[4,17,17]{2,0,1:T(4,128)S(1)}, f32[4,17,17]{2,0,1:T(4,128)S(1)}, u32[]{:S(2)}, u32[]{:S(2)}) %collective-permute-start) | collective-permute-done | bytes 4656 | tf_op jit(solution)/shard_map/ppermute | solution.py:68
  119.3 2.8 %collective-permute-start.1 = (f32[4,17,17]{2,0,1:T(4,128)S(1)}, f32[4,17,17]{2,0,1:T(4,128)S(1)}, u32[]{:S(2)}, u32[]{:S(2)}) collective-permute-start(f32[4,17,17]{2,0,1:T(4,128)S(1)} %add.227), channel_id=1, source_target_pairs={{0,2},{1,3},{2,0},{3,1},{4,6},{5,7},{6,4},{7,5},{8,10},{9,11},{10,... | collective-permute-start | bytes 13880 | tf_op jit(solution)/shard_map/ppermute | solution.py:68
  122.1 2.8 %collective-permute-done.1 = f32[4,17,17]{2,0,1:T(4,128)S(1)} collective-permute-done((f32[4,17,17]{2,0,1:T(4,128)S(1)}, f32[4,17,17]{2,0,1:T(4,128)S(1)}, u32[]{:S(2)}, u32[]{:S(2)}) %collective-permute-start.1) | collective-permute-done | bytes 4656 | tf_op jit(solution)/shard_map/ppermute | solution.py:68
  124.9 1.7 %collective-permute-start.2 = (f32[4,17,17]{2,0,1:T(4,128)S(1)}, f32[4,17,17]{2,0,1:T(4,128)S(1)}, u32[]{:S(2)}, u32[]{:S(2)}) collective-permute-start(f32[4,17,17]{2,0,1:T(4,128)S(1)} %add.228), channel_id=1, source_target_pairs={{0,4},{1,5},{2,6},{3,7},{4,0},{5,1},{6,2},{7,3},{8,12},{9,13},{10,... | collective-permute-start | bytes 13880 | tf_op jit(solution)/shard_map/ppermute | solution.py:68
  126.6 2.5 %collective-permute-done.2 = f32[4,17,17]{2,0,1:T(4,128)S(1)} collective-permute-done((f32[4,17,17]{2,0,1:T(4,128)S(1)}, f32[4,17,17]{2,0,1:T(4,128)S(1)}, u32[]{:S(2)}, u32[]{:S(2)}) %collective-permute-start.2) | collective-permute-done | bytes 4656 | tf_op jit(solution)/shard_map/ppermute | solution.py:68
  129.1 3.1 %collective-permute-start.3 = (f32[4,17,17]{2,0,1:T(4,128)S(1)}, f32[4,17,17]{2,0,1:T(4,128)S(1)}, u32[]{:S(2)}, u32[]{:S(2)}) collective-permute-start(f32[4,17,17]{2,0,1:T(4,128)S(1)} %add.229), channel_id=1, source_target_pairs={{0,8},{1,9},{2,10},{3,11},{4,12},{5,13},{6,14},{7,15},{8,0},{9,1},... | collective-permute-start | bytes 13880 | tf_op jit(solution)/shard_map/ppermute | solution.py:68
  132.2 2.5 %collective-permute-done.3 = f32[4,17,17]{2,0,1:T(4,128)S(1)} collective-permute-done((f32[4,17,17]{2,0,1:T(4,128)S(1)}, f32[4,17,17]{2,0,1:T(4,128)S(1)}, u32[]{:S(2)}, u32[]{:S(2)}) %collective-permute-start.3) | collective-permute-done | bytes 4656 | tf_op jit(solution)/shard_map/ppermute | solution.py:68
  134.6 0.0 copy-start
  134.7 0.6 gather_fusion.1
  135.2 1.7 %fusion.68 = f32[8,512,17]{1,2,0:T(8,128)S(1)} fusion(f32[8,512]{1,0:T(8,128)S(1)} %sqrt_atan2_fusion.1, f32[17]{0:T(128)S(1)} %iota_convert_fusion, f32[8,17,17]{2,1,0:T(8,128)S(1)} %gather_fusion.1, pred[8]{0:T(512)(128)(4,1)S(1)} %compare_and_fusion), kind=kOutput, calls=%fused_computation.64 | convolution fusion | flops 7174408 | bytes 304236 | tf_op jit(solution)/shard_map/ktp,ktu->kpu/dot_general | solution.py:90
  136.9 11.1 %convolution_subtract_fusion = f32[8,512,512]{2,1,0:T(8,128)} fusion(f32[8,512,17]{1,2,0:T(8,128)S(1)} %fusion.68, f32[8,512,512]{2,1,0:T(8,128)} %fusion, f32[8,512,512]{2,1,0:T(8,128)} %gather_fusion, pred[8]{0:T(512)(128)(4,1)S(1)} %compare_and_fusion.1, f32[8,512]{1,0:T(8,128)S(1)} %sqrt_atan2_fusion, f32[17]{0:T(128)S(1)} %iota_convert_fusion), kind=kOutput, calls=%fused_computation.59 | convolution fusion | flops 220270592 | bytes 25460812 | tf_op jit(solution)/shard_map/kpu,kuq->kpq/dot_general | solution.py:91
  148.0 0.0 copy-done
  (15 shorter events, 0.1 us)
Async XLA Ops:
  7.2 86.5 %all-gather.2.cloned.1.call-start = ((), (), s32[]{:S(2)}) async-start(), calls=%async_computation | async-start | bytes 16908288 | tf_op jit(solution)/shard_map/all_gather | solution.py:77
  21.3 11.9 %copy-start.3 = (s32[8]{0:T(128)S(1)}, s32[8]{0:T(128)}, u32[]{:S(2)}) copy-start(s32[8]{0:T(128)} %param.10) | copy-start | bytes 100
  21.3 12.0 %copy-start.1 = (s32[8,2]{0,1:T(2,128)S(1)}, s32[8,2]{0,1:T(2,128)}, u32[]{:S(2)}) copy-start(s32[8,2]{0,1:T(2,128)} %param.12) | copy-start | bytes 196
  103.7 11.4 %copy-start.2 = (s32[8]{0:T(128)S(1)}, s32[8]{0:T(128)}, u32[]{:S(2)}) copy-start(s32[8]{0:T(128)} %param.11) | copy-start | bytes 100
  115.3 4.0 %collective-permute-start = (f32[4,17,17]{2,0,1:T(4,128)S(1)}, f32[4,17,17]{2,0,1:T(4,128)S(1)}, u32[]{:S(2)}, u32[]{:S(2)}) collective-permute-start(f32[4,17,17]{2,0,1:T(4,128)S(1)} %fusion.78), channel_id=1, source_target_pairs={{0,1},{1,0},{2,3},{3,2},{4,5},{5,4},{6,7},{7,6},{8,9},{9,8},{10,11... | collective-permute-start | bytes 13880 | tf_op jit(solution)/shard_map/ppermute | solution.py:68
  119.3 5.5 %collective-permute-start.1 = (f32[4,17,17]{2,0,1:T(4,128)S(1)}, f32[4,17,17]{2,0,1:T(4,128)S(1)}, u32[]{:S(2)}, u32[]{:S(2)}) collective-permute-start(f32[4,17,17]{2,0,1:T(4,128)S(1)} %add.227), channel_id=1, source_target_pairs={{0,2},{1,3},{2,0},{3,1},{4,6},{5,7},{6,4},{7,5},{8,10},{9,11},{10,... | collective-permute-start | bytes 13880 | tf_op jit(solution)/shard_map/ppermute | solution.py:68
  124.9 4.2 %collective-permute-start.2 = (f32[4,17,17]{2,0,1:T(4,128)S(1)}, f32[4,17,17]{2,0,1:T(4,128)S(1)}, u32[]{:S(2)}, u32[]{:S(2)}) collective-permute-start(f32[4,17,17]{2,0,1:T(4,128)S(1)} %add.228), channel_id=1, source_target_pairs={{0,4},{1,5},{2,6},{3,7},{4,0},{5,1},{6,2},{7,3},{8,12},{9,13},{10,... | collective-permute-start | bytes 13880 | tf_op jit(solution)/shard_map/ppermute | solution.py:68
  129.1 5.5 %collective-permute-start.3 = (f32[4,17,17]{2,0,1:T(4,128)S(1)}, f32[4,17,17]{2,0,1:T(4,128)S(1)}, u32[]{:S(2)}, u32[]{:S(2)}) collective-permute-start(f32[4,17,17]{2,0,1:T(4,128)S(1)} %add.229), channel_id=1, source_target_pairs={{0,8},{1,9},{2,10},{3,11},{4,12},{5,13},{6,14},{7,15},{8,0},{9,1},... | collective-permute-start | bytes 13880 | tf_op jit(solution)/shard_map/ppermute | solution.py:68
  134.6 13.4 %copy-start = (f32[4,17,17]{2,0,1:T(4,128)}, f32[4,17,17]{2,0,1:T(4,128)S(1)}, u32[]{:S(2)}) copy-start(f32[4,17,17]{2,0,1:T(4,128)S(1)} %add_multiply_fusion) | copy-start | bytes 13876
Sparse Core Ops, SparseCore 0:
  11.1 82.4 all-gather.1

commit v4 on v3

--- a/solution.py
+++ b/solution.py
@@ -56,7 +56,7 @@
 
 
 def project_terms(differences, row_basis, col_basis):
-    middle = jnp.einsum("mtp,mpq->mtq", row_basis, differences, precision=exact_mode)
+    middle = jnp.einsum("mtp,mpq->mtq", row_basis, differences, precision=warp_mode)
     return jnp.einsum("mtq,muq->mtu", middle, col_basis, precision=exact_mode)
 
 
@@ -81,6 +81,7 @@
     warped_all = warp_batch(pieces, shifts[:, 0], shifts[:, 1], phases[:, 0], phases[:, 1])
     warped_all = lax.optimization_barrier(warped_all)
     own_diffs = warped_all - jnp.take(ref_block, piece_patch, axis=0)
+    own_diffs = lax.optimization_barrier(own_diffs)
     row_basis, col_basis = basis_pair(anchors, side_len)
     partial_value = project_terms(own_diffs, row_basis, col_basis)
     local_sums = jnp.einsum("kv,ktu->vtu", own_onehot, partial_value, precision=exact_mode)

time: 155 us -> 160 us (1.032)
  other arithmetic: 0.5 us -> 11.8 us
  matrix products: 47.9 us -> 41.6 us
    sub x0 -> x1, other arithmetic: none -> 11.3 us  [body(): own_diffs = warped_all - jnp.take(ref_block, piece_patch, axis=0)]
    dot_general x1, matrix products: 9.57 us -> 5.6 us  [project_terms(): jnp.einsum('mtp,mpq->mtq', row_basis, differences, precision=warp_mode)]
    dot_general x1, matrix products: 11.1 us -> 8.83 us  [body(): fitted = jnp.einsum('kpu,kuq->kpq', middle, col_basis, precision=warp_mode)]
where the time goes in v4:
time: 160 us
  waiting for transfers between devices  71.5 us (45%)
  matrix products  41.6 us (26%)
  between operations  14.2 us (9%)
  local copies, waits for them, and re-layouts  12.2 us (8%)
  other arithmetic  11.8 us (7%)
  starting transfers between devices  8.74 us (5%)
    all_gather x1, waiting for transfers between devices, body(): gathered = lax.all_gather(ref_patch, ('patch', 'visit'), axis=0, tiled=True)  60.3 us
    dot_general x1, matrix products, warp_batch(): return jnp.einsum('kib,kjb->kij', middle, right_matrix, precision=warp_mode)  11.9 us
    dot_general x1, matrix products, warp_batch(): jnp.einsum('kia,kab->kib', left_matrix, slab_images, precision=warp_mode)  11.6 us
    sub x1, other arithmetic, body(): own_diffs = warped_all - jnp.take(ref_block, piece_patch, axis=0)  11.3 us
    ppermute x4, waiting for transfers between devices, butterfly_sum(): value = value + lax.ppermute(value, axis_name, pairs)  10.5 us
    gather x1, local copies, waits for them, and re-layouts, body(): own_diffs = warped_all - jnp.take(ref_block, piece_patch, axis=0)  10.1 us
    dot_general x1, matrix products, body(): fitted = jnp.einsum('kpu,kuq->kpq', middle, col_basis, precision=warp_mode)  8.83 us
    ppermute x4, starting transfers between devices, butterfly_sum(): value = value + lax.ppermute(value, axis_name, pairs)  8.7 us
  transfers between devices with their start and end apart: 5, of which 5 were waited for; matrix products, arithmetic and copies ran while one was open for 16% of the time, Pallas kernels for 0%

profile of v4, /device:TPU:0, one launch (start us, length us, event | category | flops | bytes accessed | tf_op | source)
XLA Modules:
  0.0 160.0 jit_solution(18102024841983512842)
XLA Ops:
  7.2 0.0 all-gather.2.cloned.1.call-start
  7.2 0.7 all-gather.2.cloned.1.call-update
  7.9 0.8 slice_bitcast_fusion.9
  8.7 0.8 slice_bitcast_fusion.8
  9.4 0.1 fusion.117
  9.5 0.1 iota_add_fusion
  9.6 11.6 %fusion.13 = f32[8,512,512]{2,1,0:T(8,128)S(1)} fusion(f32[8,512,512]{2,1,0:T(8,128)} %param.8, f32[8]{0:T(128)S(1)} %get-tuple-element.27, f32[8]{0:T(128)S(1)} %get-tuple-element.26, f32[8]{0:T(128)S(1)} %get-tuple-element.25, f32[8]{0:T(128)S(1)} %get-tuple-element.24, f32[8]{0:T(128)S(1)} %get-tuple-element.23, f32[8]{0:T(128)S(1)} %get-tuple-element.28, ...), kind=kOutput, calls=%fused_computation.17 | convolution fusion | flops 6469713920 | bytes 16793792 | tf_op jit(solution)/shard_map/kia,kab->kib/dot_general | solution.py:36
  21.3 0.0 copy-start.3
  21.3 0.0 copy-start.1
  21.3 11.9 %fusion = f32[8,512,512]{2,1,0:T(8,128)} fusion(f32[8,512,512]{2,1,0:T(8,128)S(1)} %fusion.13, f32[8]{0:T(128)S(1)} %get-tuple-element.4, f32[8]{0:T(128)S(1)} %get-tuple-element.5, f32[8]{0:T(128)S(1)} %get-tuple-element.6, f32[8]{0:T(128)S(1)} %get-tuple-element.7, f32[8]{0:T(128)S(1)} %get-tuple-element.8, f32[8]{0:T(128)S(1)} %get-tuple-element.3, ...), kind=kOutput, calls=%fused_computation.3 | convolution fusion | flops 6469713920 | bytes 16793792 | tf_op jit(solution)/shard_map/kib,kjb->kij/dot_general | solution.py:38
  33.1 0.0 copy-done.3
  33.2 0.0 copy-done.1
  33.2 0.2 sqrt_atan2_fusion
  33.4 60.3 %all-gather.2.cloned.1.call-done = f32[128,64,512]{2,1,0:T(8,128)} async-done(((f32[1,64,512]{2,1,0:T(8,128)}), f32[128,64,512]{2,1,0:T(8,128)}) %all-gather.2.cloned.1.call-update) | async-done | bytes 16777232 | tf_op jit(solution)/shard_map/all_gather | solution.py:77
  93.7 10.1 %gather_fusion = f32[8,512,512]{2,1,0:T(8,128)} fusion(f32[16,512,512]{2,1,0:T(8,128)} %bitcast.45, s32[1024]{0:T(1024)S(1)} %pad_clamp_fusion.1), kind=kCustom, calls=%fused_computation | custom fusion | bytes 16777248 | tf_op jit(solution)/shard_map/jit(_take)/gather | solution.py:83
  103.7 11.3 %select_subtract_fusion = f32[8,512,512]{2,1,0:T(8,128)} fusion(f32[8,512,512]{2,1,0:T(8,128)} %fusion, f32[8,512,512]{2,1,0:T(8,128)} %gather_fusion, pred[8]{0:T(512)(128)(4,1)S(1)} %compare_and_fusion.1), kind=kLoop, calls=%fused_computation.2 | loop fusion | flops 4194304 | bytes 25165832 | tf_op jit(solution)/shard_map/sub | solution.py:83
  115.1 0.0 copy-start.2
  115.1 5.6 %fusion.68 = f32[8,17,512]{2,1,0:T(8,128)S(1)} fusion(f32[8,512,512]{2,1,0:T(8,128)} %select_subtract_fusion, f32[8,512]{1,0:T(8,128)S(1)} %get-tuple-element.32, f32[17]{0:T(128)S(1)} %iota_convert_fusion), kind=kOutput, calls=%fused_computation.64 | convolution fusion | flops 213979136 | bytes 8683588 | tf_op jit(solution)/shard_map/mtp,mpq->mtq/dot_general | solution.py:59
  120.7 1.8 %fusion.66 = f32[8,17,17]{2,1,0:T(8,128)S(1)} fusion(f32[8,17,512]{2,1,0:T(8,128)S(1)} %fusion.68, f32[8,512]{1,0:T(8,128)S(1)} %get-tuple-element.31, f32[17]{0:T(128)S(1)} %iota_convert_fusion), kind=kOutput, calls=%fused_computation.61 | convolution fusion | flops 14274560 | bytes 304228 | tf_op jit(solution)/shard_map/mtq,muq->mtu/dot_general | solution.py:60
  122.5 0.0 copy-done.2
  122.5 0.2 fusion.78
  122.7 1.3 collective-permute-start
  124.0 2.9 %collective-permute-done = f32[4,17,17]{2,0,1:T(4,128)S(1)} collective-permute-done((f32[4,17,17]{2,0,1:T(4,128)S(1)}, f32[4,17,17]{2,0,1:T(4,128)S(1)}, u32[]{:S(2)}, u32[]{:S(2)}) %collective-permute-start) | collective-permute-done | bytes 4656 | tf_op jit(solution)/shard_map/ppermute | solution.py:68
  126.9 2.8 %collective-permute-start.1 = (f32[4,17,17]{2,0,1:T(4,128)S(1)}, f32[4,17,17]{2,0,1:T(4,128)S(1)}, u32[]{:S(2)}, u32[]{:S(2)}) collective-permute-start(f32[4,17,17]{2,0,1:T(4,128)S(1)} %add.227), channel_id=1, source_target_pairs={{0,2},{1,3},{2,0},{3,1},{4,6},{5,7},{6,4},{7,5},{8,10},{9,11},{10,... | collective-permute-start | bytes 13880 | tf_op jit(solution)/shard_map/ppermute | solution.py:68
  129.7 2.8 %collective-permute-done.1 = f32[4,17,17]{2,0,1:T(4,128)S(1)} collective-permute-done((f32[4,17,17]{2,0,1:T(4,128)S(1)}, f32[4,17,17]{2,0,1:T(4,128)S(1)}, u32[]{:S(2)}, u32[]{:S(2)}) %collective-permute-start.1) | collective-permute-done | bytes 4656 | tf_op jit(solution)/shard_map/ppermute | solution.py:68
  132.5 1.5 collective-permute-start.2
  134.0 2.5 %collective-permute-done.2 = f32[4,17,17]{2,0,1:T(4,128)S(1)} collective-permute-done((f32[4,17,17]{2,0,1:T(4,128)S(1)}, f32[4,17,17]{2,0,1:T(4,128)S(1)}, u32[]{:S(2)}, u32[]{:S(2)}) %collective-permute-start.2) | collective-permute-done | bytes 4656 | tf_op jit(solution)/shard_map/ppermute | solution.py:68
  136.5 3.1 %collective-permute-start.3 = (f32[4,17,17]{2,0,1:T(4,128)S(1)}, f32[4,17,17]{2,0,1:T(4,128)S(1)}, u32[]{:S(2)}, u32[]{:S(2)}) collective-permute-start(f32[4,17,17]{2,0,1:T(4,128)S(1)} %add.229), channel_id=1, source_target_pairs={{0,8},{1,9},{2,10},{3,11},{4,12},{5,13},{6,14},{7,15},{8,0},{9,1},... | collective-permute-start | bytes 13880 | tf_op jit(solution)/shard_map/ppermute | solution.py:68
  139.5 2.5 %collective-permute-done.3 = f32[4,17,17]{2,0,1:T(4,128)S(1)} collective-permute-done((f32[4,17,17]{2,0,1:T(4,128)S(1)}, f32[4,17,17]{2,0,1:T(4,128)S(1)}, u32[]{:S(2)}, u32[]{:S(2)}) %collective-permute-start.3) | collective-permute-done | bytes 4656 | tf_op jit(solution)/shard_map/ppermute | solution.py:68
  142.0 0.0 copy-start
  142.0 0.6 gather_fusion.1
  142.6 1.7 %fusion.67 = f32[8,512,17]{1,2,0:T(8,128)S(1)} fusion(f32[8,512]{1,0:T(8,128)S(1)} %get-tuple-element.32, f32[17]{0:T(128)S(1)} %iota_convert_fusion, f32[8,17,17]{2,1,0:T(8,128)S(1)} %gather_fusion.1, pred[8]{0:T(512)(128)(4,1)S(1)} %compare_and_fusion), kind=kOutput, calls=%fused_computation.63 | convolution fusion | flops 7174408 | bytes 304236 | tf_op jit(solution)/shard_map/ktp,ktu->kpu/dot_general | solution.py:91
  144.3 8.8 %convolution_subtract_fusion = f32[8,512,512]{2,1,0:T(8,128)} fusion(f32[8,512,512]{2,1,0:T(8,128)} %select_subtract_fusion, f32[8,512,17]{1,2,0:T(8,128)S(1)} %fusion.67, f32[8,512]{1,0:T(8,128)S(1)} %get-tuple-element.31, f32[17]{0:T(128)S(1)} %iota_convert_fusion), kind=kOutput, calls=%fused_computation.59 | convolution fusion | flops 216076288 | bytes 17072196 | tf_op jit(solution)/shard_map/kpu,kuq->kpq/dot_general | solution.py:92
  153.1 0.0 copy-done
  (15 shorter events, 0.1 us)
Async XLA Ops:
  7.2 86.5 %all-gather.2.cloned.1.call-start = ((), (), s32[]{:S(2)}) async-start(), calls=%async_computation | async-start | bytes 16908288 | tf_op jit(solution)/shard_map/all_gather | solution.py:77
  21.3 11.9 %copy-start.3 = (s32[8]{0:T(128)S(1)}, s32[8]{0:T(128)}, u32[]{:S(2)}) copy-start(s32[8]{0:T(128)} %param.10) | copy-start | bytes 100
  21.3 11.9 %copy-start.1 = (s32[8,2]{0,1:T(2,128)S(1)}, s32[8,2]{0,1:T(2,128)}, u32[]{:S(2)}) copy-start(s32[8,2]{0,1:T(2,128)} %param.12) | copy-start | bytes 196
  115.1 7.5 %copy-start.2 = (s32[8]{0:T(128)S(1)}, s32[8]{0:T(128)}, u32[]{:S(2)}) copy-start(s32[8]{0:T(128)} %param.11) | copy-start | bytes 100
  122.7 4.2 %collective-permute-start = (f32[4,17,17]{2,0,1:T(4,128)S(1)}, f32[4,17,17]{2,0,1:T(4,128)S(1)}, u32[]{:S(2)}, u32[]{:S(2)}) collective-permute-start(f32[4,17,17]{2,0,1:T(4,128)S(1)} %fusion.78), channel_id=1, source_target_pairs={{0,1},{1,0},{2,3},{3,2},{4,5},{5,4},{6,7},{7,6},{8,9},{9,8},{10,11... | collective-permute-start | bytes 13880 | tf_op jit(solution)/shard_map/ppermute | solution.py:68
  126.9 5.5 %collective-permute-start.1 = (f32[4,17,17]{2,0,1:T(4,128)S(1)}, f32[4,17,17]{2,0,1:T(4,128)S(1)}, u32[]{:S(2)}, u32[]{:S(2)}) collective-permute-start(f32[4,17,17]{2,0,1:T(4,128)S(1)} %add.227), channel_id=1, source_target_pairs={{0,2},{1,3},{2,0},{3,1},{4,6},{5,7},{6,4},{7,5},{8,10},{9,11},{10,... | collective-permute-start | bytes 13880 | tf_op jit(solution)/shard_map/ppermute | solution.py:68
  132.5 4.0 %collective-permute-start.2 = (f32[4,17,17]{2,0,1:T(4,128)S(1)}, f32[4,17,17]{2,0,1:T(4,128)S(1)}, u32[]{:S(2)}, u32[]{:S(2)}) collective-permute-start(f32[4,17,17]{2,0,1:T(4,128)S(1)} %add.228), channel_id=1, source_target_pairs={{0,4},{1,5},{2,6},{3,7},{4,0},{5,1},{6,2},{7,3},{8,12},{9,13},{10,... | collective-permute-start | bytes 13880 | tf_op jit(solution)/shard_map/ppermute | solution.py:68
  136.5 5.5 %collective-permute-start.3 = (f32[4,17,17]{2,0,1:T(4,128)S(1)}, f32[4,17,17]{2,0,1:T(4,128)S(1)}, u32[]{:S(2)}, u32[]{:S(2)}) collective-permute-start(f32[4,17,17]{2,0,1:T(4,128)S(1)} %add.229), channel_id=1, source_target_pairs={{0,8},{1,9},{2,10},{3,11},{4,12},{5,13},{6,14},{7,15},{8,0},{9,1},... | collective-permute-start | bytes 13880 | tf_op jit(solution)/shard_map/ppermute | solution.py:68
  142.0 11.1 %copy-start = (f32[4,17,17]{2,0,1:T(4,128)}, f32[4,17,17]{2,0,1:T(4,128)S(1)}, u32[]{:S(2)}) copy-start(f32[4,17,17]{2,0,1:T(4,128)S(1)} %add_multiply_fusion) | copy-start | bytes 13876
Sparse Core Ops, SparseCore 0:
  11.1 82.4 all-gather.1

commit v5 on v2

--- a/solution.py
+++ b/solution.py
@@ -12,6 +12,7 @@
 VISIT_PARTS = ("vy", "vc")
 PATCH_PARTS = ("px", "pz")
 PIECE_AXES = VISIT_PARTS + PATCH_PARTS
+
 
 exact_mode = lax.Precision.HIGHEST
 warp_mode = lax.Precision.HIGH
@@ -60,7 +61,7 @@
 
 
 def project_terms(differences, row_basis, col_basis):
-    middle = jnp.einsum("mtp,mpq->mtq", row_basis, differences, precision=exact_mode)
+    middle = jnp.einsum("mtp,mpq->mtq", row_basis, differences, precision=warp_mode)
     return jnp.einsum("mtq,muq->mtu", middle, col_basis, precision=exact_mode)
 
 
@@ -83,29 +84,15 @@
     piece_count = pieces.shape[0]
     side_len = pieces.shape[1]
     patch_count = lax.axis_size(PATCH_PARTS)
-    y_count = lax.axis_size("vy")
-    core_count = lax.axis_size("vc")
-    slab_rows = ref_patch.shape[1]
-    half = lax.all_gather(ref_patch, PATCH_PARTS + ("vy",), axis=0, tiled=True)
-    other = lax.ppermute(half, "vc", [(0, 1), (1, 0)])
-    half = half.reshape(patch_count, y_count, slab_rows, side_len)
-    other = other.reshape(patch_count, y_count, slab_rows, side_len)
-    core = lax.axis_index("vc")
-
+    gathered = lax.all_gather(ref_patch, PATCH_PARTS + VISIT_PARTS, axis=0, tiled=True)
+    ref_block = gathered.reshape(patch_count, side_len, side_len)
+    visit_slots = jnp.arange(VIS_DEV, dtype=jnp.int32)
+    own_onehot = (piece_visit[:, None] == visit_slots[None, :]).astype(jnp.float32)
     warped_all = warp_batch(pieces, shifts[:, 0], shifts[:, 1], phases[:, 0], phases[:, 1])
     warped_all = lax.optimization_barrier(warped_all)
-
-    own_rows = jnp.take(half, piece_patch, axis=0)
-    other_rows = jnp.take(other, piece_patch, axis=0)
-    first = jnp.where(core == 0, own_rows, other_rows)
-    second = jnp.where(core == 0, other_rows, own_rows)
-    ref_rows = jnp.stack([first, second], axis=2).reshape(piece_count, side_len, side_len)
-    own_diffs = warped_all - ref_rows
-
+    own_diffs = warped_all - jnp.take(ref_block, piece_patch, axis=0)
     row_basis, col_basis = basis_pair(anchors, side_len)
     partial_value = project_terms(own_diffs, row_basis, col_basis)
-    visit_slots = jnp.arange(VIS_DEV, dtype=jnp.int32)
-    own_onehot = (piece_visit[:, None] == visit_slots[None, :]).astype(jnp.float32)
     local_sums = jnp.einsum("kv,ktu->vtu", own_onehot, partial_value, precision=exact_mode)
     totals = ring_sum(ring_sum(local_sums, "pz"), "px")
     coefficients = totals / float(patch_count * (piece_count // VIS_DEV) * side_len * side_len)

time: 194 us -> 151 us (0.78)
  waiting for transfers between devices: 89.6 us -> 69.2 us
  other arithmetic: 20.7 us -> 0.62 us
  starting transfers between devices: 10.8 us -> 7.99 us
  matrix products: 43.7 us -> 46.1 us
  local copies, waits for them, and re-layouts: 14.4 us -> 12.2 us
    all_gather x1, waiting for transfers between devices: 83.9 us -> 60.1 us  [body(): lax.all_gather(ref_patch, PATCH_PARTS + VISIT_PARTS, axis=0, tiled=True)]
    sub x1 -> x0, other arithmetic: 11.3 us -> none  [body(): own_diffs = warped_all - ref_rows]
    another operation x2 -> x0, other arithmetic: 8.9 us -> none  [body(): jnp.stack([first, second], axis=2).reshape(piece_count, side_len, side_len)]
    ppermute x6, waiting for transfers between devices: 5.01 us -> 8.46 us  [ring_sum(): received.append(lax.ppermute(value, axis_name, pairs))]
    ppermute x6, starting transfers between devices: 10.8 us -> 7.96 us  [ring_sum(): received.append(lax.ppermute(value, axis_name, pairs))]
    dot_general x1, matrix products: 8.84 us -> 11.1 us  [body(): fitted = jnp.einsum('kpu,kuq->kpq', middle, col_basis, precision=warp_mode)]
    gather x2 -> x1, local copies, waits for them, and re-layouts: 12.3 us -> 10.1 us  [body(): own_diffs = warped_all - jnp.take(ref_block, piece_patch, axis=0)]
  transfers between devices with their start and end apart: 8 -> 7, of which waited for: 5 -> 7; matrix products, arithmetic and copies ran while one was open for 16% -> 17% of each run, Pallas kernels for 0% -> 0%
where the time goes in v5:
time: 151 us; the launch traced here: 150 us
  waiting for transfers between devices  69.2 us (46%)
  matrix products  46.1 us (31%)
  between operations  14.3 us (9%)
  local copies, waits for them, and re-layouts  12.2 us (8%)
  starting transfers between devices  7.99 us (5%)
    all_gather x1, waiting for transfers between devices, body(): lax.all_gather(ref_patch, PATCH_PARTS + VISIT_PARTS, axis=0, tiled=True)  60.1 us
    dot_general x1, matrix products, warp_batch(): return jnp.einsum('kib,kjb->kij', middle, right_matrix, precision=warp_mode)  11.9 us
    dot_general x1, matrix products, warp_batch(): jnp.einsum('kia,kab->kib', left_matrix, slab_images, precision=warp_mode)  11.6 us
    dot_general x1, matrix products, body(): fitted = jnp.einsum('kpu,kuq->kpq', middle, col_basis, precision=warp_mode)  11.1 us
    gather x1, local copies, waits for them, and re-layouts, body(): own_diffs = warped_all - jnp.take(ref_block, piece_patch, axis=0)  10.1 us
    ppermute x6, waiting for transfers between devices, ring_sum(): received.append(lax.ppermute(value, axis_name, pairs))  8.46 us
    ppermute x6, starting transfers between devices, ring_sum(): received.append(lax.ppermute(value, axis_name, pairs))  7.96 us
    dot_general x1, matrix products, project_terms(): jnp.einsum('mtp,mpq->mtq', row_basis, differences, precision=warp_mode)  7.79 us
  transfers between devices with their start and end apart: 7, of which 7 were waited for; matrix products, arithmetic and copies ran while one was open for 17% of the time, Pallas kernels for 0%

profile of v5, /device:TPU:0, one launch (start us, length us, event | category | flops | bytes accessed | tf_op | source)
XLA Modules:
  0.0 150.4 jit_solution(11387652172559435666)
XLA Ops:
  7.2 0.0 all-gather.2.cloned.1.call-start
  7.2 0.7 all-gather.2.cloned.1.call-update
  7.9 0.8 slice_bitcast_fusion.9
  8.7 0.8 slice_bitcast_fusion.8
  9.5 0.1 fusion.117
  9.6 0.1 iota_add_fusion
  9.6 11.6 %fusion.13 = f32[8,512,512]{2,1,0:T(8,128)S(1)} fusion(f32[8,512,512]{2,1,0:T(8,128)} %param.8, f32[8]{0:T(128)S(1)} %get-tuple-element.27, f32[8]{0:T(128)S(1)} %get-tuple-element.26, f32[8]{0:T(128)S(1)} %get-tuple-element.25, f32[8]{0:T(128)S(1)} %get-tuple-element.24, f32[8]{0:T(128)S(1)} %get-tuple-element.23, f32[8]{0:T(128)S(1)} %get-tuple-element.28, ...), kind=kOutput, calls=%fused_computation.17 | convolution fusion | flops 6469713920 | bytes 16793792 | tf_op jit(solution)/shard_map/kia,kab->kib/dot_general | solution.py:41
  21.3 0.0 copy-start.2
  21.3 0.0 copy-start.3
  21.3 0.0 copy-start.1
  21.3 11.9 %fusion = f32[8,512,512]{2,1,0:T(8,128)} fusion(f32[8,512,512]{2,1,0:T(8,128)S(1)} %fusion.13, f32[8]{0:T(128)S(1)} %get-tuple-element.4, f32[8]{0:T(128)S(1)} %get-tuple-element.5, f32[8]{0:T(128)S(1)} %get-tuple-element.6, f32[8]{0:T(128)S(1)} %get-tuple-element.7, f32[8]{0:T(128)S(1)} %get-tuple-element.8, f32[8]{0:T(128)S(1)} %get-tuple-element.3, ...), kind=kOutput, calls=%fused_computation.3 | convolution fusion | flops 6469713920 | bytes 16793792 | tf_op jit(solution)/shard_map/kib,kjb->kij/dot_general | solution.py:43
  33.2 0.0 copy-done.2
  33.2 0.0 copy-done.3
  33.3 0.0 copy-done.1
  33.3 0.1 sqrt_atan2_fusion
  33.4 0.1 sqrt_atan2_fusion.1
  33.6 60.1 %all-gather.2.cloned.1.call-done = f32[128,64,512]{2,1,0:T(8,128)} async-done(((f32[1,64,512]{2,1,0:T(8,128)}), f32[128,64,512]{2,1,0:T(8,128)}) %all-gather.2.cloned.1.call-update) | async-done | bytes 16777232 | tf_op jit(solution)/shard_map/all_gather | solution.py:87
  93.6 10.1 %gather_fusion = f32[8,512,512]{2,1,0:T(8,128)} fusion(f32[16,512,512]{2,1,0:T(8,128)} %bitcast.55, s32[1024]{0:T(1024)S(1)} %pad_clamp_fusion.1), kind=kCustom, calls=%fused_computation | custom fusion | bytes 16777248 | tf_op jit(solution)/shard_map/jit(_take)/gather | solution.py:93
  103.7 7.8 %fusion.66 = f32[8,17,512]{2,1,0:T(8,128)S(1)} fusion(f32[8,512,512]{2,1,0:T(8,128)} %fusion, f32[8,512,512]{2,1,0:T(8,128)} %gather_fusion, pred[8]{0:T(512)(128)(4,1)S(1)} %compare_and_fusion.1, f32[8,512]{1,0:T(8,128)S(1)} %sqrt_atan2_fusion.1, f32[17]{0:T(128)S(1)} %iota_convert_fusion), kind=kOutput, calls=%fused_computation.60 | convolution fusion | flops 218173440 | bytes 17072204 | tf_op jit(solution)/shard_map/mtp,mpq->mtq/dot_general | solution.py:64
  111.5 1.9 %fusion.67 = f32[8,17,17]{2,1,0:T(8,128)S(1)} fusion(f32[8,17,512]{2,1,0:T(8,128)S(1)} %fusion.66, f32[8,512]{1,0:T(8,128)S(1)} %sqrt_atan2_fusion, f32[17]{0:T(128)S(1)} %iota_convert_fusion), kind=kOutput, calls=%fused_computation.62 | convolution fusion | flops 14274560 | bytes 304228 | tf_op jit(solution)/shard_map/mtq,muq->mtu/dot_general | solution.py:65
  113.4 0.2 fusion.78
  113.5 2.5 %collective-permute-start.2 = (f32[4,17,17]{2,0,1:T(4,128)S(1)}, f32[4,17,17]{2,0,1:T(4,128)S(1)}, u32[]{:S(2)}, u32[]{:S(2)}) collective-permute-start(f32[4,17,17]{2,0,1:T(4,128)S(1)} %fusion.78), channel_id=1, source_target_pairs={{0,3},{1,0},{2,1},{3,2},{4,7},{5,4},{6,5},{7,6},{8,11},{9,8},{10,9... | collective-permute-start | bytes 13880 | tf_op jit(solution)/shard_map/ppermute | solution.py:74
  116.1 0.7 collective-permute-start.1
  116.8 0.9 collective-permute-start
  117.7 0.2 collective-permute-done.2
  118.0 3.6 %collective-permute-done.1 = f32[4,17,17]{2,0,1:T(4,128)S(1)} collective-permute-done((f32[4,17,17]{2,0,1:T(4,128)S(1)}, f32[4,17,17]{2,0,1:T(4,128)S(1)}, u32[]{:S(2)}, u32[]{:S(2)}) %collective-permute-start.1) | collective-permute-done | bytes 4656 | tf_op jit(solution)/shard_map/ppermute | solution.py:74
  121.5 0.4 collective-permute-done
  122.0 2.1 %collective-permute-start.5 = (f32[4,17,17]{2,0,1:T(4,128)S(1)}, f32[4,17,17]{2,0,1:T(4,128)S(1)}, u32[]{:S(2)}, u32[]{:S(2)}) collective-permute-start(f32[4,17,17]{2,0,1:T(4,128)S(1)} %fusion.195), channel_id=1, source_target_pairs={{0,12},{4,0},{8,4},{12,8},{1,13},{5,1},{9,5},{13,9},{2,14},{6,2},{... | collective-permute-start | bytes 13880 | tf_op jit(solution)/shard_map/ppermute | solution.py:74
  124.1 0.8 collective-permute-start.4
  124.9 0.9 collective-permute-start.3
  125.8 0.2 collective-permute-done.5
  126.0 3.5 %collective-permute-done.4 = f32[4,17,17]{2,0,1:T(4,128)S(1)} collective-permute-done((f32[4,17,17]{2,0,1:T(4,128)S(1)}, f32[4,17,17]{2,0,1:T(4,128)S(1)}, u32[]{:S(2)}, u32[]{:S(2)}) %collective-permute-start.4) | collective-permute-done | bytes 4656 | tf_op jit(solution)/shard_map/ppermute | solution.py:74
  129.5 0.6 collective-permute-done.3
  130.1 0.0 copy-start
  130.2 0.6 gather_fusion.1
  130.7 1.7 %fusion.68 = f32[8,512,17]{1,2,0:T(8,128)S(1)} fusion(f32[8,512]{1,0:T(8,128)S(1)} %sqrt_atan2_fusion.1, f32[17]{0:T(128)S(1)} %iota_convert_fusion, f32[8,17,17]{2,1,0:T(8,128)S(1)} %gather_fusion.1, pred[8]{0:T(512)(128)(4,1)S(1)} %compare_and_fusion), kind=kOutput, calls=%fused_computation.64 | convolution fusion | flops 7174408 | bytes 304236 | tf_op jit(solution)/shard_map/ktp,ktu->kpu/dot_general | solution.py:100
  132.4 11.1 %convolution_subtract_fusion = f32[8,512,512]{2,1,0:T(8,128)} fusion(f32[8,512,17]{1,2,0:T(8,128)S(1)} %fusion.68, f32[8,512,512]{2,1,0:T(8,128)} %fusion, f32[8,512,512]{2,1,0:T(8,128)} %gather_fusion, pred[8]{0:T(512)(128)(4,1)S(1)} %compare_and_fusion.1, f32[8,512]{1,0:T(8,128)S(1)} %sqrt_atan2_fusion, f32[17]{0:T(128)S(1)} %iota_convert_fusion), kind=kOutput, calls=%fused_computation.59 | convolution fusion | flops 220270592 | bytes 25460812 | tf_op jit(solution)/shard_map/kpu,kuq->kpq/dot_general | solution.py:101
  143.5 0.0 copy-done
  (16 shorter events, 0.2 us)
Async XLA Ops:
  7.2 86.5 %all-gather.2.cloned.1.call-start = ((), (), s32[]{:S(2)}) async-start(), calls=%async_computation | async-start | bytes 16908288 | tf_op jit(solution)/shard_map/all_gather | solution.py:87
  21.3 11.9 %copy-start.2 = (s32[8]{0:T(128)S(1)}, s32[8]{0:T(128)}, u32[]{:S(2)}) copy-start(s32[8]{0:T(128)} %param.11) | copy-start | bytes 100
  21.3 11.9 %copy-start.3 = (s32[8]{0:T(128)S(1)}, s32[8]{0:T(128)}, u32[]{:S(2)}) copy-start(s32[8]{0:T(128)} %param.10) | copy-start | bytes 100
  21.3 12.0 %copy-start.1 = (s32[8,2]{0,1:T(2,128)S(1)}, s32[8,2]{0,1:T(2,128)}, u32[]{:S(2)}) copy-start(s32[8,2]{0,1:T(2,128)} %param.12) | copy-start | bytes 196
  113.5 4.4 %collective-permute-start.2 = (f32[4,17,17]{2,0,1:T(4,128)S(1)}, f32[4,17,17]{2,0,1:T(4,128)S(1)}, u32[]{:S(2)}, u32[]{:S(2)}) collective-permute-start(f32[4,17,17]{2,0,1:T(4,128)S(1)} %fusion.78), channel_id=1, source_target_pairs={{0,3},{1,0},{2,1},{3,2},{4,7},{5,4},{6,5},{7,6},{8,11},{9,8},{10,9... | collective-permute-start | bytes 13880 | tf_op jit(solution)/shard_map/ppermute | solution.py:74
  116.1 5.4 %collective-permute-start.1 = (f32[4,17,17]{2,0,1:T(4,128)S(1)}, f32[4,17,17]{2,0,1:T(4,128)S(1)}, u32[]{:S(2)}, u32[]{:S(2)}) collective-permute-start(f32[4,17,17]{2,0,1:T(4,128)S(1)} %fusion.78), channel_id=1, source_target_pairs={{0,2},{1,3},{2,0},{3,1},{4,6},{5,7},{6,4},{7,5},{8,10},{9,11},{10,... | collective-permute-start | bytes 13880 | tf_op jit(solution)/shard_map/ppermute | solution.py:74
  116.8 5.1 %collective-permute-start = (f32[4,17,17]{2,0,1:T(4,128)S(1)}, f32[4,17,17]{2,0,1:T(4,128)S(1)}, u32[]{:S(2)}, u32[]{:S(2)}) collective-permute-start(f32[4,17,17]{2,0,1:T(4,128)S(1)} %fusion.78), channel_id=1, source_target_pairs={{0,1},{1,2},{2,3},{3,0},{4,5},{5,6},{6,7},{7,4},{8,9},{9,10},{10,1... | collective-permute-start | bytes 13880 | tf_op jit(solution)/shard_map/ppermute | solution.py:74
  122.0 4.0 %collective-permute-start.5 = (f32[4,17,17]{2,0,1:T(4,128)S(1)}, f32[4,17,17]{2,0,1:T(4,128)S(1)}, u32[]{:S(2)}, u32[]{:S(2)}) collective-permute-start(f32[4,17,17]{2,0,1:T(4,128)S(1)} %fusion.195), channel_id=1, source_target_pairs={{0,12},{4,0},{8,4},{12,8},{1,13},{5,1},{9,5},{13,9},{2,14},{6,2},{... | collective-permute-start | bytes 13880 | tf_op jit(solution)/shard_map/ppermute | solution.py:74
  124.1 5.4 %collective-permute-start.4 = (f32[4,17,17]{2,0,1:T(4,128)S(1)}, f32[4,17,17]{2,0,1:T(4,128)S(1)}, u32[]{:S(2)}, u32[]{:S(2)}) collective-permute-start(f32[4,17,17]{2,0,1:T(4,128)S(1)} %fusion.195), channel_id=1, source_target_pairs={{0,8},{4,12},{8,0},{12,4},{1,9},{5,13},{9,1},{13,5},{2,10},{6,14},... | collective-permute-start | bytes 13880 | tf_op jit(solution)/shard_map/ppermute | solution.py:74
  124.9 5.1 %collective-permute-start.3 = (f32[4,17,17]{2,0,1:T(4,128)S(1)}, f32[4,17,17]{2,0,1:T(4,128)S(1)}, u32[]{:S(2)}, u32[]{:S(2)}) collective-permute-start(f32[4,17,17]{2,0,1:T(4,128)S(1)} %fusion.195), channel_id=1, source_target_pairs={{0,4},{4,8},{8,12},{12,0},{1,5},{5,9},{9,13},{13,1},{2,6},{6,10},{... | collective-permute-start | bytes 13880 | tf_op jit(solution)/shard_map/ppermute | solution.py:74
  130.1 13.4 %copy-start = (f32[4,17,17]{2,0,1:T(4,128)}, f32[4,17,17]{2,0,1:T(4,128)S(1)}, u32[]{:S(2)}) copy-start(f32[4,17,17]{2,0,1:T(4,128)S(1)} %multiply_bitcast_fusion) | copy-start | bytes 13876
Sparse Core Ops, SparseCore 0:
  11.1 82.4 all-gather.1

commit v6 on v5

--- a/solution.py
+++ b/solution.py
@@ -92,7 +92,11 @@
     warped_all = lax.optimization_barrier(warped_all)
     own_diffs = warped_all - jnp.take(ref_block, piece_patch, axis=0)
     row_basis, col_basis = basis_pair(anchors, side_len)
-    partial_value = project_terms(own_diffs, row_basis, col_basis)
+    warp_terms = project_terms(warped_all, row_basis, col_basis)
+    against_cols = jnp.einsum("qpr,kur->qpku", ref_block, col_basis, precision=warp_mode)
+    picked = against_cols[piece_patch, :, jnp.arange(piece_count), :]
+    ref_terms = jnp.einsum("ktp,kpu->ktu", row_basis, picked, precision=exact_mode)
+    partial_value = warp_terms - ref_terms
     local_sums = jnp.einsum("kv,ktu->vtu", own_onehot, partial_value, precision=exact_mode)
     totals = ring_sum(ring_sum(local_sums, "pz"), "px")
     coefficients = totals / float(patch_count * (piece_count // VIS_DEV) * side_len * side_len)

time: 151 us -> 160 us (1.060)
  matrix products: 46.1 us -> 64 us
  waiting for transfers between devices: 69.2 us -> 57.3 us
  local copies, waits for them, and re-layouts: 12.2 us -> 15.6 us
    dot_general x0 -> x2, matrix products: none -> 19.9 us  [the longest x1 18.1 us: body(): jnp.einsum('qpr,kur->qpku', ref_block, col_basis, precision=warp_mode)]
    all_gather x1, waiting for transfers between devices: 60.1 us -> 52.4 us  [body(): lax.all_gather(ref_patch, PATCH_PARTS + VISIT_PARTS, axis=0, tiled=True)]
    ppermute x6, waiting for transfers between devices: 8.46 us -> 4.27 us  [ring_sum(): received.append(lax.ppermute(value, axis_name, pairs))]
    gather x0 -> x1, local copies, waits for them, and re-layouts: none -> 3.36 us  [body(): picked = against_cols[piece_patch, :, jnp.arange(piece_count), :]]
    dot_general x1, matrix products: 7.79 us -> 5.78 us  [project_terms(): jnp.einsum('mtp,mpq->mtq', row_basis, differences, precision=warp_mode)]
  transfers between devices with their start and end apart: 7 -> 7, of which waited for: 7 -> 4; matrix products, arithmetic and copies ran while one was open for 17% -> 27% of each run, Pallas kernels for 0% -> 0%
where the time goes in v6:
time: 160 us
  matrix products  64 us (40%)
  waiting for transfers between devices  57.3 us (36%)
  local copies, waits for them, and re-layouts  15.6 us (10%)
  between operations  14.3 us (9%)
  starting transfers between devices  8.22 us (5%)
    all_gather x1, waiting for transfers between devices, body(): lax.all_gather(ref_patch, PATCH_PARTS + VISIT_PARTS, axis=0, tiled=True)  52.4 us
    dot_general x1, matrix products, body(): jnp.einsum('qpr,kur->qpku', ref_block, col_basis, precision=warp_mode)  18.1 us
    dot_general x1, matrix products, warp_batch(): return jnp.einsum('kib,kjb->kij', middle, right_matrix, precision=warp_mode)  11.9 us
    dot_general x1, matrix products, warp_batch(): jnp.einsum('kia,kab->kib', left_matrix, slab_images, precision=warp_mode)  11.6 us
    dot_general x1, matrix products, body(): fitted = jnp.einsum('kpu,kuq->kpq', middle, col_basis, precision=warp_mode)  11.1 us
    gather x1, local copies, waits for them, and re-layouts, body(): own_diffs = warped_all - jnp.take(ref_block, piece_patch, axis=0)  10.1 us
    ppermute x6, starting transfers between devices, ring_sum(): received.append(lax.ppermute(value, axis_name, pairs))  8.18 us
    dot_general x1, matrix products, project_terms(): jnp.einsum('mtp,mpq->mtq', row_basis, differences, precision=warp_mode)  5.78 us
  transfers between devices with their start and end apart: 7, of which 4 were waited for; matrix products, arithmetic and copies ran while one was open for 27% of the time, Pallas kernels for 0%

profile of v6, /device:TPU:0, one launch (start us, length us, event | category | flops | bytes accessed | tf_op | source)
XLA Modules:
  0.0 160.0 jit_solution(14223680385805970897)
XLA Ops:
  7.2 0.0 all-gather.2.cloned.1.call-start
  7.2 0.7 all-gather.2.cloned.1.call-update
  7.9 0.8 slice_bitcast_fusion.9
  8.7 0.8 slice_bitcast_fusion.8
  9.5 0.1 fusion.122
  9.6 0.1 iota_add_fusion
  9.7 11.6 %fusion.13 = f32[8,512,512]{2,1,0:T(8,128)S(1)} fusion(f32[8,512,512]{2,1,0:T(8,128)} %param.8, f32[8]{0:T(128)S(1)} %get-tuple-element.29, f32[8]{0:T(128)S(1)} %get-tuple-element.28, f32[8]{0:T(128)S(1)} %get-tuple-element.27, f32[8]{0:T(128)S(1)} %get-tuple-element.26, f32[8]{0:T(128)S(1)} %get-tuple-element.25, f32[8]{0:T(128)S(1)} %get-tuple-element.30, ...), kind=kOutput, calls=%fused_computation.18 | convolution fusion | flops 6469713920 | bytes 16793792 | tf_op jit(solution)/shard_map/kia,kab->kib/dot_general | solution.py:41
  21.3 0.0 copy-start.3
  21.3 0.0 copy-start.2
  21.3 0.0 copy-start.1
  21.3 11.9 %fusion = f32[8,512,512]{2,1,0:T(8,128)} fusion(f32[8,512,512]{2,1,0:T(8,128)S(1)} %fusion.13, f32[8]{0:T(128)S(1)} %get-tuple-element.6, f32[8]{0:T(128)S(1)} %get-tuple-element.7, f32[8]{0:T(128)S(1)} %get-tuple-element.8, f32[8]{0:T(128)S(1)} %get-tuple-element.9, f32[8]{0:T(128)S(1)} %get-tuple-element.10, f32[8]{0:T(128)S(1)} %get-tuple-element.5, ...), kind=kOutput, calls=%fused_computation.4 | convolution fusion | flops 6469713920 | bytes 16793792 | tf_op jit(solution)/shard_map/kib,kjb->kij/dot_general | solution.py:43
  33.3 0.0 copy-done.3
  33.3 0.0 copy-done.2
  33.3 0.0 copy-done.1
  33.4 0.2 sqrt_atan2_fusion
  33.5 5.8 %fusion.69 = f32[8,17,512]{2,1,0:T(8,128)S(1)} fusion(f32[8,512,512]{2,1,0:T(8,128)} %fusion, f32[8,512]{1,0:T(8,128)S(1)} %get-tuple-element.34, f32[17]{0:T(128)S(1)} %iota_convert_fusion), kind=kOutput, calls=%fused_computation.67 | convolution fusion | flops 213979136 | bytes 8683588 | tf_op jit(solution)/shard_map/mtp,mpq->mtq/dot_general | solution.py:64
  39.3 1.9 %fusion.67 = f32[8,17,17]{2,1,0:T(8,128)S(1)} fusion(f32[8,17,512]{2,1,0:T(8,128)S(1)} %fusion.69, f32[8,512]{1,0:T(8,128)S(1)} %get-tuple-element.33, f32[17]{0:T(128)S(1)} %iota_convert_fusion), kind=kOutput, calls=%fused_computation.64 | convolution fusion | flops 14274560 | bytes 304228 | tf_op jit(solution)/shard_map/mtq,muq->mtu/dot_general | solution.py:65
  41.2 52.4 %all-gather.2.cloned.1.call-done = f32[128,64,512]{2,1,0:T(8,128)} async-done(((f32[1,64,512]{2,1,0:T(8,128)}), f32[128,64,512]{2,1,0:T(8,128)}) %all-gather.2.cloned.1.call-update) | async-done | bytes 16777232 | tf_op jit(solution)/shard_map/all_gather | solution.py:87
  93.6 18.1 %convolution_bitcast_fusion = f32[16,512,8,17]{1,3,2,0:T(8,128)} fusion(f32[16,512,512,1]{2,1,3,0:T(8,128)} %bitcast.73, f32[8,512]{1,0:T(8,128)S(1)} %get-tuple-element.33, f32[17]{0:T(128)S(1)} %iota_convert_fusion), kind=kOutput, calls=%fused_computation.60 | convolution fusion | flops 3422621696 | bytes 21250116 | tf_op jit(solution)/shard_map/qpr,kur->qpku/dot_general | solution.py:96
  111.7 3.4 %gather_fusion.1 = f32[8,512,17]{1,2,0:T(8,128)S(1)} fusion(f32[16,512,8,17]{1,3,2,0:T(8,128)} %convolution_bitcast_fusion, s32[8]{0:T(128)S(1)} %get-tuple-element.3), kind=kCustom, calls=%fused_computation.1 | custom fusion | bytes 557120 | tf_op jit(solution)/shard_map/gather | solution.py:97
  115.0 1.8 %convolution_subtract_fusion = f32[8,17,17]{2,1,0:T(8,128)S(1)} fusion(f32[8,17,17]{2,1,0:T(8,128)S(1)} %fusion.67, f32[8,512,17]{1,2,0:T(8,128)S(1)} %gather_fusion.1, f32[8,512]{1,0:T(8,128)S(1)} %get-tuple-element.34, f32[17]{0:T(128)S(1)} %iota_convert_fusion), kind=kOutput, calls=%fused_computation.61 | convolution fusion | flops 14276872 | bytes 313476 | tf_op jit(solution)/shard_map/ktp,kpu->ktu/dot_general | solution.py:98
  116.8 0.2 fusion.83
  117.0 2.8 %collective-permute-start.2 = (f32[4,17,17]{2,0,1:T(4,128)S(1)}, f32[4,17,17]{2,0,1:T(4,128)S(1)}, u32[]{:S(2)}, u32[]{:S(2)}) collective-permute-start(f32[4,17,17]{2,0,1:T(4,128)S(1)} %fusion.83), channel_id=1, source_target_pairs={{0,3},{1,0},{2,1},{3,2},{4,7},{5,4},{6,5},{7,6},{8,11},{9,8},{10,9... | collective-permute-start | bytes 13880 | tf_op jit(solution)/shard_map/ppermute | solution.py:74
  119.8 0.7 collective-permute-start.1
  120.5 0.9 collective-permute-start
  121.4 10.1 %gather_fusion = f32[8,512,512]{2,1,0:T(8,128)} fusion(f32[16,512,512]{2,1,0:T(8,128)} %bitcast.74, s32[1024]{0:T(1024)S(1)} %pad_clamp_fusion.1), kind=kCustom, calls=%fused_computation | custom fusion | bytes 16777248 | tf_op jit(solution)/shard_map/jit(_take)/gather | solution.py:93
  131.5 0.0 collective-permute-done.2
  131.5 0.0 collective-permute-done.1
  131.5 0.0 collective-permute-done
  131.6 2.1 %collective-permute-start.5 = (f32[4,17,17]{2,0,1:T(4,128)S(1)}, f32[4,17,17]{2,0,1:T(4,128)S(1)}, u32[]{:S(2)}, u32[]{:S(2)}) collective-permute-start(f32[4,17,17]{2,0,1:T(4,128)S(1)} %fusion.203), channel_id=1, source_target_pairs={{0,12},{4,0},{8,4},{12,8},{1,13},{5,1},{9,5},{13,9},{2,14},{6,2},{... | collective-permute-start | bytes 13880 | tf_op jit(solution)/shard_map/ppermute | solution.py:74
  133.7 0.8 collective-permute-start.4
  134.5 0.9 collective-permute-start.3
  135.4 0.4 collective-permute-done.5
  135.8 3.3 %collective-permute-done.4 = f32[4,17,17]{2,0,1:T(4,128)S(1)} collective-permute-done((f32[4,17,17]{2,0,1:T(4,128)S(1)}, f32[4,17,17]{2,0,1:T(4,128)S(1)}, u32[]{:S(2)}, u32[]{:S(2)}) %collective-permute-start.4) | collective-permute-done | bytes 4656 | tf_op jit(solution)/shard_map/ppermute | solution.py:74
  139.1 0.5 collective-permute-done.3
  139.7 0.0 copy-start
  139.8 0.6 gather_fusion.2
  140.3 1.7 %fusion.68 = f32[8,512,17]{1,2,0:T(8,128)S(1)} fusion(f32[8,512]{1,0:T(8,128)S(1)} %get-tuple-element.34, f32[17]{0:T(128)S(1)} %iota_convert_fusion, f32[8,17,17]{2,1,0:T(8,128)S(1)} %gather_fusion.2, pred[8]{0:T(512)(128)(4,1)S(1)} %compare_and_fusion), kind=kOutput, calls=%fused_computation.66 | convolution fusion | flops 7174408 | bytes 304236 | tf_op jit(solution)/shard_map/ktp,ktu->kpu/dot_general | solution.py:104
  142.0 11.1 %subtract_subtract_fusion = f32[8,512,512]{2,1,0:T(8,128)} fusion(f32[8,512,512]{2,1,0:T(8,128)} %fusion, f32[8,512,512]{2,1,0:T(8,128)} %gather_fusion, pred[8]{0:T(512)(128)(4,1)S(1)} %compare_and_fusion.1, f32[8,512,17]{1,2,0:T(8,128)S(1)} %fusion.68, f32[8,512]{1,0:T(8,128)S(1)} %get-tuple-element.33, f32[17]{0:T(128)S(1)} %iota_convert_fusion), kind=kOutput, calls=%fused_computation.3 | convolution fusion | flops 220270592 | bytes 25460812 | tf_op jit(solution)/shard_map/kpu,kuq->kpq/dot_general | solution.py:105
  153.1 0.0 copy-done
  (16 shorter events, 0.2 us)
Async XLA Ops:
  7.2 86.4 %all-gather.2.cloned.1.call-start = ((), (), s32[]{:S(2)}) async-start(), calls=%async_computation | async-start | bytes 16908288 | tf_op jit(solution)/shard_map/all_gather | solution.py:87
  21.3 12.0 %copy-start.3 = (s32[8]{0:T(128)S(1)}, s32[8]{0:T(128)}, u32[]{:S(2)}) copy-start(s32[8]{0:T(128)} %param.10) | copy-start | bytes 100
  21.3 12.0 %copy-start.2 = (s32[8]{0:T(128)S(1)}, s32[8]{0:T(128)}, u32[]{:S(2)}) copy-start(s32[8]{0:T(128)} %param.11) | copy-start | bytes 100
  21.3 12.0 %copy-start.1 = (s32[8,2]{0,1:T(2,128)S(1)}, s32[8,2]{0,1:T(2,128)}, u32[]{:S(2)}) copy-start(s32[8,2]{0,1:T(2,128)} %param.12) | copy-start | bytes 196
  117.0 14.5 %collective-permute-start.2 = (f32[4,17,17]{2,0,1:T(4,128)S(1)}, f32[4,17,17]{2,0,1:T(4,128)S(1)}, u32[]{:S(2)}, u32[]{:S(2)}) collective-permute-start(f32[4,17,17]{2,0,1:T(4,128)S(1)} %fusion.83), channel_id=1, source_target_pairs={{0,3},{1,0},{2,1},{3,2},{4,7},{5,4},{6,5},{7,6},{8,11},{9,8},{10,9... | collective-permute-start | bytes 13880 | tf_op jit(solution)/shard_map/ppermute | solution.py:74
  119.8 11.7 %collective-permute-start.1 = (f32[4,17,17]{2,0,1:T(4,128)S(1)}, f32[4,17,17]{2,0,1:T(4,128)S(1)}, u32[]{:S(2)}, u32[]{:S(2)}) collective-permute-start(f32[4,17,17]{2,0,1:T(4,128)S(1)} %fusion.83), channel_id=1, source_target_pairs={{0,2},{1,3},{2,0},{3,1},{4,6},{5,7},{6,4},{7,5},{8,10},{9,11},{10,... | collective-permute-start | bytes 13880 | tf_op jit(solution)/shard_map/ppermute | solution.py:74
  120.5 11.0 %collective-permute-start = (f32[4,17,17]{2,0,1:T(4,128)S(1)}, f32[4,17,17]{2,0,1:T(4,128)S(1)}, u32[]{:S(2)}, u32[]{:S(2)}) collective-permute-start(f32[4,17,17]{2,0,1:T(4,128)S(1)} %fusion.83), channel_id=1, source_target_pairs={{0,1},{1,2},{2,3},{3,0},{4,5},{5,6},{6,7},{7,4},{8,9},{9,10},{10,1... | collective-permute-start | bytes 13880 | tf_op jit(solution)/shard_map/ppermute | solution.py:74
  131.6 4.2 %collective-permute-start.5 = (f32[4,17,17]{2,0,1:T(4,128)S(1)}, f32[4,17,17]{2,0,1:T(4,128)S(1)}, u32[]{:S(2)}, u32[]{:S(2)}) collective-permute-start(f32[4,17,17]{2,0,1:T(4,128)S(1)} %fusion.203), channel_id=1, source_target_pairs={{0,12},{4,0},{8,4},{12,8},{1,13},{5,1},{9,5},{13,9},{2,14},{6,2},{... | collective-permute-start | bytes 13880 | tf_op jit(solution)/shard_map/ppermute | solution.py:74
  133.7 5.4 %collective-permute-start.4 = (f32[4,17,17]{2,0,1:T(4,128)S(1)}, f32[4,17,17]{2,0,1:T(4,128)S(1)}, u32[]{:S(2)}, u32[]{:S(2)}) collective-permute-start(f32[4,17,17]{2,0,1:T(4,128)S(1)} %fusion.203), channel_id=1, source_target_pairs={{0,8},{4,12},{8,0},{12,4},{1,9},{5,13},{9,1},{13,5},{2,10},{6,14},... | collective-permute-start | bytes 13880 | tf_op jit(solution)/shard_map/ppermute | solution.py:74
  134.5 5.1 %collective-permute-start.3 = (f32[4,17,17]{2,0,1:T(4,128)S(1)}, f32[4,17,17]{2,0,1:T(4,128)S(1)}, u32[]{:S(2)}, u32[]{:S(2)}) collective-permute-start(f32[4,17,17]{2,0,1:T(4,128)S(1)} %fusion.203), channel_id=1, source_target_pairs={{0,4},{4,8},{8,12},{12,0},{1,5},{5,9},{9,13},{13,1},{2,6},{6,10},{... | collective-permute-start | bytes 13880 | tf_op jit(solution)/shard_map/ppermute | solution.py:74
  139.7 13.4 %copy-start = (f32[4,17,17]{2,0,1:T(4,128)}, f32[4,17,17]{2,0,1:T(4,128)S(1)}, u32[]{:S(2)}) copy-start(f32[4,17,17]{2,0,1:T(4,128)S(1)} %multiply_bitcast_fusion) | copy-start | bytes 13876
Sparse Core Ops, SparseCore 0:
  11.1 82.4 all-gather.1

commit v7 on v6

--- a/solution.py
+++ b/solution.py
@@ -93,7 +93,7 @@
     own_diffs = warped_all - jnp.take(ref_block, piece_patch, axis=0)
     row_basis, col_basis = basis_pair(anchors, side_len)
     warp_terms = project_terms(warped_all, row_basis, col_basis)
-    against_cols = jnp.einsum("qpr,kur->qpku", ref_block, col_basis, precision=warp_mode)
+    against_cols = jnp.einsum("qpr,kur->qpku", ref_block, col_basis, precision=lax.Precision.DEFAULT)
     picked = against_cols[piece_patch, :, jnp.arange(piece_count), :]
     ref_terms = jnp.einsum("ktp,kpu->ktu", row_basis, picked, precision=exact_mode)
     partial_value = warp_terms - ref_terms

time: 160 us -> 155 us (0.969)
  matrix products: 64 us -> 58.8 us
    dot_general x1, matrix products: 18.1 us -> 12.6 us  [body(): jnp.einsum('qpr,kur->qpku', ref_block, col_basis, precision=lax.Precision...]
  transfers between devices with their start and end apart: 7 -> 7, of which waited for: 4 -> 4; matrix products, arithmetic and copies ran while one was open for 27% -> 28% of each run, Pallas kernels for 0% -> 0%
where the time goes in v7:
time: 155 us
  matrix products  58.8 us (38%)
  waiting for transfers between devices  57.3 us (37%)
  local copies, waits for them, and re-layouts  15.6 us (10%)
  between operations  14.3 us (9%)
  starting transfers between devices  8 us (5%)
    all_gather x1, waiting for transfers between devices, body(): lax.all_gather(ref_patch, PATCH_PARTS + VISIT_PARTS, axis=0, tiled=True)  52.4 us
    dot_general x1, matrix products, body(): jnp.einsum('qpr,kur->qpku', ref_block, col_basis, precision=lax.Precision...  12.6 us
    dot_general x1, matrix products, warp_batch(): return jnp.einsum('kib,kjb->kij', middle, right_matrix, precision=warp_mode)  11.9 us
    dot_general x1, matrix products, warp_batch(): jnp.einsum('kia,kab->kib', left_matrix, slab_images, precision=warp_mode)  11.6 us
    dot_general x1, matrix products, body(): fitted = jnp.einsum('kpu,kuq->kpq', middle, col_basis, precision=warp_mode)  11.3 us
    gather x1, local copies, waits for them, and re-layouts, body(): own_diffs = warped_all - jnp.take(ref_block, piece_patch, axis=0)  10.1 us
    ppermute x6, starting transfers between devices, ring_sum(): received.append(lax.ppermute(value, axis_name, pairs))  7.96 us
    dot_general x1, matrix products, project_terms(): jnp.einsum('mtp,mpq->mtq', row_basis, differences, precision=warp_mode)  5.78 us
  transfers between devices with their start and end apart: 7, of which 4 were waited for; matrix products, arithmetic and copies ran while one was open for 28% of the time, Pallas kernels for 0%

profile of v7, /device:TPU:0, one launch (start us, length us, event | category | flops | bytes accessed | tf_op | source)
XLA Modules:
  0.0 154.5 jit_solution(14116814183095906666)
XLA Ops:
  7.2 0.0 all-gather.2.cloned.1.call-start
  7.2 0.7 all-gather.2.cloned.1.call-update
  7.9 0.8 slice_bitcast_fusion.9
  8.7 0.8 slice_bitcast_fusion.8
  9.5 0.1 fusion.122
  9.6 0.1 iota_add_fusion
  9.7 11.6 %fusion.13 = f32[8,512,512]{2,1,0:T(8,128)S(1)} fusion(f32[8,512,512]{2,1,0:T(8,128)} %param.8, f32[8]{0:T(128)S(1)} %get-tuple-element.29, f32[8]{0:T(128)S(1)} %get-tuple-element.28, f32[8]{0:T(128)S(1)} %get-tuple-element.27, f32[8]{0:T(128)S(1)} %get-tuple-element.26, f32[8]{0:T(128)S(1)} %get-tuple-element.25, f32[8]{0:T(128)S(1)} %get-tuple-element.30, ...), kind=kOutput, calls=%fused_computation.18 | convolution fusion | flops 6469713920 | bytes 16793792 | tf_op jit(solution)/shard_map/kia,kab->kib/dot_general | solution.py:41
  21.3 0.0 copy-start.3
  21.3 0.0 copy-start.2
  21.3 0.0 copy-start.1
  21.3 11.9 %fusion = f32[8,512,512]{2,1,0:T(8,128)} fusion(f32[8,512,512]{2,1,0:T(8,128)S(1)} %fusion.13, f32[8]{0:T(128)S(1)} %get-tuple-element.6, f32[8]{0:T(128)S(1)} %get-tuple-element.7, f32[8]{0:T(128)S(1)} %get-tuple-element.8, f32[8]{0:T(128)S(1)} %get-tuple-element.9, f32[8]{0:T(128)S(1)} %get-tuple-element.10, f32[8]{0:T(128)S(1)} %get-tuple-element.5, ...), kind=kOutput, calls=%fused_computation.4 | convolution fusion | flops 6469713920 | bytes 16793792 | tf_op jit(solution)/shard_map/kib,kjb->kij/dot_general | solution.py:43
  33.3 0.0 copy-done.3
  33.3 0.0 copy-done.2
  33.3 0.0 copy-done.1
  33.4 0.2 sqrt_atan2_fusion
  33.5 5.8 %fusion.69 = f32[8,17,512]{2,1,0:T(8,128)S(1)} fusion(f32[8,512,512]{2,1,0:T(8,128)} %fusion, f32[8,512]{1,0:T(8,128)S(1)} %get-tuple-element.34, f32[17]{0:T(128)S(1)} %iota_convert_fusion), kind=kOutput, calls=%fused_computation.67 | convolution fusion | flops 213979136 | bytes 8683588 | tf_op jit(solution)/shard_map/mtp,mpq->mtq/dot_general | solution.py:64
  39.3 1.9 %fusion.67 = f32[8,17,17]{2,1,0:T(8,128)S(1)} fusion(f32[8,17,512]{2,1,0:T(8,128)S(1)} %fusion.69, f32[8,512]{1,0:T(8,128)S(1)} %get-tuple-element.33, f32[17]{0:T(128)S(1)} %iota_convert_fusion), kind=kOutput, calls=%fused_computation.64 | convolution fusion | flops 14274560 | bytes 304228 | tf_op jit(solution)/shard_map/mtq,muq->mtu/dot_general | solution.py:65
  41.2 52.4 %all-gather.2.cloned.1.call-done = f32[128,64,512]{2,1,0:T(8,128)} async-done(((f32[1,64,512]{2,1,0:T(8,128)}), f32[128,64,512]{2,1,0:T(8,128)}) %all-gather.2.cloned.1.call-update) | async-done | bytes 16777232 | tf_op jit(solution)/shard_map/all_gather | solution.py:87
  93.6 12.6 %convolution_bitcast_fusion = f32[16,512,8,17]{1,3,2,0:T(8,128)} fusion(f32[16,512,512,1]{2,1,3,0:T(8,128)} %bitcast.73, f32[8,512]{1,0:T(8,128)S(1)} %get-tuple-element.33, f32[17]{0:T(128)S(1)} %iota_convert_fusion), kind=kOutput, calls=%fused_computation.60 | convolution fusion | flops 1140920320 | bytes 21250116 | tf_op jit(solution)/shard_map/qpr,kur->qpku/dot_general | solution.py:96
  106.2 3.4 %gather_fusion.1 = f32[8,512,17]{1,2,0:T(8,128)S(1)} fusion(f32[16,512,8,17]{1,3,2,0:T(8,128)} %convolution_bitcast_fusion, s32[8]{0:T(128)S(1)} %get-tuple-element.3), kind=kCustom, calls=%fused_computation.1 | custom fusion | bytes 557120 | tf_op jit(solution)/shard_map/gather | solution.py:97
  109.6 1.8 %convolution_subtract_fusion = f32[8,17,17]{2,1,0:T(8,128)S(1)} fusion(f32[8,17,17]{2,1,0:T(8,128)S(1)} %fusion.67, f32[8,512,17]{1,2,0:T(8,128)S(1)} %gather_fusion.1, f32[8,512]{1,0:T(8,128)S(1)} %get-tuple-element.34, f32[17]{0:T(128)S(1)} %iota_convert_fusion), kind=kOutput, calls=%fused_computation.61 | convolution fusion | flops 14276872 | bytes 313476 | tf_op jit(solution)/shard_map/ktp,kpu->ktu/dot_general | solution.py:98
  111.4 0.2 fusion.83
  111.6 2.5 %collective-permute-start.2 = (f32[4,17,17]{2,0,1:T(4,128)S(1)}, f32[4,17,17]{2,0,1:T(4,128)S(1)}, u32[]{:S(2)}, u32[]{:S(2)}) collective-permute-start(f32[4,17,17]{2,0,1:T(4,128)S(1)} %fusion.83), channel_id=1, source_target_pairs={{0,3},{1,0},{2,1},{3,2},{4,7},{5,4},{6,5},{7,6},{8,11},{9,8},{10,9... | collective-permute-start | bytes 13880 | tf_op jit(solution)/shard_map/ppermute | solution.py:74
  114.1 0.7 collective-permute-start.1
  114.8 0.9 collective-permute-start
  115.8 10.1 %gather_fusion = f32[8,512,512]{2,1,0:T(8,128)} fusion(f32[16,512,512]{2,1,0:T(8,128)} %bitcast.74, s32[1024]{0:T(1024)S(1)} %pad_clamp_fusion.1), kind=kCustom, calls=%fused_computation | custom fusion | bytes 16777248 | tf_op jit(solution)/shard_map/jit(_take)/gather | solution.py:93
  125.8 0.0 collective-permute-done.2
  125.8 0.0 collective-permute-done.1
  125.8 0.0 collective-permute-done
  125.9 2.1 %collective-permute-start.5 = (f32[4,17,17]{2,0,1:T(4,128)S(1)}, f32[4,17,17]{2,0,1:T(4,128)S(1)}, u32[]{:S(2)}, u32[]{:S(2)}) collective-permute-start(f32[4,17,17]{2,0,1:T(4,128)S(1)} %fusion.203), channel_id=1, source_target_pairs={{0,12},{4,0},{8,4},{12,8},{1,13},{5,1},{9,5},{13,9},{2,14},{6,2},{... | collective-permute-start | bytes 13880 | tf_op jit(solution)/shard_map/ppermute | solution.py:74
  128.1 0.8 collective-permute-start.4
  128.9 0.9 collective-permute-start.3
  129.8 0.4 collective-permute-done.5
  130.2 3.3 %collective-permute-done.4 = f32[4,17,17]{2,0,1:T(4,128)S(1)} collective-permute-done((f32[4,17,17]{2,0,1:T(4,128)S(1)}, f32[4,17,17]{2,0,1:T(4,128)S(1)}, u32[]{:S(2)}, u32[]{:S(2)}) %collective-permute-start.4) | collective-permute-done | bytes 4656 | tf_op jit(solution)/shard_map/ppermute | solution.py:74
  133.5 0.5 collective-permute-done.3
  134.1 0.0 copy-start
  134.1 0.6 gather_fusion.2
  134.7 1.7 %fusion.68 = f32[8,512,17]{1,2,0:T(8,128)S(1)} fusion(f32[8,512]{1,0:T(8,128)S(1)} %get-tuple-element.34, f32[17]{0:T(128)S(1)} %iota_convert_fusion, f32[8,17,17]{2,1,0:T(8,128)S(1)} %gather_fusion.2, pred[8]{0:T(512)(128)(4,1)S(1)} %compare_and_fusion), kind=kOutput, calls=%fused_computation.66 | convolution fusion | flops 7174408 | bytes 304236 | tf_op jit(solution)/shard_map/ktp,ktu->kpu/dot_general | solution.py:104
  136.4 11.3 %subtract_subtract_fusion = f32[8,512,512]{2,1,0:T(8,128)} fusion(f32[8,512,512]{2,1,0:T(8,128)} %fusion, f32[8,512,512]{2,1,0:T(8,128)} %gather_fusion, pred[8]{0:T(512)(128)(4,1)S(1)} %compare_and_fusion.1, f32[8,512,17]{1,2,0:T(8,128)S(1)} %fusion.68, f32[8,512]{1,0:T(8,128)S(1)} %get-tuple-element.33, f32[17]{0:T(128)S(1)} %iota_convert_fusion), kind=kOutput, calls=%fused_computation.3 | convolution fusion | flops 220270592 | bytes 25460812 | tf_op jit(solution)/shard_map/kpu,kuq->kpq/dot_general | solution.py:105
  147.7 0.0 copy-done
  (16 shorter events, 0.2 us)
Async XLA Ops:
  7.2 86.4 %all-gather.2.cloned.1.call-start = ((), (), s32[]{:S(2)}) async-start(), calls=%async_computation | async-start | bytes 16908288 | tf_op jit(solution)/shard_map/all_gather | solution.py:87
  21.3 12.0 %copy-start.3 = (s32[8]{0:T(128)S(1)}, s32[8]{0:T(128)}, u32[]{:S(2)}) copy-start(s32[8]{0:T(128)} %param.10) | copy-start | bytes 100
  21.3 12.0 %copy-start.2 = (s32[8]{0:T(128)S(1)}, s32[8]{0:T(128)}, u32[]{:S(2)}) copy-start(s32[8]{0:T(128)} %param.11) | copy-start | bytes 100
  21.3 12.0 %copy-start.1 = (s32[8,2]{0,1:T(2,128)S(1)}, s32[8,2]{0,1:T(2,128)}, u32[]{:S(2)}) copy-start(s32[8,2]{0,1:T(2,128)} %param.12) | copy-start | bytes 196
  111.6 14.3 %collective-permute-start.2 = (f32[4,17,17]{2,0,1:T(4,128)S(1)}, f32[4,17,17]{2,0,1:T(4,128)S(1)}, u32[]{:S(2)}, u32[]{:S(2)}) collective-permute-start(f32[4,17,17]{2,0,1:T(4,128)S(1)} %fusion.83), channel_id=1, source_target_pairs={{0,3},{1,0},{2,1},{3,2},{4,7},{5,4},{6,5},{7,6},{8,11},{9,8},{10,9... | collective-permute-start | bytes 13880 | tf_op jit(solution)/shard_map/ppermute | solution.py:74
  114.1 11.7 %collective-permute-start.1 = (f32[4,17,17]{2,0,1:T(4,128)S(1)}, f32[4,17,17]{2,0,1:T(4,128)S(1)}, u32[]{:S(2)}, u32[]{:S(2)}) collective-permute-start(f32[4,17,17]{2,0,1:T(4,128)S(1)} %fusion.83), channel_id=1, source_target_pairs={{0,2},{1,3},{2,0},{3,1},{4,6},{5,7},{6,4},{7,5},{8,10},{9,11},{10,... | collective-permute-start | bytes 13880 | tf_op jit(solution)/shard_map/ppermute | solution.py:74
  114.8 11.0 %collective-permute-start = (f32[4,17,17]{2,0,1:T(4,128)S(1)}, f32[4,17,17]{2,0,1:T(4,128)S(1)}, u32[]{:S(2)}, u32[]{:S(2)}) collective-permute-start(f32[4,17,17]{2,0,1:T(4,128)S(1)} %fusion.83), channel_id=1, source_target_pairs={{0,1},{1,2},{2,3},{3,0},{4,5},{5,6},{6,7},{7,4},{8,9},{9,10},{10,1... | collective-permute-start | bytes 13880 | tf_op jit(solution)/shard_map/ppermute | solution.py:74
  125.9 4.2 %collective-permute-start.5 = (f32[4,17,17]{2,0,1:T(4,128)S(1)}, f32[4,17,17]{2,0,1:T(4,128)S(1)}, u32[]{:S(2)}, u32[]{:S(2)}) collective-permute-start(f32[4,17,17]{2,0,1:T(4,128)S(1)} %fusion.203), channel_id=1, source_target_pairs={{0,12},{4,0},{8,4},{12,8},{1,13},{5,1},{9,5},{13,9},{2,14},{6,2},{... | collective-permute-start | bytes 13880 | tf_op jit(solution)/shard_map/ppermute | solution.py:74
  128.1 5.4 %collective-permute-start.4 = (f32[4,17,17]{2,0,1:T(4,128)S(1)}, f32[4,17,17]{2,0,1:T(4,128)S(1)}, u32[]{:S(2)}, u32[]{:S(2)}) collective-permute-start(f32[4,17,17]{2,0,1:T(4,128)S(1)} %fusion.203), channel_id=1, source_target_pairs={{0,8},{4,12},{8,0},{12,4},{1,9},{5,13},{9,1},{13,5},{2,10},{6,14},... | collective-permute-start | bytes 13880 | tf_op jit(solution)/shard_map/ppermute | solution.py:74
  128.9 5.1 %collective-permute-start.3 = (f32[4,17,17]{2,0,1:T(4,128)S(1)}, f32[4,17,17]{2,0,1:T(4,128)S(1)}, u32[]{:S(2)}, u32[]{:S(2)}) collective-permute-start(f32[4,17,17]{2,0,1:T(4,128)S(1)} %fusion.203), channel_id=1, source_target_pairs={{0,4},{4,8},{8,12},{12,0},{1,5},{5,9},{9,13},{13,1},{2,6},{6,10},{... | collective-permute-start | bytes 13880 | tf_op jit(solution)/shard_map/ppermute | solution.py:74
  134.1 13.6 %copy-start = (f32[4,17,17]{2,0,1:T(4,128)}, f32[4,17,17]{2,0,1:T(4,128)S(1)}, u32[]{:S(2)}) copy-start(f32[4,17,17]{2,0,1:T(4,128)S(1)} %multiply_bitcast_fusion) | copy-start | bytes 13876
Sparse Core Ops, SparseCore 0:
  11.1 82.4 all-gather.1

commit v8 on v7

--- a/solution.py
+++ b/solution.py
@@ -1,6 +1,8 @@
 import jax
 import jax.numpy as jnp
 from jax import lax
+from jax.experimental import pallas as pl
+from jax.experimental.pallas import tpu as pltpu
 from jax.sharding import Mesh
 from jax.sharding import PartitionSpec as P
 
@@ -65,6 +67,44 @@
     return jnp.einsum("mtq,muq->mtu", middle, col_basis, precision=exact_mode)
 
 
+BASIS_ROWS = 24
+
+
+def reference_terms_kernel(patch_of, ref_ref, row_ref, col_ref, out_ref):
+    middle = jnp.dot(row_ref[0], ref_ref[0], preferred_element_type=jnp.float32, precision=exact_mode)
+    out_ref[0] = lax.dot_general(
+        middle, col_ref[0], (((1,), (1,)), ((), ())), preferred_element_type=jnp.float32, precision=exact_mode
+    )
+
+
+def reference_terms(ref_block, piece_patch, row_basis, col_basis):
+    piece_count, terms, side_len = row_basis.shape
+    pad = ((0, 0), (0, BASIS_ROWS - terms), (0, 0))
+    rows = jnp.pad(row_basis, pad)
+    cols = jnp.pad(col_basis, pad)
+    basis_spec = pl.BlockSpec((1, BASIS_ROWS, side_len), lambda k, patch_of: (k, 0, 0))
+    out = pl.pallas_call(
+        reference_terms_kernel,
+        out_shape=jax.ShapeDtypeStruct((piece_count, BASIS_ROWS, BASIS_ROWS), jnp.float32),
+        grid_spec=pltpu.PrefetchScalarGridSpec(
+            num_scalar_prefetch=1,
+            grid=(piece_count,),
+            in_specs=[
+                pl.BlockSpec((1, side_len, side_len), lambda k, patch_of: (patch_of[k], 0, 0)),
+                basis_spec,
+                basis_spec,
+            ],
+            out_specs=pl.BlockSpec((1, BASIS_ROWS, BASIS_ROWS), lambda k, patch_of: (k, 0, 0)),
+        ),
+        cost_estimate=pl.CostEstimate(
+            flops=2 * piece_count * BASIS_ROWS * side_len * (side_len + BASIS_ROWS),
+            bytes_accessed=4 * piece_count * side_len * (side_len + 2 * BASIS_ROWS),
+            transcendentals=0,
+        ),
+    )(piece_patch, ref_block, rows, cols)
+    return out[:, :terms, :terms]
+
+
 def ring_sum(value, axis_name):
     count = lax.axis_size(axis_name)
     me = lax.axis_index(axis_name)
@@ -93,9 +133,7 @@
     own_diffs = warped_all - jnp.take(ref_block, piece_patch, axis=0)
     row_basis, col_basis = basis_pair(anchors, side_len)
     warp_terms = project_terms(warped_all, row_basis, col_basis)
-    against_cols = jnp.einsum("qpr,kur->qpku", ref_block, col_basis, precision=lax.Precision.DEFAULT)
-    picked = against_cols[piece_patch, :, jnp.arange(piece_count), :]
-    ref_terms = jnp.einsum("ktp,kpu->ktu", row_basis, picked, precision=exact_mode)
+    ref_terms = reference_terms(ref_block, piece_patch, row_basis, col_basis)
     partial_value = warp_terms - ref_terms
     local_sums = jnp.einsum("kv,ktu->vtu", own_onehot, partial_value, precision=exact_mode)
     totals = ring_sum(ring_sum(local_sums, "pz"), "px")

time: 155 us -> 150 us (0.968)
  matrix products: 58.8 us -> 44.9 us
  Pallas kernels: 0 us -> 10.2 us
  waiting for transfers between devices: 57.3 us -> 54.4 us
  other arithmetic: 0.54 us -> 3.1 us
    dot_general x2 -> x0, matrix products: 14.5 us -> none  [the longest x1 12.6 us: body(): jnp.einsum('qpr,kur->qpku', ref_block, col_basis, precision=lax.Precision...]
    pallas_call x0 -> x1, Pallas kernels: none -> 10.2 us  [reference_terms(): pl.pallas_call(reference_terms_kernel, out_shape=jax.ShapeDtypeStruct((pi...]
    gather x1 -> x0, local copies, waits for them, and re-layouts: 3.36 us -> none  [body(): picked = against_cols[piece_patch, :, jnp.arange(piece_count), :]]
    all_gather x1, waiting for transfers between devices: 52.4 us -> 49.5 us  [body(): lax.all_gather(ref_patch, PATCH_PARTS + VISIT_PARTS, axis=0, tiled=True)]
    cos x0 -> x1, other arithmetic: none -> 2.56 us  [chebyshev_rows(): return jnp.cos(orders[:, None] * jnp.arccos(coordinate)[None, :])]
  transfers between devices with their start and end apart: 7 -> 7, of which waited for: 4 -> 3; matrix products, arithmetic and copies ran while one was open for 28% -> 31% of each run, Pallas kernels for 0% -> 0%
where the time goes in v8:
time: 150 us
  waiting for transfers between devices  54.4 us (36%)
  matrix products  44.9 us (30%)
  local copies, waits for them, and re-layouts  14.5 us (10%)
  between operations  14.2 us (9%)
  Pallas kernels  10.2 us (7%)
  starting transfers between devices  8.18 us (5%)
  other arithmetic  3.1 us (2%)
    all_gather x1, waiting for transfers between devices, body(): lax.all_gather(ref_patch, PATCH_PARTS + VISIT_PARTS, axis=0, tiled=True)  49.5 us
    dot_general x1, matrix products, warp_batch(): return jnp.einsum('kib,kjb->kij', middle, right_matrix, precision=warp_mode)  11.9 us
    dot_general x1, matrix products, warp_batch(): jnp.einsum('kia,kab->kib', left_matrix, slab_images, precision=warp_mode)  11.8 us
    dot_general x1, matrix products, body(): fitted = jnp.einsum('kpu,kuq->kpq', middle, col_basis, precision=warp_mode)  11.1 us
    pallas_call x1, Pallas kernels, reference_terms(): pl.pallas_call(reference_terms_kernel, out_shape=jax.ShapeDtypeStruct((pi...  10.2 us
    gather x1, local copies, waits for them, and re-layouts, body(): own_diffs = warped_all - jnp.take(ref_block, piece_patch, axis=0)  10.1 us
    ppermute x6, starting transfers between devices, ring_sum(): received.append(lax.ppermute(value, axis_name, pairs))  8.14 us
    dot_general x1, matrix products, project_terms(): jnp.einsum('mtp,mpq->mtq', row_basis, differences, precision=warp_mode)  5.59 us
  transfers between devices with their start and end apart: 7, of which 3 were waited for; matrix products, arithmetic and copies ran while one was open for 31% of the time, Pallas kernels for 0%

profile of v8, /device:TPU:0, one launch (start us, length us, event | category | flops | bytes accessed | tf_op | source)
XLA Modules:
  0.0 149.5 jit_solution(4540660397670786808)
XLA Ops:
  7.2 0.0 all-gather.2.cloned.1.call-start
  7.2 0.7 all-gather.2.cloned.1.call-update
  7.9 0.8 slice_bitcast_fusion
  8.7 0.2 sqrt_atan2_fusion
  8.9 2.6 %multiply_cosine_fusion = (f32[8,17,512]{2,1,0:T(8,128)S(1)}, f32[8,17,512]{2,1,0:T(8,128)S(1)}) fusion(f32[8,512]{1,0:T(8,128)S(1)} %get-tuple-element.33, f32[17]{0:T(128)S(1)} %iota_convert_fusion, f32[8,512]{1,0:T(8,128)S(1)} %get-tuple-element.34), kind=kLoop, calls=%fused_computation.60 | loop fusion | flops 139264 | bytes 589892 | tf_op jit(solution)/shard_map/vmap()/cos | solution.py:52
  11.4 0.8 pad.8.col_ref
  12.2 0.8 pad.7.row_ref
  13.0 0.8 slice_bitcast_fusion.9
  13.7 0.8 slice_bitcast_fusion.8
  14.5 0.1 fusion.116
  14.6 0.1 iota_add_fusion
  14.7 11.8 %fusion.13 = f32[8,512,512]{2,1,0:T(8,128)S(1)} fusion(f32[8,512,512]{2,1,0:T(8,128)} %param.8, f32[8]{0:T(128)S(1)} %get-tuple-element.29, f32[8]{0:T(128)S(1)} %get-tuple-element.28, f32[8]{0:T(128)S(1)} %get-tuple-element.27, f32[8]{0:T(128)S(1)} %get-tuple-element.26, f32[8]{0:T(128)S(1)} %get-tuple-element.25, f32[8]{0:T(128)S(1)} %get-tuple-element.30, ...), kind=kOutput, calls=%fused_computation.17 | convolution fusion | flops 6469713920 | bytes 16793792 | tf_op jit(solution)/shard_map/kia,kab->kib/dot_general | solution.py:43
  26.5 0.0 copy-start.2
  26.5 0.0 copy-start.1
  26.5 11.9 %fusion = f32[8,512,512]{2,1,0:T(8,128)} fusion(f32[8,512,512]{2,1,0:T(8,128)S(1)} %fusion.13, f32[8]{0:T(128)S(1)} %get-tuple-element.4, f32[8]{0:T(128)S(1)} %get-tuple-element.5, f32[8]{0:T(128)S(1)} %get-tuple-element.6, f32[8]{0:T(128)S(1)} %get-tuple-element.7, f32[8]{0:T(128)S(1)} %get-tuple-element.8, f32[8]{0:T(128)S(1)} %get-tuple-element.3, ...), kind=kOutput, calls=%fused_computation.3 | convolution fusion | flops 6469713920 | bytes 16793792 | tf_op jit(solution)/shard_map/kib,kjb->kij/dot_general | solution.py:45
  38.4 0.0 copy-done.2
  38.4 0.0 copy-done.1
  38.5 5.6 %fusion.67 = f32[8,17,512]{2,1,0:T(8,128)S(1)} fusion(f32[8,512,512]{2,1,0:T(8,128)} %fusion, f32[8,512]{1,0:T(8,128)S(1)} %get-tuple-element.34, f32[17]{0:T(128)S(1)} %iota_convert_fusion), kind=kOutput, calls=%fused_computation.63 | convolution fusion | flops 213979136 | bytes 8683588 | tf_op jit(solution)/shard_map/mtp,mpq->mtq/dot_general | solution.py:66
  44.1 49.5 %all-gather.2.cloned.1.call-done = f32[128,64,512]{2,1,0:T(8,128)} async-done(((f32[1,64,512]{2,1,0:T(8,128)}), f32[128,64,512]{2,1,0:T(8,128)}) %all-gather.2.cloned.1.call-update) | async-done | bytes 16777232 | tf_op jit(solution)/shard_map/all_gather | solution.py:127
  93.6 10.2 %shard_map.86 = f32[8,24,24]{2,1,0:T(8,128)} custom-call(s32[8]{0:T(128)} %patch_of.1, f32[16,512,512]{2,1,0:T(8,128)} %bitcast.56, f32[8,24,512]{2,1,0:T(8,128)} %pad.7.row_ref, f32[8,24,512]{2,1,0:T(8,128)} %pad.8.col_ref), custom_call_target="tpu_custom_call" | custom-call | flops 105381888 | bytes 9175040 | tf_op jit(solution)/shard_map/pallas_call | solution.py:86
  103.8 2.7 %convolution_subtract_fusion = f32[8,17,17]{2,1,0:T(8,128)S(1)} fusion(f32[8,17,512]{2,1,0:T(8,128)S(1)} %fusion.67, f32[8,512]{1,0:T(8,128)S(1)} %get-tuple-element.33, f32[17]{0:T(128)S(1)} %iota_convert_fusion, f32[8,24,24]{2,1,0:T(8,128)} %shard_map.86), kind=kOutput, calls=%fused_computation.59 | convolution fusion | flops 14276872 | bytes 313476 | tf_op jit(solution)/shard_map/mtq,muq->mtu/dot_general | solution.py:67
  106.6 0.2 fusion.77
  106.7 2.7 %collective-permute-start.2 = (f32[4,17,17]{2,0,1:T(4,128)S(1)}, f32[4,17,17]{2,0,1:T(4,128)S(1)}, u32[]{:S(2)}, u32[]{:S(2)}) collective-permute-start(f32[4,17,17]{2,0,1:T(4,128)S(1)} %fusion.77), channel_id=1, source_target_pairs={{0,3},{1,0},{2,1},{3,2},{4,7},{5,4},{6,5},{7,6},{8,11},{9,8},{10,9... | collective-permute-start | bytes 13880 | tf_op jit(solution)/shard_map/ppermute | solution.py:114
  109.5 0.5 collective-permute-start.1
  109.9 0.6 collective-permute-start
  110.5 10.1 %gather_fusion = f32[8,512,512]{2,1,0:T(8,128)} fusion(f32[16,512,512]{2,1,0:T(8,128)} %bitcast.57, s32[1024]{0:T(1024)S(1)} %pad_clamp_fusion.1), kind=kCustom, calls=%fused_computation | custom fusion | bytes 16777248 | tf_op jit(solution)/shard_map/jit(_take)/gather | solution.py:133
  120.6 0.0 collective-permute-done.2
  120.6 0.0 collective-permute-done.1
  120.6 0.0 collective-permute-done
  120.7 2.6 %collective-permute-start.5 = (f32[4,17,17]{2,0,1:T(4,128)S(1)}, f32[4,17,17]{2,0,1:T(4,128)S(1)}, u32[]{:S(2)}, u32[]{:S(2)}) collective-permute-start(f32[4,17,17]{2,0,1:T(4,128)S(1)} %fusion.194), channel_id=1, source_target_pairs={{0,12},{4,0},{8,4},{12,8},{1,13},{5,1},{9,5},{13,9},{2,14},{6,2},{... | collective-permute-start | bytes 13880 | tf_op jit(solution)/shard_map/ppermute | solution.py:114
  123.3 0.8 collective-permute-start.4
  124.1 1.0 collective-permute-start.3
  125.1 0.0 collective-permute-done.5
  125.1 3.6 %collective-permute-done.4 = f32[4,17,17]{2,0,1:T(4,128)S(1)} collective-permute-done((f32[4,17,17]{2,0,1:T(4,128)S(1)}, f32[4,17,17]{2,0,1:T(4,128)S(1)}, u32[]{:S(2)}, u32[]{:S(2)}) %collective-permute-start.4) | collective-permute-done | bytes 4656 | tf_op jit(solution)/shard_map/ppermute | solution.py:114
  128.7 0.5 collective-permute-done.3
  129.3 0.0 copy-start
  129.3 0.6 gather_fusion.1
  129.9 1.7 %fusion.66 = f32[8,512,17]{1,2,0:T(8,128)S(1)} fusion(f32[8,512]{1,0:T(8,128)S(1)} %get-tuple-element.34, f32[17]{0:T(128)S(1)} %iota_convert_fusion, f32[8,17,17]{2,1,0:T(8,128)S(1)} %gather_fusion.1, pred[8]{0:T(512)(128)(4,1)S(1)} %compare_and_fusion), kind=kOutput, calls=%fused_computation.62 | convolution fusion | flops 7174408 | bytes 304236 | tf_op jit(solution)/shard_map/ktp,ktu->kpu/dot_general | solution.py:142
  131.6 11.1 %subtract_subtract_fusion = f32[8,512,512]{2,1,0:T(8,128)} fusion(f32[8,512,512]{2,1,0:T(8,128)} %fusion, f32[8,512,512]{2,1,0:T(8,128)} %gather_fusion, pred[8]{0:T(512)(128)(4,1)S(1)} %compare_and_fusion.1, f32[8,512,17]{1,2,0:T(8,128)S(1)} %fusion.66, f32[8,512]{1,0:T(8,128)S(1)} %get-tuple-element.33, f32[17]{0:T(128)S(1)} %iota_convert_fusion), kind=kOutput, calls=%fused_computation.2 | convolution fusion | flops 220270592 | bytes 25460812 | tf_op jit(solution)/shard_map/kpu,kuq->kpq/dot_general | solution.py:143
  142.7 0.0 copy-done
  (15 shorter events, 0.2 us)
Async XLA Ops:
  7.2 86.4 %all-gather.2.cloned.1.call-start = ((), (), s32[]{:S(2)}) async-start(), calls=%async_computation | async-start | bytes 16908288 | tf_op jit(solution)/shard_map/all_gather | solution.py:127
  26.5 11.9 %copy-start.2 = (s32[8]{0:T(128)S(1)}, s32[8]{0:T(128)}, u32[]{:S(2)}) copy-start(s32[8]{0:T(128)} %param.11) | copy-start | bytes 100
  26.5 11.9 %copy-start.1 = (s32[8]{0:T(128)S(1)}, s32[8]{0:T(128)}, u32[]{:S(2)}) copy-start(s32[8]{0:T(128)} %patch_of.1) | copy-start | bytes 100
  106.7 13.9 %collective-permute-start.2 = (f32[4,17,17]{2,0,1:T(4,128)S(1)}, f32[4,17,17]{2,0,1:T(4,128)S(1)}, u32[]{:S(2)}, u32[]{:S(2)}) collective-permute-start(f32[4,17,17]{2,0,1:T(4,128)S(1)} %fusion.77), channel_id=1, source_target_pairs={{0,3},{1,0},{2,1},{3,2},{4,7},{5,4},{6,5},{7,6},{8,11},{9,8},{10,9... | collective-permute-start | bytes 13880 | tf_op jit(solution)/shard_map/ppermute | solution.py:114
  109.5 11.1 %collective-permute-start.1 = (f32[4,17,17]{2,0,1:T(4,128)S(1)}, f32[4,17,17]{2,0,1:T(4,128)S(1)}, u32[]{:S(2)}, u32[]{:S(2)}) collective-permute-start(f32[4,17,17]{2,0,1:T(4,128)S(1)} %fusion.77), channel_id=1, source_target_pairs={{0,2},{1,3},{2,0},{3,1},{4,6},{5,7},{6,4},{7,5},{8,10},{9,11},{10,... | collective-permute-start | bytes 13880 | tf_op jit(solution)/shard_map/ppermute | solution.py:114
  109.9 10.6 %collective-permute-start = (f32[4,17,17]{2,0,1:T(4,128)S(1)}, f32[4,17,17]{2,0,1:T(4,128)S(1)}, u32[]{:S(2)}, u32[]{:S(2)}) collective-permute-start(f32[4,17,17]{2,0,1:T(4,128)S(1)} %fusion.77), channel_id=1, source_target_pairs={{0,1},{1,2},{2,3},{3,0},{4,5},{5,6},{6,7},{7,4},{8,9},{9,10},{10,1... | collective-permute-start | bytes 13880 | tf_op jit(solution)/shard_map/ppermute | solution.py:114
  120.7 4.4 %collective-permute-start.5 = (f32[4,17,17]{2,0,1:T(4,128)S(1)}, f32[4,17,17]{2,0,1:T(4,128)S(1)}, u32[]{:S(2)}, u32[]{:S(2)}) collective-permute-start(f32[4,17,17]{2,0,1:T(4,128)S(1)} %fusion.194), channel_id=1, source_target_pairs={{0,12},{4,0},{8,4},{12,8},{1,13},{5,1},{9,5},{13,9},{2,14},{6,2},{... | collective-permute-start | bytes 13880 | tf_op jit(solution)/shard_map/ppermute | solution.py:114
  123.3 5.4 %collective-permute-start.4 = (f32[4,17,17]{2,0,1:T(4,128)S(1)}, f32[4,17,17]{2,0,1:T(4,128)S(1)}, u32[]{:S(2)}, u32[]{:S(2)}) collective-permute-start(f32[4,17,17]{2,0,1:T(4,128)S(1)} %fusion.194), channel_id=1, source_target_pairs={{0,8},{4,12},{8,0},{12,4},{1,9},{5,13},{9,1},{13,5},{2,10},{6,14},... | collective-permute-start | bytes 13880 | tf_op jit(solution)/shard_map/ppermute | solution.py:114
  124.1 5.1 %collective-permute-start.3 = (f32[4,17,17]{2,0,1:T(4,128)S(1)}, f32[4,17,17]{2,0,1:T(4,128)S(1)}, u32[]{:S(2)}, u32[]{:S(2)}) collective-permute-start(f32[4,17,17]{2,0,1:T(4,128)S(1)} %fusion.194), channel_id=1, source_target_pairs={{0,4},{4,8},{8,12},{12,0},{1,5},{5,9},{9,13},{13,1},{2,6},{6,10},{... | collective-permute-start | bytes 13880 | tf_op jit(solution)/shard_map/ppermute | solution.py:114
  129.3 13.4 %copy-start = (f32[4,17,17]{2,0,1:T(4,128)}, f32[4,17,17]{2,0,1:T(4,128)S(1)}, u32[]{:S(2)}) copy-start(f32[4,17,17]{2,0,1:T(4,128)S(1)} %multiply_bitcast_fusion) | copy-start | bytes 13876
Sparse Core Ops, SparseCore 0:
  11.1 82.4 all-gather.1

commit v9 on v8

--- a/solution.py
+++ b/solution.py
@@ -71,10 +71,10 @@
 
 
 def reference_terms_kernel(patch_of, ref_ref, row_ref, col_ref, out_ref):
-    middle = jnp.dot(row_ref[0], ref_ref[0], preferred_element_type=jnp.float32, precision=exact_mode)
-    out_ref[0] = lax.dot_general(
-        middle, col_ref[0], (((1,), (1,)), ((), ())), preferred_element_type=jnp.float32, precision=exact_mode
+    against_cols = lax.dot_general(
+        ref_ref[0], col_ref[0], (((1,), (1,)), ((), ())), preferred_element_type=jnp.float32, precision=exact_mode
     )
+    out_ref[0] = jnp.dot(row_ref[0], against_cols, preferred_element_type=jnp.float32, precision=exact_mode)
 
 
 def reference_terms(ref_block, piece_patch, row_basis, col_basis):

time: 150 us -> 153 us (1.020)
  Pallas kernels: 10.2 us -> 13.2 us
    pallas_call x1, Pallas kernels: 10.2 us -> 13.2 us  [reference_terms(): pl.pallas_call(reference_terms_kernel, out_shape=jax.ShapeDtypeStruct((pi...]
  transfers between devices with their start and end apart: 7 -> 7, of which waited for: 3 -> 4; matrix products, arithmetic and copies ran while one was open for 31% -> 30% of each run, Pallas kernels for 0% -> 0%
where the time goes in v9:
time: 153 us
  waiting for transfers between devices  54.5 us (36%)
  matrix products  44.9 us (29%)
  local copies, waits for them, and re-layouts  14.5 us (9%)
  between operations  14.2 us (9%)
  Pallas kernels  13.2 us (9%)
  starting transfers between devices  8.21 us (5%)
  other arithmetic  3.1 us (2%)
    all_gather x1, waiting for transfers between devices, body(): lax.all_gather(ref_patch, PATCH_PARTS + VISIT_PARTS, axis=0, tiled=True)  49.5 us
    pallas_call x1, Pallas kernels, reference_terms(): pl.pallas_call(reference_terms_kernel, out_shape=jax.ShapeDtypeStruct((pi...  13.2 us
    dot_general x1, matrix products, warp_batch(): return jnp.einsum('kib,kjb->kij', middle, right_matrix, precision=warp_mode)  11.9 us
    dot_general x1, matrix products, warp_batch(): jnp.einsum('kia,kab->kib', left_matrix, slab_images, precision=warp_mode)  11.8 us
    dot_general x1, matrix products, body(): fitted = jnp.einsum('kpu,kuq->kpq', middle, col_basis, precision=warp_mode)  11.1 us
    gather x1, local copies, waits for them, and re-layouts, body(): own_diffs = warped_all - jnp.take(ref_block, piece_patch, axis=0)  10.1 us
    ppermute x6, starting transfers between devices, ring_sum(): received.append(lax.ppermute(value, axis_name, pairs))  8.17 us
    dot_general x1, matrix products, project_terms(): jnp.einsum('mtp,mpq->mtq', row_basis, differences, precision=warp_mode)  5.59 us
  transfers between devices with their start and end apart: 7, of which 4 were waited for; matrix products, arithmetic and copies ran while one was open for 30% of the time, Pallas kernels for 0%

profile of v9, /device:TPU:0, one launch (start us, length us, event | category | flops | bytes accessed | tf_op | source)
XLA Modules:
  0.0 152.6 jit_solution(6397096405692332113)
XLA Ops:
  7.2 0.0 all-gather.2.cloned.1.call-start
  7.2 0.7 all-gather.2.cloned.1.call-update
  7.9 0.8 slice_bitcast_fusion
  8.7 0.2 sqrt_atan2_fusion
  8.9 2.6 %multiply_cosine_fusion = (f32[8,17,512]{2,1,0:T(8,128)S(1)}, f32[8,17,512]{2,1,0:T(8,128)S(1)}) fusion(f32[8,512]{1,0:T(8,128)S(1)} %get-tuple-element.33, f32[17]{0:T(128)S(1)} %iota_convert_fusion, f32[8,512]{1,0:T(8,128)S(1)} %get-tuple-element.34), kind=kLoop, calls=%fused_computation.60 | loop fusion | flops 139264 | bytes 589892 | tf_op jit(solution)/shard_map/vmap()/cos | solution.py:52
  11.4 0.8 pad.8.col_ref
  12.2 0.8 pad.7.row_ref
  13.0 0.8 slice_bitcast_fusion.9
  13.7 0.8 slice_bitcast_fusion.8
  14.5 0.1 fusion.116
  14.6 0.1 iota_add_fusion
  14.7 11.8 %fusion.13 = f32[8,512,512]{2,1,0:T(8,128)S(1)} fusion(f32[8,512,512]{2,1,0:T(8,128)} %param.8, f32[8]{0:T(128)S(1)} %get-tuple-element.29, f32[8]{0:T(128)S(1)} %get-tuple-element.28, f32[8]{0:T(128)S(1)} %get-tuple-element.27, f32[8]{0:T(128)S(1)} %get-tuple-element.26, f32[8]{0:T(128)S(1)} %get-tuple-element.25, f32[8]{0:T(128)S(1)} %get-tuple-element.30, ...), kind=kOutput, calls=%fused_computation.17 | convolution fusion | flops 6469713920 | bytes 16793792 | tf_op jit(solution)/shard_map/kia,kab->kib/dot_general | solution.py:43
  26.5 0.0 copy-start.2
  26.5 0.0 copy-start.1
  26.5 11.9 %fusion = f32[8,512,512]{2,1,0:T(8,128)} fusion(f32[8,512,512]{2,1,0:T(8,128)S(1)} %fusion.13, f32[8]{0:T(128)S(1)} %get-tuple-element.4, f32[8]{0:T(128)S(1)} %get-tuple-element.5, f32[8]{0:T(128)S(1)} %get-tuple-element.6, f32[8]{0:T(128)S(1)} %get-tuple-element.7, f32[8]{0:T(128)S(1)} %get-tuple-element.8, f32[8]{0:T(128)S(1)} %get-tuple-element.3, ...), kind=kOutput, calls=%fused_computation.3 | convolution fusion | flops 6469713920 | bytes 16793792 | tf_op jit(solution)/shard_map/kib,kjb->kij/dot_general | solution.py:45
  38.4 0.0 copy-done.2
  38.4 0.0 copy-done.1
  38.5 5.6 %fusion.67 = f32[8,17,512]{2,1,0:T(8,128)S(1)} fusion(f32[8,512,512]{2,1,0:T(8,128)} %fusion, f32[8,512]{1,0:T(8,128)S(1)} %get-tuple-element.34, f32[17]{0:T(128)S(1)} %iota_convert_fusion), kind=kOutput, calls=%fused_computation.63 | convolution fusion | flops 213979136 | bytes 8683588 | tf_op jit(solution)/shard_map/mtp,mpq->mtq/dot_general | solution.py:66
  44.1 49.5 %all-gather.2.cloned.1.call-done = f32[128,64,512]{2,1,0:T(8,128)} async-done(((f32[1,64,512]{2,1,0:T(8,128)}), f32[128,64,512]{2,1,0:T(8,128)}) %all-gather.2.cloned.1.call-update) | async-done | bytes 16777232 | tf_op jit(solution)/shard_map/all_gather | solution.py:127
  93.6 13.2 %shard_map.86 = f32[8,24,24]{2,1,0:T(8,128)} custom-call(s32[8]{0:T(128)} %patch_of.1, f32[16,512,512]{2,1,0:T(8,128)} %bitcast.56, f32[8,24,512]{2,1,0:T(8,128)} %pad.7.row_ref, f32[8,24,512]{2,1,0:T(8,128)} %pad.8.col_ref), custom_call_target="tpu_custom_call" | custom-call | flops 105381888 | bytes 9175040 | tf_op jit(solution)/shard_map/pallas_call | solution.py:86
  106.8 2.7 %convolution_subtract_fusion = f32[8,17,17]{2,1,0:T(8,128)S(1)} fusion(f32[8,17,512]{2,1,0:T(8,128)S(1)} %fusion.67, f32[8,512]{1,0:T(8,128)S(1)} %get-tuple-element.33, f32[17]{0:T(128)S(1)} %iota_convert_fusion, f32[8,24,24]{2,1,0:T(8,128)} %shard_map.86), kind=kOutput, calls=%fused_computation.59 | convolution fusion | flops 14276872 | bytes 313476 | tf_op jit(solution)/shard_map/mtq,muq->mtu/dot_general | solution.py:67
  109.5 0.2 fusion.77
  109.7 2.5 %collective-permute-start.2 = (f32[4,17,17]{2,0,1:T(4,128)S(1)}, f32[4,17,17]{2,0,1:T(4,128)S(1)}, u32[]{:S(2)}, u32[]{:S(2)}) collective-permute-start(f32[4,17,17]{2,0,1:T(4,128)S(1)} %fusion.77), channel_id=1, source_target_pairs={{0,3},{1,0},{2,1},{3,2},{4,7},{5,4},{6,5},{7,6},{8,11},{9,8},{10,9... | collective-permute-start | bytes 13880 | tf_op jit(solution)/shard_map/ppermute | solution.py:114
  112.2 0.7 collective-permute-start.1
  112.9 0.9 collective-permute-start
  113.9 10.1 %gather_fusion = f32[8,512,512]{2,1,0:T(8,128)} fusion(f32[16,512,512]{2,1,0:T(8,128)} %bitcast.57, s32[1024]{0:T(1024)S(1)} %pad_clamp_fusion.1), kind=kCustom, calls=%fused_computation | custom fusion | bytes 16777248 | tf_op jit(solution)/shard_map/jit(_take)/gather | solution.py:133
  123.9 0.0 collective-permute-done.2
  123.9 0.0 collective-permute-done.1
  123.9 0.0 collective-permute-done
  124.0 2.3 %collective-permute-start.5 = (f32[4,17,17]{2,0,1:T(4,128)S(1)}, f32[4,17,17]{2,0,1:T(4,128)S(1)}, u32[]{:S(2)}, u32[]{:S(2)}) collective-permute-start(f32[4,17,17]{2,0,1:T(4,128)S(1)} %fusion.194), channel_id=1, source_target_pairs={{0,12},{4,0},{8,4},{12,8},{1,13},{5,1},{9,5},{13,9},{2,14},{6,2},{... | collective-permute-start | bytes 13880 | tf_op jit(solution)/shard_map/ppermute | solution.py:114
  126.3 0.8 collective-permute-start.4
  127.2 0.9 collective-permute-start.3
  128.1 0.4 collective-permute-done.5
  128.5 3.3 %collective-permute-done.4 = f32[4,17,17]{2,0,1:T(4,128)S(1)} collective-permute-done((f32[4,17,17]{2,0,1:T(4,128)S(1)}, f32[4,17,17]{2,0,1:T(4,128)S(1)}, u32[]{:S(2)}, u32[]{:S(2)}) %collective-permute-start.4) | collective-permute-done | bytes 4656 | tf_op jit(solution)/shard_map/ppermute | solution.py:114
  131.8 0.6 collective-permute-done.3
  132.4 0.0 copy-start
  132.4 0.6 gather_fusion.1
  133.0 1.7 %fusion.66 = f32[8,512,17]{1,2,0:T(8,128)S(1)} fusion(f32[8,512]{1,0:T(8,128)S(1)} %get-tuple-element.34, f32[17]{0:T(128)S(1)} %iota_convert_fusion, f32[8,17,17]{2,1,0:T(8,128)S(1)} %gather_fusion.1, pred[8]{0:T(512)(128)(4,1)S(1)} %compare_and_fusion), kind=kOutput, calls=%fused_computation.62 | convolution fusion | flops 7174408 | bytes 304236 | tf_op jit(solution)/shard_map/ktp,ktu->kpu/dot_general | solution.py:142
  134.7 11.1 %subtract_subtract_fusion = f32[8,512,512]{2,1,0:T(8,128)} fusion(f32[8,512,512]{2,1,0:T(8,128)} %fusion, f32[8,512,512]{2,1,0:T(8,128)} %gather_fusion, pred[8]{0:T(512)(128)(4,1)S(1)} %compare_and_fusion.1, f32[8,512,17]{1,2,0:T(8,128)S(1)} %fusion.66, f32[8,512]{1,0:T(8,128)S(1)} %get-tuple-element.33, f32[17]{0:T(128)S(1)} %iota_convert_fusion), kind=kOutput, calls=%fused_computation.2 | convolution fusion | flops 220270592 | bytes 25460812 | tf_op jit(solution)/shard_map/kpu,kuq->kpq/dot_general | solution.py:143
  145.8 0.0 copy-done
  (15 shorter events, 0.2 us)
Async XLA Ops:
  7.2 86.4 %all-gather.2.cloned.1.call-start = ((), (), s32[]{:S(2)}) async-start(), calls=%async_computation | async-start | bytes 16908288 | tf_op jit(solution)/shard_map/all_gather | solution.py:127
  26.5 11.9 %copy-start.2 = (s32[8]{0:T(128)S(1)}, s32[8]{0:T(128)}, u32[]{:S(2)}) copy-start(s32[8]{0:T(128)} %param.11) | copy-start | bytes 100
  26.5 11.9 %copy-start.1 = (s32[8]{0:T(128)S(1)}, s32[8]{0:T(128)}, u32[]{:S(2)}) copy-start(s32[8]{0:T(128)} %patch_of.1) | copy-start | bytes 100
  109.7 14.3 %collective-permute-start.2 = (f32[4,17,17]{2,0,1:T(4,128)S(1)}, f32[4,17,17]{2,0,1:T(4,128)S(1)}, u32[]{:S(2)}, u32[]{:S(2)}) collective-permute-start(f32[4,17,17]{2,0,1:T(4,128)S(1)} %fusion.77), channel_id=1, source_target_pairs={{0,3},{1,0},{2,1},{3,2},{4,7},{5,4},{6,5},{7,6},{8,11},{9,8},{10,9... | collective-permute-start | bytes 13880 | tf_op jit(solution)/shard_map/ppermute | solution.py:114
  112.2 11.7 %collective-permute-start.1 = (f32[4,17,17]{2,0,1:T(4,128)S(1)}, f32[4,17,17]{2,0,1:T(4,128)S(1)}, u32[]{:S(2)}, u32[]{:S(2)}) collective-permute-start(f32[4,17,17]{2,0,1:T(4,128)S(1)} %fusion.77), channel_id=1, source_target_pairs={{0,2},{1,3},{2,0},{3,1},{4,6},{5,7},{6,4},{7,5},{8,10},{9,11},{10,... | collective-permute-start | bytes 13880 | tf_op jit(solution)/shard_map/ppermute | solution.py:114
  112.9 11.0 %collective-permute-start = (f32[4,17,17]{2,0,1:T(4,128)S(1)}, f32[4,17,17]{2,0,1:T(4,128)S(1)}, u32[]{:S(2)}, u32[]{:S(2)}) collective-permute-start(f32[4,17,17]{2,0,1:T(4,128)S(1)} %fusion.77), channel_id=1, source_target_pairs={{0,1},{1,2},{2,3},{3,0},{4,5},{5,6},{6,7},{7,4},{8,9},{9,10},{10,1... | collective-permute-start | bytes 13880 | tf_op jit(solution)/shard_map/ppermute | solution.py:114
  124.0 4.5 %collective-permute-start.5 = (f32[4,17,17]{2,0,1:T(4,128)S(1)}, f32[4,17,17]{2,0,1:T(4,128)S(1)}, u32[]{:S(2)}, u32[]{:S(2)}) collective-permute-start(f32[4,17,17]{2,0,1:T(4,128)S(1)} %fusion.194), channel_id=1, source_target_pairs={{0,12},{4,0},{8,4},{12,8},{1,13},{5,1},{9,5},{13,9},{2,14},{6,2},{... | collective-permute-start | bytes 13880 | tf_op jit(solution)/shard_map/ppermute | solution.py:114
  126.3 5.4 %collective-permute-start.4 = (f32[4,17,17]{2,0,1:T(4,128)S(1)}, f32[4,17,17]{2,0,1:T(4,128)S(1)}, u32[]{:S(2)}, u32[]{:S(2)}) collective-permute-start(f32[4,17,17]{2,0,1:T(4,128)S(1)} %fusion.194), channel_id=1, source_target_pairs={{0,8},{4,12},{8,0},{12,4},{1,9},{5,13},{9,1},{13,5},{2,10},{6,14},... | collective-permute-start | bytes 13880 | tf_op jit(solution)/shard_map/ppermute | solution.py:114
  127.2 5.1 %collective-permute-start.3 = (f32[4,17,17]{2,0,1:T(4,128)S(1)}, f32[4,17,17]{2,0,1:T(4,128)S(1)}, u32[]{:S(2)}, u32[]{:S(2)}) collective-permute-start(f32[4,17,17]{2,0,1:T(4,128)S(1)} %fusion.194), channel_id=1, source_target_pairs={{0,4},{4,8},{8,12},{12,0},{1,5},{5,9},{9,13},{13,1},{2,6},{6,10},{... | collective-permute-start | bytes 13880 | tf_op jit(solution)/shard_map/ppermute | solution.py:114
  132.4 13.4 %copy-start = (f32[4,17,17]{2,0,1:T(4,128)}, f32[4,17,17]{2,0,1:T(4,128)S(1)}, u32[]{:S(2)}) copy-start(f32[4,17,17]{2,0,1:T(4,128)S(1)} %multiply_bitcast_fusion) | copy-start | bytes 13876
Sparse Core Ops, SparseCore 0:
  11.1 82.4 all-gather.1

commit v10 on v8

--- a/solution.py
+++ b/solution.py
@@ -71,7 +71,15 @@
 
 
 def reference_terms_kernel(patch_of, ref_ref, row_ref, col_ref, out_ref):
-    middle = jnp.dot(row_ref[0], ref_ref[0], preferred_element_type=jnp.float32, precision=exact_mode)
+    rows = row_ref[0]
+    image = ref_ref[0]
+    rows_high = rows.astype(jnp.bfloat16)
+    rows_low = (rows - rows_high.astype(jnp.float32)).astype(jnp.bfloat16)
+    image_high = image.astype(jnp.bfloat16)
+    image_low = (image - image_high.astype(jnp.float32)).astype(jnp.bfloat16)
+    middle = jnp.dot(rows_high, image_high, preferred_element_type=jnp.float32)
+    middle = middle + jnp.dot(rows_low, image_high, preferred_element_type=jnp.float32)
+    middle = middle + jnp.dot(rows_high, image_low, preferred_element_type=jnp.float32)
     out_ref[0] = lax.dot_general(
         middle, col_ref[0], (((1,), (1,)), ((), ())), preferred_element_type=jnp.float32, precision=exact_mode
     )

time: 150 us -> 149 us (level)
  transfers between devices with their start and end apart: 7 -> 7, of which waited for: 3 -> 4; matrix products, arithmetic and copies ran while one was open for 31% -> 31% of each run, Pallas kernels for 0% -> 0%
where the time goes in v10:
time: 149 us
  waiting for transfers between devices  54.5 us (37%)
  matrix products  44.9 us (30%)
  local copies, waits for them, and re-layouts  14.5 us (10%)
  between operations  14.2 us (10%)
  Pallas kernels  9.48 us (6%)
  starting transfers between devices  7.94 us (5%)
  other arithmetic  3.1 us (2%)
    all_gather x1, waiting for transfers between devices, body(): lax.all_gather(ref_patch, PATCH_PARTS + VISIT_PARTS, axis=0, tiled=True)  49.5 us
    dot_general x1, matrix products, warp_batch(): return jnp.einsum('kib,kjb->kij', middle, right_matrix, precision=warp_mode)  11.9 us
    dot_general x1, matrix products, warp_batch(): jnp.einsum('kia,kab->kib', left_matrix, slab_images, precision=warp_mode)  11.8 us
    dot_general x1, matrix products, body(): fitted = jnp.einsum('kpu,kuq->kpq', middle, col_basis, precision=warp_mode)  11.1 us
    gather x1, local copies, waits for them, and re-layouts, body(): own_diffs = warped_all - jnp.take(ref_block, piece_patch, axis=0)  10.1 us
    pallas_call x1, Pallas kernels, reference_terms(): pl.pallas_call(reference_terms_kernel, out_shape=jax.ShapeDtypeStruct((pi...  9.48 us
    ppermute x6, starting transfers between devices, ring_sum(): received.append(lax.ppermute(value, axis_name, pairs))  7.9 us
    dot_general x1, matrix products, project_terms(): jnp.einsum('mtp,mpq->mtq', row_basis, differences, precision=warp_mode)  5.59 us
  transfers between devices with their start and end apart: 7, of which 4 were waited for; matrix products, arithmetic and copies ran while one was open for 31% of the time, Pallas kernels for 0%

profile of v10, /device:TPU:0, one launch (start us, length us, event | category | flops | bytes accessed | tf_op | source)
XLA Modules:
  0.0 148.7 jit_solution(10899412566257692782)
XLA Ops:
  7.2 0.0 all-gather.2.cloned.1.call-start
  7.2 0.7 all-gather.2.cloned.1.call-update
  7.9 0.8 slice_bitcast_fusion
  8.7 0.2 sqrt_atan2_fusion
  8.9 2.6 %multiply_cosine_fusion = (f32[8,17,512]{2,1,0:T(8,128)S(1)}, f32[8,17,512]{2,1,0:T(8,128)S(1)}) fusion(f32[8,512]{1,0:T(8,128)S(1)} %get-tuple-element.33, f32[17]{0:T(128)S(1)} %iota_convert_fusion, f32[8,512]{1,0:T(8,128)S(1)} %get-tuple-element.34), kind=kLoop, calls=%fused_computation.60 | loop fusion | flops 139264 | bytes 589892 | tf_op jit(solution)/shard_map/vmap()/cos | solution.py:52
  11.4 0.8 pad.8.col_ref
  12.2 0.8 pad.7.row_ref
  13.0 0.8 slice_bitcast_fusion.9
  13.7 0.8 slice_bitcast_fusion.8
  14.5 0.1 fusion.116
  14.6 0.1 iota_add_fusion
  14.7 11.8 %fusion.13 = f32[8,512,512]{2,1,0:T(8,128)S(1)} fusion(f32[8,512,512]{2,1,0:T(8,128)} %param.8, f32[8]{0:T(128)S(1)} %get-tuple-element.29, f32[8]{0:T(128)S(1)} %get-tuple-element.28, f32[8]{0:T(128)S(1)} %get-tuple-element.27, f32[8]{0:T(128)S(1)} %get-tuple-element.26, f32[8]{0:T(128)S(1)} %get-tuple-element.25, f32[8]{0:T(128)S(1)} %get-tuple-element.30, ...), kind=kOutput, calls=%fused_computation.17 | convolution fusion | flops 6469713920 | bytes 16793792 | tf_op jit(solution)/shard_map/kia,kab->kib/dot_general | solution.py:43
  26.5 0.0 copy-start.2
  26.5 0.0 copy-start.1
  26.5 11.9 %fusion = f32[8,512,512]{2,1,0:T(8,128)} fusion(f32[8,512,512]{2,1,0:T(8,128)S(1)} %fusion.13, f32[8]{0:T(128)S(1)} %get-tuple-element.4, f32[8]{0:T(128)S(1)} %get-tuple-element.5, f32[8]{0:T(128)S(1)} %get-tuple-element.6, f32[8]{0:T(128)S(1)} %get-tuple-element.7, f32[8]{0:T(128)S(1)} %get-tuple-element.8, f32[8]{0:T(128)S(1)} %get-tuple-element.3, ...), kind=kOutput, calls=%fused_computation.3 | convolution fusion | flops 6469713920 | bytes 16793792 | tf_op jit(solution)/shard_map/kib,kjb->kij/dot_general | solution.py:45
  38.4 0.0 copy-done.2
  38.4 0.0 copy-done.1
  38.5 5.6 %fusion.67 = f32[8,17,512]{2,1,0:T(8,128)S(1)} fusion(f32[8,512,512]{2,1,0:T(8,128)} %fusion, f32[8,512]{1,0:T(8,128)S(1)} %get-tuple-element.34, f32[17]{0:T(128)S(1)} %iota_convert_fusion), kind=kOutput, calls=%fused_computation.63 | convolution fusion | flops 213979136 | bytes 8683588 | tf_op jit(solution)/shard_map/mtp,mpq->mtq/dot_general | solution.py:66
  44.1 49.5 %all-gather.2.cloned.1.call-done = f32[128,64,512]{2,1,0:T(8,128)} async-done(((f32[1,64,512]{2,1,0:T(8,128)}), f32[128,64,512]{2,1,0:T(8,128)}) %all-gather.2.cloned.1.call-update) | async-done | bytes 16777232 | tf_op jit(solution)/shard_map/all_gather | solution.py:135
  93.6 9.5 %shard_map.86 = f32[8,24,24]{2,1,0:T(8,128)} custom-call(s32[8]{0:T(128)} %patch_of.1, f32[16,512,512]{2,1,0:T(8,128)} %bitcast.56, f32[8,24,512]{2,1,0:T(8,128)} %pad.7.row_ref, f32[8,24,512]{2,1,0:T(8,128)} %pad.8.col_ref), custom_call_target="tpu_custom_call" | custom-call | flops 105381888 | bytes 9175040 | tf_op jit(solution)/shard_map/pallas_call | solution.py:94
  103.1 2.7 %convolution_subtract_fusion = f32[8,17,17]{2,1,0:T(8,128)S(1)} fusion(f32[8,17,512]{2,1,0:T(8,128)S(1)} %fusion.67, f32[8,512]{1,0:T(8,128)S(1)} %get-tuple-element.33, f32[17]{0:T(128)S(1)} %iota_convert_fusion, f32[8,24,24]{2,1,0:T(8,128)} %shard_map.86), kind=kOutput, calls=%fused_computation.59 | convolution fusion | flops 14276872 | bytes 313476 | tf_op jit(solution)/shard_map/mtq,muq->mtu/dot_general | solution.py:67
  105.8 0.2 fusion.77
  106.0 2.5 %collective-permute-start.2 = (f32[4,17,17]{2,0,1:T(4,128)S(1)}, f32[4,17,17]{2,0,1:T(4,128)S(1)}, u32[]{:S(2)}, u32[]{:S(2)}) collective-permute-start(f32[4,17,17]{2,0,1:T(4,128)S(1)} %fusion.77), channel_id=1, source_target_pairs={{0,3},{1,0},{2,1},{3,2},{4,7},{5,4},{6,5},{7,6},{8,11},{9,8},{10,9... | collective-permute-start | bytes 13880 | tf_op jit(solution)/shard_map/ppermute | solution.py:122
  108.5 0.6 collective-permute-start.1
  109.0 1.1 collective-permute-start
  110.2 10.1 %gather_fusion = f32[8,512,512]{2,1,0:T(8,128)} fusion(f32[16,512,512]{2,1,0:T(8,128)} %bitcast.57, s32[1024]{0:T(1024)S(1)} %pad_clamp_fusion.1), kind=kCustom, calls=%fused_computation | custom fusion | bytes 16777248 | tf_op jit(solution)/shard_map/jit(_take)/gather | solution.py:141
  120.2 0.0 collective-permute-done.2
  120.3 0.0 collective-permute-done.1
  120.3 0.0 collective-permute-done
  120.3 2.0 %collective-permute-start.5 = (f32[4,17,17]{2,0,1:T(4,128)S(1)}, f32[4,17,17]{2,0,1:T(4,128)S(1)}, u32[]{:S(2)}, u32[]{:S(2)}) collective-permute-start(f32[4,17,17]{2,0,1:T(4,128)S(1)} %fusion.194), channel_id=1, source_target_pairs={{0,12},{4,0},{8,4},{12,8},{1,13},{5,1},{9,5},{13,9},{2,14},{6,2},{... | collective-permute-start | bytes 13880 | tf_op jit(solution)/shard_map/ppermute | solution.py:122
  122.4 0.9 collective-permute-start.4
  123.3 0.8 collective-permute-start.3
  124.1 0.5 collective-permute-done.5
  124.6 3.2 %collective-permute-done.4 = f32[4,17,17]{2,0,1:T(4,128)S(1)} collective-permute-done((f32[4,17,17]{2,0,1:T(4,128)S(1)}, f32[4,17,17]{2,0,1:T(4,128)S(1)}, u32[]{:S(2)}, u32[]{:S(2)}) %collective-permute-start.4) | collective-permute-done | bytes 4656 | tf_op jit(solution)/shard_map/ppermute | solution.py:122
  127.8 0.6 collective-permute-done.3
  128.5 0.0 copy-start
  128.5 0.6 gather_fusion.1
  129.1 1.7 %fusion.66 = f32[8,512,17]{1,2,0:T(8,128)S(1)} fusion(f32[8,512]{1,0:T(8,128)S(1)} %get-tuple-element.34, f32[17]{0:T(128)S(1)} %iota_convert_fusion, f32[8,17,17]{2,1,0:T(8,128)S(1)} %gather_fusion.1, pred[8]{0:T(512)(128)(4,1)S(1)} %compare_and_fusion), kind=kOutput, calls=%fused_computation.62 | convolution fusion | flops 7174408 | bytes 304236 | tf_op jit(solution)/shard_map/ktp,ktu->kpu/dot_general | solution.py:150
  130.8 11.1 %subtract_subtract_fusion = f32[8,512,512]{2,1,0:T(8,128)} fusion(f32[8,512,512]{2,1,0:T(8,128)} %fusion, f32[8,512,512]{2,1,0:T(8,128)} %gather_fusion, pred[8]{0:T(512)(128)(4,1)S(1)} %compare_and_fusion.1, f32[8,512,17]{1,2,0:T(8,128)S(1)} %fusion.66, f32[8,512]{1,0:T(8,128)S(1)} %get-tuple-element.33, f32[17]{0:T(128)S(1)} %iota_convert_fusion), kind=kOutput, calls=%fused_computation.2 | convolution fusion | flops 220270592 | bytes 25460812 | tf_op jit(solution)/shard_map/kpu,kuq->kpq/dot_general | solution.py:151
  141.9 0.0 copy-done
  (15 shorter events, 0.2 us)
Async XLA Ops:
  7.2 86.4 %all-gather.2.cloned.1.call-start = ((), (), s32[]{:S(2)}) async-start(), calls=%async_computation | async-start | bytes 16908288 | tf_op jit(solution)/shard_map/all_gather | solution.py:135
  26.5 11.9 %copy-start.2 = (s32[8]{0:T(128)S(1)}, s32[8]{0:T(128)}, u32[]{:S(2)}) copy-start(s32[8]{0:T(128)} %param.11) | copy-start | bytes 100
  26.5 11.9 %copy-start.1 = (s32[8]{0:T(128)S(1)}, s32[8]{0:T(128)}, u32[]{:S(2)}) copy-start(s32[8]{0:T(128)} %patch_of.1) | copy-start | bytes 100
  106.0 14.3 %collective-permute-start.2 = (f32[4,17,17]{2,0,1:T(4,128)S(1)}, f32[4,17,17]{2,0,1:T(4,128)S(1)}, u32[]{:S(2)}, u32[]{:S(2)}) collective-permute-start(f32[4,17,17]{2,0,1:T(4,128)S(1)} %fusion.77), channel_id=1, source_target_pairs={{0,3},{1,0},{2,1},{3,2},{4,7},{5,4},{6,5},{7,6},{8,11},{9,8},{10,9... | collective-permute-start | bytes 13880 | tf_op jit(solution)/shard_map/ppermute | solution.py:122
  108.5 11.8 %collective-permute-start.1 = (f32[4,17,17]{2,0,1:T(4,128)S(1)}, f32[4,17,17]{2,0,1:T(4,128)S(1)}, u32[]{:S(2)}, u32[]{:S(2)}) collective-permute-start(f32[4,17,17]{2,0,1:T(4,128)S(1)} %fusion.77), channel_id=1, source_target_pairs={{0,2},{1,3},{2,0},{3,1},{4,6},{5,7},{6,4},{7,5},{8,10},{9,11},{10,... | collective-permute-start | bytes 13880 | tf_op jit(solution)/shard_map/ppermute | solution.py:122
  109.0 11.2 %collective-permute-start = (f32[4,17,17]{2,0,1:T(4,128)S(1)}, f32[4,17,17]{2,0,1:T(4,128)S(1)}, u32[]{:S(2)}, u32[]{:S(2)}) collective-permute-start(f32[4,17,17]{2,0,1:T(4,128)S(1)} %fusion.77), channel_id=1, source_target_pairs={{0,1},{1,2},{2,3},{3,0},{4,5},{5,6},{6,7},{7,4},{8,9},{9,10},{10,1... | collective-permute-start | bytes 13880 | tf_op jit(solution)/shard_map/ppermute | solution.py:122
  120.3 4.2 %collective-permute-start.5 = (f32[4,17,17]{2,0,1:T(4,128)S(1)}, f32[4,17,17]{2,0,1:T(4,128)S(1)}, u32[]{:S(2)}, u32[]{:S(2)}) collective-permute-start(f32[4,17,17]{2,0,1:T(4,128)S(1)} %fusion.194), channel_id=1, source_target_pairs={{0,12},{4,0},{8,4},{12,8},{1,13},{5,1},{9,5},{13,9},{2,14},{6,2},{... | collective-permute-start | bytes 13880 | tf_op jit(solution)/shard_map/ppermute | solution.py:122
  122.4 5.4 %collective-permute-start.4 = (f32[4,17,17]{2,0,1:T(4,128)S(1)}, f32[4,17,17]{2,0,1:T(4,128)S(1)}, u32[]{:S(2)}, u32[]{:S(2)}) collective-permute-start(f32[4,17,17]{2,0,1:T(4,128)S(1)} %fusion.194), channel_id=1, source_target_pairs={{0,8},{4,12},{8,0},{12,4},{1,9},{5,13},{9,1},{13,5},{2,10},{6,14},... | collective-permute-start | bytes 13880 | tf_op jit(solution)/shard_map/ppermute | solution.py:122
  123.3 5.1 %collective-permute-start.3 = (f32[4,17,17]{2,0,1:T(4,128)S(1)}, f32[4,17,17]{2,0,1:T(4,128)S(1)}, u32[]{:S(2)}, u32[]{:S(2)}) collective-permute-start(f32[4,17,17]{2,0,1:T(4,128)S(1)} %fusion.194), channel_id=1, source_target_pairs={{0,4},{4,8},{8,12},{12,0},{1,5},{5,9},{9,13},{13,1},{2,6},{6,10},{... | collective-permute-start | bytes 13880 | tf_op jit(solution)/shard_map/ppermute | solution.py:122
  128.5 13.4 %copy-start = (f32[4,17,17]{2,0,1:T(4,128)}, f32[4,17,17]{2,0,1:T(4,128)S(1)}, u32[]{:S(2)}) copy-start(f32[4,17,17]{2,0,1:T(4,128)S(1)} %multiply_bitcast_fusion) | copy-start | bytes 13876
Sparse Core Ops, SparseCore 0:
  11.1 82.4 all-gather.1

commit v11 on v10

--- a/solution.py
+++ b/solution.py
@@ -113,6 +113,42 @@
     return out[:, :terms, :terms]
 
 
+def matched_kernel(patch_of, warped_ref, ref_ref, rows_ref, coef_ref, col_ref, out_ref):
+    middle = jnp.dot(rows_ref[0], coef_ref[0], preferred_element_type=jnp.float32, precision=exact_mode)
+    fitted = jnp.dot(middle, col_ref[0], preferred_element_type=jnp.float32, precision=exact_mode)
+    out_ref[0] = (warped_ref[0] - ref_ref[0]) - fitted
+
+
+def matched_pieces(warped_all, ref_block, piece_patch, row_basis, chosen, col_basis):
+    piece_count, terms, side_len = row_basis.shape
+    extra = BASIS_ROWS - terms
+    rows = jnp.pad(jnp.transpose(row_basis, (0, 2, 1)), ((0, 0), (0, 0), (0, extra)))
+    coefs = jnp.pad(chosen, ((0, 0), (0, extra), (0, extra)))
+    cols = jnp.pad(col_basis, ((0, 0), (0, extra), (0, 0)))
+    image_spec = pl.BlockSpec((1, side_len, side_len), lambda k, patch_of: (k, 0, 0))
+    return pl.pallas_call(
+        matched_kernel,
+        out_shape=jax.ShapeDtypeStruct(warped_all.shape, jnp.float32),
+        grid_spec=pltpu.PrefetchScalarGridSpec(
+            num_scalar_prefetch=1,
+            grid=(piece_count,),
+            in_specs=[
+                image_spec,
+                pl.BlockSpec((1, side_len, side_len), lambda k, patch_of: (patch_of[k], 0, 0)),
+                pl.BlockSpec((1, side_len, BASIS_ROWS), lambda k, patch_of: (k, 0, 0)),
+                pl.BlockSpec((1, BASIS_ROWS, BASIS_ROWS), lambda k, patch_of: (k, 0, 0)),
+                pl.BlockSpec((1, BASIS_ROWS, side_len), lambda k, patch_of: (k, 0, 0)),
+            ],
+            out_specs=image_spec,
+        ),
+        cost_estimate=pl.CostEstimate(
+            flops=2 * piece_count * side_len * BASIS_ROWS * (side_len + BASIS_ROWS),
+            bytes_accessed=12 * piece_count * side_len * side_len,
+            transcendentals=0,
+        ),
+    )(piece_patch, warped_all, ref_block, rows, coefs, cols)
+
+
 def ring_sum(value, axis_name):
     count = lax.axis_size(axis_name)
     me = lax.axis_index(axis_name)
@@ -138,7 +174,6 @@
     own_onehot = (piece_visit[:, None] == visit_slots[None, :]).astype(jnp.float32)
     warped_all = warp_batch(pieces, shifts[:, 0], shifts[:, 1], phases[:, 0], phases[:, 1])
     warped_all = lax.optimization_barrier(warped_all)
-    own_diffs = warped_all - jnp.take(ref_block, piece_patch, axis=0)
     row_basis, col_basis = basis_pair(anchors, side_len)
     warp_terms = project_terms(warped_all, row_basis, col_basis)
     ref_terms = reference_terms(ref_block, piece_patch, row_basis, col_basis)
@@ -147,9 +182,8 @@
     totals = ring_sum(ring_sum(local_sums, "pz"), "px")
     coefficients = totals / float(patch_count * (piece_count // VIS_DEV) * side_len * side_len)
     chosen = jnp.take(coefficients, piece_visit, axis=0)
-    middle = jnp.einsum("ktp,ktu->kpu", row_basis, chosen, precision=warp_mode)
-    fitted = jnp.einsum("kpu,kuq->kpq", middle, col_basis, precision=warp_mode)
-    return (own_diffs - fitted, coefficients)
+    matched = matched_pieces(warped_all, ref_block, piece_patch, row_basis, chosen, col_basis)
+    return (matched, coefficients)
 
 
 def solution(mesh):

time: 149 us -> 147 us (0.987)
  Pallas kernels: 9.48 us -> 26.5 us
  matrix products: 44.9 us -> 29.3 us
  local copies, waits for them, and re-layouts: 14.5 us -> 5.84 us
  other arithmetic: 3.1 us -> 9.85 us
  waiting for transfers between devices: 54.5 us -> 50.6 us
  starting transfers between devices: 7.94 us -> 10.3 us
    pallas_call x0 -> x1, Pallas kernels: none -> 17.1 us  [matched_pieces(): pl.pallas_call(matched_kernel, out_shape=jax.ShapeDtypeStruct(warped_all....]
    dot_general x2 -> x0, matrix products: 12.8 us -> none  [the longest x1 11.1 us: body(): fitted = jnp.einsum('kpu,kuq->kpq', middle, col_basis, precision=warp_mode)]
    gather x1 -> x0, local copies, waits for them, and re-layouts: 10.1 us -> none  [body(): own_diffs = warped_all - jnp.take(ref_block, piece_patch, axis=0)]
    cos x1 -> x2, other arithmetic: 2.56 us -> 9.25 us  [chebyshev_rows(): return jnp.cos(orders[:, None] * jnp.arccos(coordinate)[None, :])]
    all_gather x1, waiting for transfers between devices: 49.5 us -> 46.5 us  [body(): lax.all_gather(ref_patch, PATCH_PARTS + VISIT_PARTS, axis=0, tiled=True)]
    ppermute x6, starting transfers between devices: 7.9 us -> 10.3 us  [ring_sum(): received.append(lax.ppermute(value, axis_name, pairs))]
    pad x0 -> x2, local copies, waits for them, and re-layouts: none -> 2.17 us  [the longest x1 1.52 us: matched_pieces(): jnp.pad(jnp.transpose(row_basis, (0, 2, 1)), ((0, 0), (0, 0), (0, extra)))]
    dot_general x1, matrix products: 5.59 us -> 3.92 us  [project_terms(): jnp.einsum('mtp,mpq->mtq', row_basis, differences, precision=warp_mode)]
  transfers between devices with their start and end apart: 7 -> 7, of which waited for: 4 -> 5; matrix products, arithmetic and copies ran while one was open for 31% -> 28% of each run, Pallas kernels for 0% -> 0%
where the time goes in v11:
time: 147 us
  waiting for transfers between devices  50.6 us (34%)
  matrix products  29.3 us (20%)
  Pallas kernels  26.5 us (18%)
  between operations  14.2 us (10%)
  starting transfers between devices  10.3 us (7%)
  other arithmetic  9.85 us (7%)
  local copies, waits for them, and re-layouts  5.84 us (4%)
    all_gather x1, waiting for transfers between devices, body(): lax.all_gather(ref_patch, PATCH_PARTS + VISIT_PARTS, axis=0, tiled=True)  46.5 us
    pallas_call x1, Pallas kernels, matched_pieces(): pl.pallas_call(matched_kernel, out_shape=jax.ShapeDtypeStruct(warped_all....  17.1 us
    dot_general x1, matrix products, warp_batch(): jnp.einsum('kia,kab->kib', left_matrix, slab_images, precision=warp_mode)  11.6 us
    dot_general x1, matrix products, warp_batch(): return jnp.einsum('kib,kjb->kij', middle, right_matrix, precision=warp_mode)  10.8 us
    ppermute x6, starting transfers between devices, ring_sum(): received.append(lax.ppermute(value, axis_name, pairs))  10.3 us
    pallas_call x1, Pallas kernels, reference_terms(): pl.pallas_call(reference_terms_kernel, out_shape=jax.ShapeDtypeStruct((pi...  9.49 us
    cos x2, other arithmetic, chebyshev_rows(): return jnp.cos(orders[:, None] * jnp.arccos(coordinate)[None, :])  9.25 us
    dot_general x1, matrix products, project_terms(): jnp.einsum('mtp,mpq->mtq', row_basis, differences, precision=warp_mode)  3.92 us
  transfers between devices with their start and end apart: 7, of which 5 were waited for; matrix products, arithmetic and copies ran while one was open for 28% of the time, Pallas kernels for 0%

profile of v11, /device:TPU:0, one launch (start us, length us, event | category | flops | bytes accessed | tf_op | source)
XLA Modules:
  0.0 146.7 jit_solution(4818541337602119881)
XLA Ops:
  7.2 0.0 all-gather.2.cloned.1.call-start
  7.2 0.7 all-gather.2.cloned.1.call-update
  8.0 0.8 slice_bitcast_fusion.8
  8.7 0.8 slice_bitcast_fusion.9
  9.5 0.1 fusion.104
  9.6 0.1 iota_add_fusion
  9.7 11.6 %fusion.13 = f32[8,512,512]{2,1,0:T(8,128)S(1)} fusion(f32[8,512,512]{2,1,0:T(8,128)} %param.8, f32[8]{0:T(128)S(1)} %get-tuple-element.29, f32[8]{0:T(128)S(1)} %get-tuple-element.28, f32[8]{0:T(128)S(1)} %get-tuple-element.27, f32[8]{0:T(128)S(1)} %get-tuple-element.26, f32[8]{0:T(128)S(1)} %get-tuple-element.25, f32[8]{0:T(128)S(1)} %get-tuple-element.30, ...), kind=kOutput, calls=%fused_computation.15 | convolution fusion | flops 6469713920 | bytes 16793792 | tf_op jit(solution)/shard_map/kia,kab->kib/dot_general | solution.py:43
  21.3 0.0 copy-start.2
  21.3 0.0 copy-start.3
  21.3 10.8 %fusion.warped_ref = f32[8,512,512]{2,1,0:T(8,128)S(1)} fusion(f32[8,512,512]{2,1,0:T(8,128)S(1)} %fusion.13, f32[8]{0:T(128)S(1)} %get-tuple-element.4, f32[8]{0:T(128)S(1)} %get-tuple-element.5, f32[8]{0:T(128)S(1)} %get-tuple-element.6, f32[8]{0:T(128)S(1)} %get-tuple-element.7, f32[8]{0:T(128)S(1)} %get-tuple-element.8, f32[8]{0:T(128)S(1)} %get-tuple-element.3, ...), kind=kOutput, calls=%fused_computation.1 | convolution fusion | flops 6469713920 | bytes 16793792 | tf_op jit(solution)/shard_map/kib,kjb->kij/dot_general | solution.py:45
  32.2 0.0 copy-start
  32.2 0.0 copy-done.2
  32.2 0.2 sqrt_atan2_fusion
  32.4 2.6 %multiply_cosine_fusion.1 = (f32[8,17,512]{2,1,0:T(8,128)S(1)}, f32[8,17,512]{2,1,0:T(8,128)S(1)}) fusion(f32[8,512]{1,0:T(8,128)S(1)} %get-tuple-element.33, f32[17]{0:T(128)S(1)} %iota_convert_fusion, f32[8,512]{1,0:T(8,128)S(1)} %get-tuple-element.34), kind=kLoop, calls=%fused_computation.59 | loop fusion | flops 139264 | bytes 589892 | tf_op jit(solution)/shard_map/vmap()/cos | solution.py:52
  34.9 0.8 pad.18.col_ref
  35.7 0.8 pad.17.row_ref
  36.5 0.0 copy-done.3
  36.5 6.7 %multiply_cosine_fusion = f32[8,512,17]{2,1,0:T(8,128)S(1)} fusion(f32[8,512]{1,0:T(8,128)S(1)} %get-tuple-element.34, f32[17]{0:T(128)S(1)} %iota_convert_fusion), kind=kLoop, calls=%fused_computation.57 | loop fusion | flops 69632 | bytes 294980 | tf_op jit(solution)/shard_map/vmap()/cos | solution.py:52
  43.2 0.0 copy-done
  43.2 3.9 %fusion.66 = f32[8,17,512]{2,1,0:T(8,128)S(1)} fusion(f32[8,512,512]{2,1,0:T(8,128)S(1)} %fusion.warped_ref, f32[8,512]{1,0:T(8,128)S(1)} %get-tuple-element.34, f32[17]{0:T(128)S(1)} %iota_convert_fusion), kind=kOutput, calls=%fused_computation.63 | convolution fusion | flops 213979136 | bytes 8683588 | tf_op jit(solution)/shard_map/mtp,mpq->mtq/dot_general | solution.py:66
  47.2 46.5 %all-gather.2.cloned.1.call-done = f32[128,64,512]{2,1,0:T(8,128)} async-done(((f32[1,64,512]{2,1,0:T(8,128)}), f32[128,64,512]{2,1,0:T(8,128)}) %all-gather.2.cloned.1.call-update) | async-done | bytes 16777232 | tf_op jit(solution)/shard_map/all_gather | solution.py:171
  93.6 9.5 %shard_map.86 = f32[8,24,24]{2,1,0:T(8,128)} custom-call(s32[8]{0:T(128)} %patch_of.3, f32[16,512,512]{2,1,0:T(8,128)} %bitcast.55, f32[8,24,512]{2,1,0:T(8,128)} %pad.17.row_ref, f32[8,24,512]{2,1,0:T(8,128)} %pad.18.col_ref), custom_call_target="tpu_custom_call" | custom-call | flops 105381888 | bytes 9175040 | tf_op jit(solution)/shard_map/pallas_call | solution.py:94
  103.1 2.7 %convolution_subtract_fusion = f32[8,17,17]{2,1,0:T(8,128)S(1)} fusion(f32[8,17,512]{2,1,0:T(8,128)S(1)} %fusion.66, f32[8,512]{1,0:T(8,128)S(1)} %get-tuple-element.33, f32[17]{0:T(128)S(1)} %iota_convert_fusion, f32[8,24,24]{2,1,0:T(8,128)} %shard_map.86), kind=kOutput, calls=%fused_computation.58 | convolution fusion | flops 14276872 | bytes 313476 | tf_op jit(solution)/shard_map/mtq,muq->mtu/dot_general | solution.py:67
  105.8 0.2 fusion.67
  106.0 1.1 collective-permute-start
  107.1 2.9 %collective-permute-start.1 = (f32[4,17,17]{2,0,1:T(4,128)S(1)}, f32[4,17,17]{2,0,1:T(4,128)S(1)}, u32[]{:S(2)}, u32[]{:S(2)}) collective-permute-start(f32[4,17,17]{2,0,1:T(4,128)S(1)} %fusion.67), channel_id=1, source_target_pairs={{0,2},{1,3},{2,0},{3,1},{4,6},{5,7},{6,4},{7,5},{8,10},{9,11},{10,... | collective-permute-start | bytes 13880 | tf_op jit(solution)/shard_map/ppermute | solution.py:158
  110.0 1.3 collective-permute-start.2
  111.3 1.5 %pad.16.rows_ref = f32[8,512,24]{2,1,0:T(8,128)} pad(f32[8,512,17]{2,1,0:T(8,128)S(1)} %multiply_cosine_fusion, f32[]{:T(128)} %constant.137.clone.1), padding=0_0x0_0x0_7 | pad | bytes 671748 | tf_op jit(solution)/shard_map/jit(_pad)/pad | solution.py:125
  112.8 0.0 collective-permute-done
  112.8 0.0 collective-permute-done.1
  112.8 1.1 collective-permute-done.2
  114.0 0.8 collective-permute-start.3
  114.8 2.6 %collective-permute-start.4 = (f32[4,17,17]{2,0,1:T(4,128)S(1)}, f32[4,17,17]{2,0,1:T(4,128)S(1)}, u32[]{:S(2)}, u32[]{:S(2)}) collective-permute-start(f32[4,17,17]{2,0,1:T(4,128)S(1)} %fusion.180), channel_id=1, source_target_pairs={{0,8},{4,12},{8,0},{12,4},{1,9},{5,13},{9,1},{13,5},{2,10},{6,14},... | collective-permute-start | bytes 13880 | tf_op jit(solution)/shard_map/ppermute | solution.py:158
  117.5 1.5 %collective-permute-start.5 = (f32[4,17,17]{2,0,1:T(4,128)S(1)}, f32[4,17,17]{2,0,1:T(4,128)S(1)}, u32[]{:S(2)}, u32[]{:S(2)}) collective-permute-start(f32[4,17,17]{2,0,1:T(4,128)S(1)} %fusion.180), channel_id=1, source_target_pairs={{0,12},{4,0},{8,4},{12,8},{1,13},{5,1},{9,5},{13,9},{2,14},{6,2},{... | collective-permute-start | bytes 13880 | tf_op jit(solution)/shard_map/ppermute | solution.py:158
  119.0 0.2 collective-permute-done.3
  119.2 1.0 collective-permute-done.4
  120.3 1.1 collective-permute-done.5
  121.5 0.0 copy-start.1
  121.5 0.6 gather_fusion
  122.1 0.1 broadcast_select_fusion
  122.2 0.6 pad.19.coef_ref
  122.8 17.1 %shard_map.87 = f32[8,512,512]{2,1,0:T(8,128)} custom-call(s32[8]{0:T(128)} %patch_of.3, f32[8,512,512]{2,1,0:T(8,128)} %copy-done, f32[16,512,512]{2,1,0:T(8,128)} %bitcast.56, f32[8,512,24]{2,1,0:T(8,128)} %pad.16.rows_ref, f32[8,24,24]{2,1,0:T(8,128)} %pad.19.coef_ref, f32[8,24,512]{2,1,0:T(8,128)} %pad.18.col_ref), custom_call_target="tpu_custom_call" | custom-call | flops 105381888 | bytes 25165824 | tf_op jit(solution)/shard_map/pallas_call | solution.py:129
  139.9 0.0 copy-done.1
  (13 shorter events, 0.2 us)
Async XLA Ops:
  7.2 86.4 %all-gather.2.cloned.1.call-start = ((), (), s32[]{:S(2)}) async-start(), calls=%async_computation | async-start | bytes 16908288 | tf_op jit(solution)/shard_map/all_gather | solution.py:171
  21.3 10.9 %copy-start.2 = (s32[8,2]{0,1:T(2,128)S(1)}, s32[8,2]{0,1:T(2,128)}, u32[]{:S(2)}) copy-start(s32[8,2]{0,1:T(2,128)} %param.12) | copy-start | bytes 196
  21.3 15.2 %copy-start.3 = (s32[8]{0:T(128)S(1)}, s32[8]{0:T(128)}, u32[]{:S(2)}) copy-start(s32[8]{0:T(128)} %param.11) | copy-start | bytes 100
  32.2 11.1 %copy-start = (f32[8,512,512]{2,1,0:T(8,128)}, f32[8,512,512]{2,1,0:T(8,128)S(1)}, u32[]{:S(2)}) copy-start(f32[8,512,512]{2,1,0:T(8,128)S(1)} %fusion.warped_ref) | copy-start | bytes 25165828
  106.0 6.8 %collective-permute-start = (f32[4,17,17]{2,0,1:T(4,128)S(1)}, f32[4,17,17]{2,0,1:T(4,128)S(1)}, u32[]{:S(2)}, u32[]{:S(2)}) collective-permute-start(f32[4,17,17]{2,0,1:T(4,128)S(1)} %fusion.67), channel_id=1, source_target_pairs={{0,1},{1,2},{2,3},{3,0},{4,5},{5,6},{6,7},{7,4},{8,9},{9,10},{10,1... | collective-permute-start | bytes 13880 | tf_op jit(solution)/shard_map/ppermute | solution.py:158
  107.1 5.8 %collective-permute-start.1 = (f32[4,17,17]{2,0,1:T(4,128)S(1)}, f32[4,17,17]{2,0,1:T(4,128)S(1)}, u32[]{:S(2)}, u32[]{:S(2)}) collective-permute-start(f32[4,17,17]{2,0,1:T(4,128)S(1)} %fusion.67), channel_id=1, source_target_pairs={{0,2},{1,3},{2,0},{3,1},{4,6},{5,7},{6,4},{7,5},{8,10},{9,11},{10,... | collective-permute-start | bytes 13880 | tf_op jit(solution)/shard_map/ppermute | solution.py:158
  110.0 3.9 %collective-permute-start.2 = (f32[4,17,17]{2,0,1:T(4,128)S(1)}, f32[4,17,17]{2,0,1:T(4,128)S(1)}, u32[]{:S(2)}, u32[]{:S(2)}) collective-permute-start(f32[4,17,17]{2,0,1:T(4,128)S(1)} %fusion.67), channel_id=1, source_target_pairs={{0,3},{1,0},{2,1},{3,2},{4,7},{5,4},{6,5},{7,6},{8,11},{9,8},{10,9... | collective-permute-start | bytes 13880 | tf_op jit(solution)/shard_map/ppermute | solution.py:158
  114.0 5.2 %collective-permute-start.3 = (f32[4,17,17]{2,0,1:T(4,128)S(1)}, f32[4,17,17]{2,0,1:T(4,128)S(1)}, u32[]{:S(2)}, u32[]{:S(2)}) collective-permute-start(f32[4,17,17]{2,0,1:T(4,128)S(1)} %fusion.180), channel_id=1, source_target_pairs={{0,4},{4,8},{8,12},{12,0},{1,5},{5,9},{9,13},{13,1},{2,6},{6,10},{... | collective-permute-start | bytes 13880 | tf_op jit(solution)/shard_map/ppermute | solution.py:158
  114.8 5.4 %collective-permute-start.4 = (f32[4,17,17]{2,0,1:T(4,128)S(1)}, f32[4,17,17]{2,0,1:T(4,128)S(1)}, u32[]{:S(2)}, u32[]{:S(2)}) collective-permute-start(f32[4,17,17]{2,0,1:T(4,128)S(1)} %fusion.180), channel_id=1, source_target_pairs={{0,8},{4,12},{8,0},{12,4},{1,9},{5,13},{9,1},{13,5},{2,10},{6,14},... | collective-permute-start | bytes 13880 | tf_op jit(solution)/shard_map/ppermute | solution.py:158
  117.5 3.9 %collective-permute-start.5 = (f32[4,17,17]{2,0,1:T(4,128)S(1)}, f32[4,17,17]{2,0,1:T(4,128)S(1)}, u32[]{:S(2)}, u32[]{:S(2)}) collective-permute-start(f32[4,17,17]{2,0,1:T(4,128)S(1)} %fusion.180), channel_id=1, source_target_pairs={{0,12},{4,0},{8,4},{12,8},{1,13},{5,1},{9,5},{13,9},{2,14},{6,2},{... | collective-permute-start | bytes 13880 | tf_op jit(solution)/shard_map/ppermute | solution.py:158
  121.5 18.4 %copy-start.1 = (f32[4,17,17]{2,0,1:T(4,128)}, f32[4,17,17]{2,0,1:T(4,128)S(1)}, u32[]{:S(2)}) copy-start(f32[4,17,17]{2,0,1:T(4,128)S(1)} %multiply_bitcast_fusion) | copy-start | bytes 13876
Sparse Core Ops, SparseCore 0:
  11.1 82.4 all-gather.1

commit v12 on v11

--- a/solution.py
+++ b/solution.py
@@ -115,7 +115,14 @@
 
 def matched_kernel(patch_of, warped_ref, ref_ref, rows_ref, coef_ref, col_ref, out_ref):
     middle = jnp.dot(rows_ref[0], coef_ref[0], preferred_element_type=jnp.float32, precision=exact_mode)
-    fitted = jnp.dot(middle, col_ref[0], preferred_element_type=jnp.float32, precision=exact_mode)
+    cols = col_ref[0]
+    middle_high = middle.astype(jnp.bfloat16)
+    middle_low = (middle - middle_high.astype(jnp.float32)).astype(jnp.bfloat16)
+    cols_high = cols.astype(jnp.bfloat16)
+    cols_low = (cols - cols_high.astype(jnp.float32)).astype(jnp.bfloat16)
+    fitted = jnp.dot(middle_high, cols_high, preferred_element_type=jnp.float32)
+    fitted = fitted + jnp.dot(middle_low, cols_high, preferred_element_type=jnp.float32)
+    fitted = fitted + jnp.dot(middle_high, cols_low, preferred_element_type=jnp.float32)
     out_ref[0] = (warped_ref[0] - ref_ref[0]) - fitted
 
 

time: 147 us -> 146 us (level)
  Pallas kernels: 26.5 us -> 24.9 us
where the time goes in v12:
time: 146 us; the launch traced here: 145 us
  waiting for transfers between devices  50.6 us (35%)
  matrix products  29.3 us (20%)
  Pallas kernels  24.9 us (17%)
  between operations  14.2 us (10%)
  starting transfers between devices  10.6 us (7%)
  other arithmetic  9.85 us (7%)
  local copies, waits for them, and re-layouts  5.84 us (4%)
    all_gather x1, waiting for transfers between devices, body(): lax.all_gather(ref_patch, PATCH_PARTS + VISIT_PARTS, axis=0, tiled=True)  46.5 us
    pallas_call x1, Pallas kernels, matched_pieces(): pl.pallas_call(matched_kernel, out_shape=jax.ShapeDtypeStruct(warped_all....  15.6 us
    dot_general x1, matrix products, warp_batch(): jnp.einsum('kia,kab->kib', left_matrix, slab_images, precision=warp_mode)  11.6 us
    dot_general x1, matrix products, warp_batch(): return jnp.einsum('kib,kjb->kij', middle, right_matrix, precision=warp_mode)  10.8 us
    ppermute x6, starting transfers between devices, ring_sum(): received.append(lax.ppermute(value, axis_name, pairs))  10.6 us
    pallas_call x1, Pallas kernels, reference_terms(): pl.pallas_call(reference_terms_kernel, out_shape=jax.ShapeDtypeStruct((pi...  9.29 us
    cos x2, other arithmetic, chebyshev_rows(): return jnp.cos(orders[:, None] * jnp.arccos(coordinate)[None, :])  9.25 us
    dot_general x1, matrix products, project_terms(): jnp.einsum('mtp,mpq->mtq', row_basis, differences, precision=warp_mode)  3.92 us
  transfers between devices with their start and end apart: 7, of which 5 were waited for; matrix products, arithmetic and copies ran while one was open for 28% of the time, Pallas kernels for 0%

profile of v12, /device:TPU:0, one launch (start us, length us, event | category | flops | bytes accessed | tf_op | source)
XLA Modules:
  0.0 145.3 jit_solution(2770389805078995706)
XLA Ops:
  7.2 0.0 all-gather.2.cloned.1.call-start
  7.2 0.7 all-gather.2.cloned.1.call-update
  8.0 0.8 slice_bitcast_fusion.8
  8.7 0.8 slice_bitcast_fusion.9
  9.5 0.1 fusion.104
  9.6 0.1 iota_add_fusion
  9.7 11.6 %fusion.13 = f32[8,512,512]{2,1,0:T(8,128)S(1)} fusion(f32[8,512,512]{2,1,0:T(8,128)} %param.8, f32[8]{0:T(128)S(1)} %get-tuple-element.29, f32[8]{0:T(128)S(1)} %get-tuple-element.28, f32[8]{0:T(128)S(1)} %get-tuple-element.27, f32[8]{0:T(128)S(1)} %get-tuple-element.26, f32[8]{0:T(128)S(1)} %get-tuple-element.25, f32[8]{0:T(128)S(1)} %get-tuple-element.30, ...), kind=kOutput, calls=%fused_computation.15 | convolution fusion | flops 6469713920 | bytes 16793792 | tf_op jit(solution)/shard_map/kia,kab->kib/dot_general | solution.py:43
  21.3 0.0 copy-start.2
  21.3 0.0 copy-start.3
  21.3 10.8 %fusion.warped_ref = f32[8,512,512]{2,1,0:T(8,128)S(1)} fusion(f32[8,512,512]{2,1,0:T(8,128)S(1)} %fusion.13, f32[8]{0:T(128)S(1)} %get-tuple-element.4, f32[8]{0:T(128)S(1)} %get-tuple-element.5, f32[8]{0:T(128)S(1)} %get-tuple-element.6, f32[8]{0:T(128)S(1)} %get-tuple-element.7, f32[8]{0:T(128)S(1)} %get-tuple-element.8, f32[8]{0:T(128)S(1)} %get-tuple-element.3, ...), kind=kOutput, calls=%fused_computation.1 | convolution fusion | flops 6469713920 | bytes 16793792 | tf_op jit(solution)/shard_map/kib,kjb->kij/dot_general | solution.py:45
  32.2 0.0 copy-start
  32.2 0.0 copy-done.2
  32.2 0.2 sqrt_atan2_fusion
  32.4 2.6 %multiply_cosine_fusion.1 = (f32[8,17,512]{2,1,0:T(8,128)S(1)}, f32[8,17,512]{2,1,0:T(8,128)S(1)}) fusion(f32[8,512]{1,0:T(8,128)S(1)} %get-tuple-element.33, f32[17]{0:T(128)S(1)} %iota_convert_fusion, f32[8,512]{1,0:T(8,128)S(1)} %get-tuple-element.34), kind=kLoop, calls=%fused_computation.59 | loop fusion | flops 139264 | bytes 589892 | tf_op jit(solution)/shard_map/vmap()/cos | solution.py:52
  34.9 0.8 pad.18.col_ref
  35.7 0.8 pad.17.row_ref
  36.5 0.0 copy-done.3
  36.5 6.7 %multiply_cosine_fusion = f32[8,512,17]{2,1,0:T(8,128)S(1)} fusion(f32[8,512]{1,0:T(8,128)S(1)} %get-tuple-element.34, f32[17]{0:T(128)S(1)} %iota_convert_fusion), kind=kLoop, calls=%fused_computation.57 | loop fusion | flops 69632 | bytes 294980 | tf_op jit(solution)/shard_map/vmap()/cos | solution.py:52
  43.2 0.0 copy-done
  43.2 3.9 %fusion.66 = f32[8,17,512]{2,1,0:T(8,128)S(1)} fusion(f32[8,512,512]{2,1,0:T(8,128)S(1)} %fusion.warped_ref, f32[8,512]{1,0:T(8,128)S(1)} %get-tuple-element.34, f32[17]{0:T(128)S(1)} %iota_convert_fusion), kind=kOutput, calls=%fused_computation.63 | convolution fusion | flops 213979136 | bytes 8683588 | tf_op jit(solution)/shard_map/mtp,mpq->mtq/dot_general | solution.py:66
  47.2 46.5 %all-gather.2.cloned.1.call-done = f32[128,64,512]{2,1,0:T(8,128)} async-done(((f32[1,64,512]{2,1,0:T(8,128)}), f32[128,64,512]{2,1,0:T(8,128)}) %all-gather.2.cloned.1.call-update) | async-done | bytes 16777232 | tf_op jit(solution)/shard_map/all_gather | solution.py:178
  93.6 9.3 %shard_map.86 = f32[8,24,24]{2,1,0:T(8,128)} custom-call(s32[8]{0:T(128)} %patch_of.3, f32[16,512,512]{2,1,0:T(8,128)} %bitcast.55, f32[8,24,512]{2,1,0:T(8,128)} %pad.17.row_ref, f32[8,24,512]{2,1,0:T(8,128)} %pad.18.col_ref), custom_call_target="tpu_custom_call" | custom-call | flops 105381888 | bytes 9175040 | tf_op jit(solution)/shard_map/pallas_call | solution.py:94
  102.9 2.7 %convolution_subtract_fusion = f32[8,17,17]{2,1,0:T(8,128)S(1)} fusion(f32[8,17,512]{2,1,0:T(8,128)S(1)} %fusion.66, f32[8,512]{1,0:T(8,128)S(1)} %get-tuple-element.33, f32[17]{0:T(128)S(1)} %iota_convert_fusion, f32[8,24,24]{2,1,0:T(8,128)} %shard_map.86), kind=kOutput, calls=%fused_computation.58 | convolution fusion | flops 14276872 | bytes 313476 | tf_op jit(solution)/shard_map/mtq,muq->mtu/dot_general | solution.py:67
  105.6 0.2 fusion.67
  105.8 1.1 collective-permute-start
  107.0 3.1 %collective-permute-start.1 = (f32[4,17,17]{2,0,1:T(4,128)S(1)}, f32[4,17,17]{2,0,1:T(4,128)S(1)}, u32[]{:S(2)}, u32[]{:S(2)}) collective-permute-start(f32[4,17,17]{2,0,1:T(4,128)S(1)} %fusion.67), channel_id=1, source_target_pairs={{0,2},{1,3},{2,0},{3,1},{4,6},{5,7},{6,4},{7,5},{8,10},{9,11},{10,... | collective-permute-start | bytes 13880 | tf_op jit(solution)/shard_map/ppermute | solution.py:165
  110.0 1.4 collective-permute-start.2
  111.4 1.5 %pad.16.rows_ref = f32[8,512,24]{2,1,0:T(8,128)} pad(f32[8,512,17]{2,1,0:T(8,128)S(1)} %multiply_cosine_fusion, f32[]{:T(128)} %constant.137.clone.1), padding=0_0x0_0x0_7 | pad | bytes 671748 | tf_op jit(solution)/shard_map/jit(_pad)/pad | solution.py:132
  112.9 0.0 collective-permute-done
  112.9 0.0 collective-permute-done.1
  112.9 1.0 collective-permute-done.2
  114.0 0.6 collective-permute-start.3
  114.7 2.8 %collective-permute-start.4 = (f32[4,17,17]{2,0,1:T(4,128)S(1)}, f32[4,17,17]{2,0,1:T(4,128)S(1)}, u32[]{:S(2)}, u32[]{:S(2)}) collective-permute-start(f32[4,17,17]{2,0,1:T(4,128)S(1)} %fusion.180), channel_id=1, source_target_pairs={{0,8},{4,12},{8,0},{12,4},{1,9},{5,13},{9,1},{13,5},{2,10},{6,14},... | collective-permute-start | bytes 13880 | tf_op jit(solution)/shard_map/ppermute | solution.py:165
  117.5 1.5 %collective-permute-start.5 = (f32[4,17,17]{2,0,1:T(4,128)S(1)}, f32[4,17,17]{2,0,1:T(4,128)S(1)}, u32[]{:S(2)}, u32[]{:S(2)}) collective-permute-start(f32[4,17,17]{2,0,1:T(4,128)S(1)} %fusion.180), channel_id=1, source_target_pairs={{0,12},{4,0},{8,4},{12,8},{1,13},{5,1},{9,5},{13,9},{2,14},{6,2},{... | collective-permute-start | bytes 13880 | tf_op jit(solution)/shard_map/ppermute | solution.py:165
  119.1 0.2 collective-permute-done.3
  119.2 0.9 collective-permute-done.4
  120.1 1.3 collective-permute-done.5
  121.5 0.0 copy-start.1
  121.6 0.6 gather_fusion
  122.1 0.1 broadcast_select_fusion
  122.2 0.6 pad.19.coef_ref
  122.8 15.6 %shard_map.87 = f32[8,512,512]{2,1,0:T(8,128)} custom-call(s32[8]{0:T(128)} %patch_of.3, f32[8,512,512]{2,1,0:T(8,128)} %copy-done, f32[16,512,512]{2,1,0:T(8,128)} %bitcast.56, f32[8,512,24]{2,1,0:T(8,128)} %pad.16.rows_ref, f32[8,24,24]{2,1,0:T(8,128)} %pad.19.coef_ref, f32[8,24,512]{2,1,0:T(8,128)} %pad.18.col_ref), custom_call_target="tpu_custom_call" | custom-call | flops 105381888 | bytes 25165824 | tf_op jit(solution)/shard_map/pallas_call | solution.py:136
  138.4 0.0 copy-done.1
  (13 shorter events, 0.2 us)
Async XLA Ops:
  7.2 86.4 %all-gather.2.cloned.1.call-start = ((), (), s32[]{:S(2)}) async-start(), calls=%async_computation | async-start | bytes 16908288 | tf_op jit(solution)/shard_map/all_gather | solution.py:178
  21.3 10.9 %copy-start.2 = (s32[8,2]{0,1:T(2,128)S(1)}, s32[8,2]{0,1:T(2,128)}, u32[]{:S(2)}) copy-start(s32[8,2]{0,1:T(2,128)} %param.12) | copy-start | bytes 196
  21.3 15.2 %copy-start.3 = (s32[8]{0:T(128)S(1)}, s32[8]{0:T(128)}, u32[]{:S(2)}) copy-start(s32[8]{0:T(128)} %param.11) | copy-start | bytes 100
  32.2 11.1 %copy-start = (f32[8,512,512]{2,1,0:T(8,128)}, f32[8,512,512]{2,1,0:T(8,128)S(1)}, u32[]{:S(2)}) copy-start(f32[8,512,512]{2,1,0:T(8,128)S(1)} %fusion.warped_ref) | copy-start | bytes 25165828
  105.8 7.1 %collective-permute-start = (f32[4,17,17]{2,0,1:T(4,128)S(1)}, f32[4,17,17]{2,0,1:T(4,128)S(1)}, u32[]{:S(2)}, u32[]{:S(2)}) collective-permute-start(f32[4,17,17]{2,0,1:T(4,128)S(1)} %fusion.67), channel_id=1, source_target_pairs={{0,1},{1,2},{2,3},{3,0},{4,5},{5,6},{6,7},{7,4},{8,9},{9,10},{10,1... | collective-permute-start | bytes 13880 | tf_op jit(solution)/shard_map/ppermute | solution.py:165
  107.0 6.0 %collective-permute-start.1 = (f32[4,17,17]{2,0,1:T(4,128)S(1)}, f32[4,17,17]{2,0,1:T(4,128)S(1)}, u32[]{:S(2)}, u32[]{:S(2)}) collective-permute-start(f32[4,17,17]{2,0,1:T(4,128)S(1)} %fusion.67), channel_id=1, source_target_pairs={{0,2},{1,3},{2,0},{3,1},{4,6},{5,7},{6,4},{7,5},{8,10},{9,11},{10,... | collective-permute-start | bytes 13880 | tf_op jit(solution)/shard_map/ppermute | solution.py:165
  110.0 3.9 %collective-permute-start.2 = (f32[4,17,17]{2,0,1:T(4,128)S(1)}, f32[4,17,17]{2,0,1:T(4,128)S(1)}, u32[]{:S(2)}, u32[]{:S(2)}) collective-permute-start(f32[4,17,17]{2,0,1:T(4,128)S(1)} %fusion.67), channel_id=1, source_target_pairs={{0,3},{1,0},{2,1},{3,2},{4,7},{5,4},{6,5},{7,6},{8,11},{9,8},{10,9... | collective-permute-start | bytes 13880 | tf_op jit(solution)/shard_map/ppermute | solution.py:165
  114.0 5.2 %collective-permute-start.3 = (f32[4,17,17]{2,0,1:T(4,128)S(1)}, f32[4,17,17]{2,0,1:T(4,128)S(1)}, u32[]{:S(2)}, u32[]{:S(2)}) collective-permute-start(f32[4,17,17]{2,0,1:T(4,128)S(1)} %fusion.180), channel_id=1, source_target_pairs={{0,4},{4,8},{8,12},{12,0},{1,5},{5,9},{9,13},{13,1},{2,6},{6,10},{... | collective-permute-start | bytes 13880 | tf_op jit(solution)/shard_map/ppermute | solution.py:165
  114.7 5.4 %collective-permute-start.4 = (f32[4,17,17]{2,0,1:T(4,128)S(1)}, f32[4,17,17]{2,0,1:T(4,128)S(1)}, u32[]{:S(2)}, u32[]{:S(2)}) collective-permute-start(f32[4,17,17]{2,0,1:T(4,128)S(1)} %fusion.180), channel_id=1, source_target_pairs={{0,8},{4,12},{8,0},{12,4},{1,9},{5,13},{9,1},{13,5},{2,10},{6,14},... | collective-permute-start | bytes 13880 | tf_op jit(solution)/shard_map/ppermute | solution.py:165
  117.5 3.9 %collective-permute-start.5 = (f32[4,17,17]{2,0,1:T(4,128)S(1)}, f32[4,17,17]{2,0,1:T(4,128)S(1)}, u32[]{:S(2)}, u32[]{:S(2)}) collective-permute-start(f32[4,17,17]{2,0,1:T(4,128)S(1)} %fusion.180), channel_id=1, source_target_pairs={{0,12},{4,0},{8,4},{12,8},{1,13},{5,1},{9,5},{13,9},{2,14},{6,2},{... | collective-permute-start | bytes 13880 | tf_op jit(solution)/shard_map/ppermute | solution.py:165
  121.5 16.9 %copy-start.1 = (f32[4,17,17]{2,0,1:T(4,128)}, f32[4,17,17]{2,0,1:T(4,128)S(1)}, u32[]{:S(2)}) copy-start(f32[4,17,17]{2,0,1:T(4,128)S(1)} %multiply_bitcast_fusion) | copy-start | bytes 13876
Sparse Core Ops, SparseCore 0:
  11.1 82.4 all-gather.1

commit v13 on v12

--- a/solution.py
+++ b/solution.py
@@ -128,10 +128,9 @@
 
 def matched_pieces(warped_all, ref_block, piece_patch, row_basis, chosen, col_basis):
     piece_count, terms, side_len = row_basis.shape
-    extra = BASIS_ROWS - terms
-    rows = jnp.pad(jnp.transpose(row_basis, (0, 2, 1)), ((0, 0), (0, 0), (0, extra)))
-    coefs = jnp.pad(chosen, ((0, 0), (0, extra), (0, extra)))
-    cols = jnp.pad(col_basis, ((0, 0), (0, extra), (0, 0)))
+    rows = jnp.transpose(row_basis, (0, 2, 1))
+    coefs = chosen
+    cols = col_basis
     image_spec = pl.BlockSpec((1, side_len, side_len), lambda k, patch_of: (k, 0, 0))
     return pl.pallas_call(
         matched_kernel,
@@ -142,9 +141,9 @@
             in_specs=[
                 image_spec,
                 pl.BlockSpec((1, side_len, side_len), lambda k, patch_of: (patch_of[k], 0, 0)),
-                pl.BlockSpec((1, side_len, BASIS_ROWS), lambda k, patch_of: (k, 0, 0)),
-                pl.BlockSpec((1, BASIS_ROWS, BASIS_ROWS), lambda k, patch_of: (k, 0, 0)),
-                pl.BlockSpec((1, BASIS_ROWS, side_len), lambda k, patch_of: (k, 0, 0)),
+                pl.BlockSpec((1, side_len, terms), lambda k, patch_of: (k, 0, 0)),
+                pl.BlockSpec((1, terms, terms), lambda k, patch_of: (k, 0, 0)),
+                pl.BlockSpec((1, terms, side_len), lambda k, patch_of: (k, 0, 0)),
             ],
             out_specs=image_spec,
         ),

time: 146 us -> 146 us (level)
  matrix products: 29.3 us -> 32.1 us
  waiting for transfers between devices: 50.6 us -> 48.2 us
  local copies, waits for them, and re-layouts: 5.84 us -> 3.73 us
  other arithmetic: 9.85 us -> 11.9 us
    all_gather x1, waiting for transfers between devices: 46.5 us -> 42.3 us  [body(): lax.all_gather(ref_patch, PATCH_PARTS + VISIT_PARTS, axis=0, tiled=True)]
    pad x2 -> x0, local copies, waits for them, and re-layouts: 2.17 us -> none  [the longest x1 1.52 us: matched_pieces(): jnp.pad(jnp.transpose(row_basis, (0, 2, 1)), ((0, 0), (0, 0), (0, extra)))]
    ppermute x6, waiting for transfers between devices: 3.42 us -> 5.15 us  [ring_sum(): received.append(lax.ppermute(value, axis_name, pairs))]
    dot_general x1, matrix products: 3.92 us -> 5.58 us  [project_terms(): jnp.einsum('mtp,mpq->mtq', row_basis, differences, precision=warp_mode)]
  transfers between devices with their start and end apart: 7 -> 7, of which waited for: 5 -> 6; matrix products, arithmetic and copies ran while one was open for 28% -> 30% of each run, Pallas kernels for 0% -> 0%
where the time goes in v13:
time: 146 us
  waiting for transfers between devices  48.2 us (33%)
  matrix products  32.1 us (22%)
  Pallas kernels  25.1 us (17%)
  between operations  14.2 us (10%)
  other arithmetic  11.9 us (8%)
  starting transfers between devices  10.4 us (7%)
  local copies, waits for them, and re-layouts  3.73 us (3%)
    all_gather x1, waiting for transfers between devices, body(): lax.all_gather(ref_patch, PATCH_PARTS + VISIT_PARTS, axis=0, tiled=True)  42.3 us
    pallas_call x1, Pallas kernels, matched_pieces(): pl.pallas_call(matched_kernel, out_shape=jax.ShapeDtypeStruct(warped_all....  15.7 us
    dot_general x1, matrix products, warp_batch(): return jnp.einsum('kib,kjb->kij', middle, right_matrix, precision=warp_mode)  11.9 us
    dot_general x1, matrix products, warp_batch(): jnp.einsum('kia,kab->kib', left_matrix, slab_images, precision=warp_mode)  11.6 us
    cos x2, other arithmetic, chebyshev_rows(): return jnp.cos(orders[:, None] * jnp.arccos(coordinate)[None, :])  10.7 us
    ppermute x6, starting transfers between devices, ring_sum(): received.append(lax.ppermute(value, axis_name, pairs))  10.4 us
    pallas_call x1, Pallas kernels, reference_terms(): pl.pallas_call(reference_terms_kernel, out_shape=jax.ShapeDtypeStruct((pi...  9.36 us
    dot_general x1, matrix products, project_terms(): jnp.einsum('mtp,mpq->mtq', row_basis, differences, precision=warp_mode)  5.58 us
  transfers between devices with their start and end apart: 7, of which 6 were waited for; matrix products, arithmetic and copies ran while one was open for 30% of the time, Pallas kernels for 0%

profile of v13, /device:TPU:0, one launch (start us, length us, event | category | flops | bytes accessed | tf_op | source)
XLA Modules:
  0.0 145.5 jit_solution(4196758104545360383)
XLA Ops:
  7.2 0.0 all-gather.2.cloned.1.call-start
  7.2 0.7 all-gather.2.cloned.1.call-update
  8.0 0.8 slice_bitcast_fusion.8
  8.7 0.8 slice_bitcast_fusion.9
  9.5 0.1 fusion.104
  9.6 0.1 iota_add_fusion
  9.7 11.6 %fusion.13 = f32[8,512,512]{2,1,0:T(8,128)S(1)} fusion(f32[8,512,512]{2,1,0:T(8,128)} %param.8, f32[8]{0:T(128)S(1)} %get-tuple-element.29, f32[8]{0:T(128)S(1)} %get-tuple-element.28, f32[8]{0:T(128)S(1)} %get-tuple-element.27, f32[8]{0:T(128)S(1)} %get-tuple-element.26, f32[8]{0:T(128)S(1)} %get-tuple-element.25, f32[8]{0:T(128)S(1)} %get-tuple-element.30, ...), kind=kOutput, calls=%fused_computation.15 | convolution fusion | flops 6469713920 | bytes 16793792 | tf_op jit(solution)/shard_map/kia,kab->kib/dot_general | solution.py:43
  21.3 0.0 copy-start.2
  21.3 0.0 copy-start.3
  21.3 11.9 %fusion.warped_ref = f32[8,512,512]{2,1,0:T(8,128)} fusion(f32[8,512,512]{2,1,0:T(8,128)S(1)} %fusion.13, f32[8]{0:T(128)S(1)} %get-tuple-element.4, f32[8]{0:T(128)S(1)} %get-tuple-element.5, f32[8]{0:T(128)S(1)} %get-tuple-element.6, f32[8]{0:T(128)S(1)} %get-tuple-element.7, f32[8]{0:T(128)S(1)} %get-tuple-element.8, f32[8]{0:T(128)S(1)} %get-tuple-element.3, ...), kind=kOutput, calls=%fused_computation.1 | convolution fusion | flops 6469713920 | bytes 16793792 | tf_op jit(solution)/shard_map/kib,kjb->kij/dot_general | solution.py:45
  33.3 0.0 copy-done.2
  33.3 0.2 sqrt_atan2_fusion
  33.5 2.6 %multiply_cosine_fusion.1 = (f32[8,17,512]{2,1,0:T(8,128)S(1)}, f32[8,17,512]{2,1,0:T(8,128)S(1)}) fusion(f32[8,512]{1,0:T(8,128)S(1)} %get-tuple-element.33, f32[17]{0:T(128)S(1)} %iota_convert_fusion, f32[8,512]{1,0:T(8,128)S(1)} %get-tuple-element.34), kind=kLoop, calls=%fused_computation.59 | loop fusion | flops 139264 | bytes 589892 | tf_op jit(solution)/shard_map/vmap()/cos | solution.py:52
  36.0 0.0 copy-start
  36.0 0.8 pad.8.col_ref
  36.9 0.8 pad.7.row_ref
  37.6 0.0 copy-done.3
  37.7 8.1 %multiply_cosine_fusion.rows_ref = f32[8,512,17]{2,1,0:T(8,128)} fusion(f32[8,512]{1,0:T(8,128)S(1)} %get-tuple-element.34, f32[17]{0:T(128)S(1)} %iota_convert_fusion), kind=kLoop, calls=%fused_computation.57 | loop fusion | flops 69632 | bytes 294980 | tf_op jit(solution)/shard_map/vmap()/cos | solution.py:52
  45.8 5.6 %fusion.66 = f32[8,17,512]{2,1,0:T(8,128)S(1)} fusion(f32[8,512,512]{2,1,0:T(8,128)} %fusion.warped_ref, f32[8,512]{1,0:T(8,128)S(1)} %get-tuple-element.34, f32[17]{0:T(128)S(1)} %iota_convert_fusion), kind=kOutput, calls=%fused_computation.63 | convolution fusion | flops 213979136 | bytes 8683588 | tf_op jit(solution)/shard_map/mtp,mpq->mtq/dot_general | solution.py:66
  51.4 42.3 %all-gather.2.cloned.1.call-done = f32[128,64,512]{2,1,0:T(8,128)} async-done(((f32[1,64,512]{2,1,0:T(8,128)}), f32[128,64,512]{2,1,0:T(8,128)}) %all-gather.2.cloned.1.call-update) | async-done | bytes 16777232 | tf_op jit(solution)/shard_map/all_gather | solution.py:177
  93.7 9.4 %shard_map.86 = f32[8,24,24]{2,1,0:T(8,128)} custom-call(s32[8]{0:T(128)} %patch_of.3, f32[16,512,512]{2,1,0:T(8,128)} %bitcast.55, f32[8,24,512]{2,1,0:T(8,128)} %pad.7.row_ref, f32[8,24,512]{2,1,0:T(8,128)} %pad.8.col_ref), custom_call_target="tpu_custom_call" | custom-call | flops 105381888 | bytes 9175040 | tf_op jit(solution)/shard_map/pallas_call | solution.py:94
  103.0 0.0 copy-done
  103.0 2.7 %convolution_subtract_fusion = f32[8,17,17]{2,1,0:T(8,128)S(1)} fusion(f32[8,17,512]{2,1,0:T(8,128)S(1)} %fusion.66, f32[8,512]{1,0:T(8,128)S(1)} %get-tuple-element.33, f32[17]{0:T(128)S(1)} %iota_convert_fusion, f32[8,24,24]{2,1,0:T(8,128)} %shard_map.86), kind=kOutput, calls=%fused_computation.58 | convolution fusion | flops 14276872 | bytes 313476 | tf_op jit(solution)/shard_map/mtq,muq->mtu/dot_general | solution.py:67
  105.8 0.2 fusion.67
  106.0 1.2 collective-permute-start
  107.2 2.9 %collective-permute-start.1 = (f32[4,17,17]{2,0,1:T(4,128)S(1)}, f32[4,17,17]{2,0,1:T(4,128)S(1)}, u32[]{:S(2)}, u32[]{:S(2)}) collective-permute-start(f32[4,17,17]{2,0,1:T(4,128)S(1)} %fusion.67), channel_id=1, source_target_pairs={{0,2},{1,3},{2,0},{3,1},{4,6},{5,7},{6,4},{7,5},{8,10},{9,11},{10,... | collective-permute-start | bytes 13880 | tf_op jit(solution)/shard_map/ppermute | solution.py:164
  110.1 1.3 collective-permute-start.2
  111.4 0.0 collective-permute-done
  111.4 1.2 collective-permute-done.1
  112.6 1.4 collective-permute-done.2
  114.1 0.7 collective-permute-start.3
  114.8 2.8 %collective-permute-start.4 = (f32[4,17,17]{2,0,1:T(4,128)S(1)}, f32[4,17,17]{2,0,1:T(4,128)S(1)}, u32[]{:S(2)}, u32[]{:S(2)}) collective-permute-start(f32[4,17,17]{2,0,1:T(4,128)S(1)} %fusion.180), channel_id=1, source_target_pairs={{0,8},{4,12},{8,0},{12,4},{1,9},{5,13},{9,1},{13,5},{2,10},{6,14},... | collective-permute-start | bytes 13880 | tf_op jit(solution)/shard_map/ppermute | solution.py:164
  117.7 1.4 collective-permute-start.5
  119.1 0.3 collective-permute-done.3
  119.3 1.0 collective-permute-done.4
  120.3 1.3 collective-permute-done.5
  121.7 0.0 copy-start.1
  121.7 0.6 gather_fusion
  122.3 0.7 broadcast_select_fusion.coef_ref
  123.0 15.7 %shard_map.87 = f32[8,512,512]{2,1,0:T(8,128)} custom-call(s32[8]{0:T(128)} %patch_of.3, f32[8,512,512]{2,1,0:T(8,128)} %fusion.warped_ref, f32[16,512,512]{2,1,0:T(8,128)} %bitcast.56, f32[8,512,17]{2,1,0:T(8,128)} %multiply_cosine_fusion.rows_ref, f32[8,17,17]{2,1,0:T(8,128)} %broadcast_select_fusion.coef_ref, f32[8,17,512]{2,1,0:T(8,128)} %copy-done), custom_call_target="tpu_custom_call" | custom-call | flops 105381888 | bytes 25165824 | tf_op jit(solution)/shard_map/pallas_call | solution.py:135
  138.7 0.0 copy-done.1
  (13 shorter events, 0.2 us)
Async XLA Ops:
  7.2 86.5 %all-gather.2.cloned.1.call-start = ((), (), s32[]{:S(2)}) async-start(), calls=%async_computation | async-start | bytes 16908288 | tf_op jit(solution)/shard_map/all_gather | solution.py:177
  21.3 12.0 %copy-start.2 = (s32[8,2]{0,1:T(2,128)S(1)}, s32[8,2]{0,1:T(2,128)}, u32[]{:S(2)}) copy-start(s32[8,2]{0,1:T(2,128)} %param.12) | copy-start | bytes 196
  21.3 16.3 %copy-start.3 = (s32[8]{0:T(128)S(1)}, s32[8]{0:T(128)}, u32[]{:S(2)}) copy-start(s32[8]{0:T(128)} %param.11) | copy-start | bytes 100
  36.0 67.0 %copy-start = (f32[8,17,512]{2,1,0:T(8,128)}, f32[8,17,512]{2,1,0:T(8,128)S(1)}, u32[]{:S(2)}) copy-start(f32[8,17,512]{2,1,0:T(8,128)S(1)} %get-tuple-element.21.col_ref) | copy-start | bytes 835588
  106.0 5.4 %collective-permute-start = (f32[4,17,17]{2,0,1:T(4,128)S(1)}, f32[4,17,17]{2,0,1:T(4,128)S(1)}, u32[]{:S(2)}, u32[]{:S(2)}) collective-permute-start(f32[4,17,17]{2,0,1:T(4,128)S(1)} %fusion.67), channel_id=1, source_target_pairs={{0,1},{1,2},{2,3},{3,0},{4,5},{5,6},{6,7},{7,4},{8,9},{9,10},{10,1... | collective-permute-start | bytes 13880 | tf_op jit(solution)/shard_map/ppermute | solution.py:164
  107.2 5.4 %collective-permute-start.1 = (f32[4,17,17]{2,0,1:T(4,128)S(1)}, f32[4,17,17]{2,0,1:T(4,128)S(1)}, u32[]{:S(2)}, u32[]{:S(2)}) collective-permute-start(f32[4,17,17]{2,0,1:T(4,128)S(1)} %fusion.67), channel_id=1, source_target_pairs={{0,2},{1,3},{2,0},{3,1},{4,6},{5,7},{6,4},{7,5},{8,10},{9,11},{10,... | collective-permute-start | bytes 13880 | tf_op jit(solution)/shard_map/ppermute | solution.py:164
  110.1 3.9 %collective-permute-start.2 = (f32[4,17,17]{2,0,1:T(4,128)S(1)}, f32[4,17,17]{2,0,1:T(4,128)S(1)}, u32[]{:S(2)}, u32[]{:S(2)}) collective-permute-start(f32[4,17,17]{2,0,1:T(4,128)S(1)} %fusion.67), channel_id=1, source_target_pairs={{0,3},{1,0},{2,1},{3,2},{4,7},{5,4},{6,5},{7,6},{8,11},{9,8},{10,9... | collective-permute-start | bytes 13880 | tf_op jit(solution)/shard_map/ppermute | solution.py:164
  114.1 5.2 %collective-permute-start.3 = (f32[4,17,17]{2,0,1:T(4,128)S(1)}, f32[4,17,17]{2,0,1:T(4,128)S(1)}, u32[]{:S(2)}, u32[]{:S(2)}) collective-permute-start(f32[4,17,17]{2,0,1:T(4,128)S(1)} %fusion.180), channel_id=1, source_target_pairs={{0,4},{4,8},{8,12},{12,0},{1,5},{5,9},{9,13},{13,1},{2,6},{6,10},{... | collective-permute-start | bytes 13880 | tf_op jit(solution)/shard_map/ppermute | solution.py:164
  114.8 5.4 %collective-permute-start.4 = (f32[4,17,17]{2,0,1:T(4,128)S(1)}, f32[4,17,17]{2,0,1:T(4,128)S(1)}, u32[]{:S(2)}, u32[]{:S(2)}) collective-permute-start(f32[4,17,17]{2,0,1:T(4,128)S(1)} %fusion.180), channel_id=1, source_target_pairs={{0,8},{4,12},{8,0},{12,4},{1,9},{5,13},{9,1},{13,5},{2,10},{6,14},... | collective-permute-start | bytes 13880 | tf_op jit(solution)/shard_map/ppermute | solution.py:164
  117.7 3.9 %collective-permute-start.5 = (f32[4,17,17]{2,0,1:T(4,128)S(1)}, f32[4,17,17]{2,0,1:T(4,128)S(1)}, u32[]{:S(2)}, u32[]{:S(2)}) collective-permute-start(f32[4,17,17]{2,0,1:T(4,128)S(1)} %fusion.180), channel_id=1, source_target_pairs={{0,12},{4,0},{8,4},{12,8},{1,13},{5,1},{9,5},{13,9},{2,14},{6,2},{... | collective-permute-start | bytes 13880 | tf_op jit(solution)/shard_map/ppermute | solution.py:164
  121.7 17.0 %copy-start.1 = (f32[4,17,17]{2,0,1:T(4,128)}, f32[4,17,17]{2,0,1:T(4,128)S(1)}, u32[]{:S(2)}) copy-start(f32[4,17,17]{2,0,1:T(4,128)S(1)} %multiply_bitcast_fusion) | copy-start | bytes 13876
Sparse Core Ops, SparseCore 0:
  11.1 82.5 all-gather.1

commit v14 on v12

--- a/solution.py
+++ b/solution.py
@@ -71,10 +71,9 @@
 
 
 def reference_terms_kernel(patch_of, ref_ref, row_ref, col_ref, out_ref):
-    rows = row_ref[0]
     image = ref_ref[0]
-    rows_high = rows.astype(jnp.bfloat16)
-    rows_low = (rows - rows_high.astype(jnp.float32)).astype(jnp.bfloat16)
+    rows_high = row_ref[0, 0]
+    rows_low = row_ref[0, 1]
     image_high = image.astype(jnp.bfloat16)
     image_low = (image - image_high.astype(jnp.float32)).astype(jnp.bfloat16)
     middle = jnp.dot(rows_high, image_high, preferred_element_type=jnp.float32)
@@ -88,7 +87,10 @@
 def reference_terms(ref_block, piece_patch, row_basis, col_basis):
     piece_count, terms, side_len = row_basis.shape
     pad = ((0, 0), (0, BASIS_ROWS - terms), (0, 0))
-    rows = jnp.pad(row_basis, pad)
+    padded_rows = jnp.pad(row_basis, pad)
+    rows_high = padded_rows.astype(jnp.bfloat16)
+    rows_low = (padded_rows - rows_high.astype(jnp.float32)).astype(jnp.bfloat16)
+    rows = jnp.stack([rows_high, rows_low], axis=1)
     cols = jnp.pad(col_basis, pad)
     basis_spec = pl.BlockSpec((1, BASIS_ROWS, side_len), lambda k, patch_of: (k, 0, 0))
     out = pl.pallas_call(
@@ -99,7 +101,7 @@
             grid=(piece_count,),
             in_specs=[
                 pl.BlockSpec((1, side_len, side_len), lambda k, patch_of: (patch_of[k], 0, 0)),
-                basis_spec,
+                pl.BlockSpec((1, 2, BASIS_ROWS, side_len), lambda k, patch_of: (k, 0, 0, 0)),
                 basis_spec,
             ],
             out_specs=pl.BlockSpec((1, BASIS_ROWS, BASIS_ROWS), lambda k, patch_of: (k, 0, 0)),

time: 146 us -> 146 us (level)
  no operation moved by 1% of the time
where the time goes in v14:
time: 146 us; the launch traced here: 145 us
  waiting for transfers between devices  50 us (34%)
  matrix products  29.3 us (20%)
  Pallas kernels  25 us (17%)
  between operations  14.3 us (10%)
  starting transfers between devices  10.5 us (7%)
  other arithmetic  9.92 us (7%)
  local copies, waits for them, and re-layouts  5.88 us (4%)
    all_gather x1, waiting for transfers between devices, body(): lax.all_gather(ref_patch, PATCH_PARTS + VISIT_PARTS, axis=0, tiled=True)  46.3 us
    pallas_call x1, Pallas kernels, matched_pieces(): pl.pallas_call(matched_kernel, out_shape=jax.ShapeDtypeStruct(warped_all....  15.6 us
    dot_general x1, matrix products, warp_batch(): jnp.einsum('kia,kab->kib', left_matrix, slab_images, precision=warp_mode)  11.6 us
    dot_general x1, matrix products, warp_batch(): return jnp.einsum('kib,kjb->kij', middle, right_matrix, precision=warp_mode)  10.8 us
    ppermute x6, starting transfers between devices, ring_sum(): received.append(lax.ppermute(value, axis_name, pairs))  10.4 us
    pallas_call x1, Pallas kernels, reference_terms(): pl.pallas_call(reference_terms_kernel, out_shape=jax.ShapeDtypeStruct((pi...  9.36 us
    cos x2, other arithmetic, chebyshev_rows(): return jnp.cos(orders[:, None] * jnp.arccos(coordinate)[None, :])  9.25 us
    dot_general x1, matrix products, project_terms(): jnp.einsum('mtp,mpq->mtq', row_basis, differences, precision=warp_mode)  3.92 us
  transfers between devices with their start and end apart: 7, of which 5 were waited for; matrix products, arithmetic and copies ran while one was open for 28% of the time, Pallas kernels for 0%

profile of v14, /device:TPU:0, one launch (start us, length us, event | category | flops | bytes accessed | tf_op | source)
XLA Modules:
  0.0 144.9 jit_solution(11135321080294639099)
XLA Ops:
  7.2 0.0 all-gather.2.cloned.1.call-start
  7.2 0.7 all-gather.2.cloned.1.call-update
  8.0 0.8 slice_bitcast_fusion.8
  8.7 0.8 slice_bitcast_fusion.9
  9.5 0.1 fusion.106
  9.6 0.1 iota_add_fusion
  9.7 11.6 %fusion.13 = f32[8,512,512]{2,1,0:T(8,128)S(1)} fusion(f32[8,512,512]{2,1,0:T(8,128)} %param.8, f32[8]{0:T(128)S(1)} %get-tuple-element.29, f32[8]{0:T(128)S(1)} %get-tuple-element.28, f32[8]{0:T(128)S(1)} %get-tuple-element.27, f32[8]{0:T(128)S(1)} %get-tuple-element.26, f32[8]{0:T(128)S(1)} %get-tuple-element.25, f32[8]{0:T(128)S(1)} %get-tuple-element.30, ...), kind=kOutput, calls=%fused_computation.15 | convolution fusion | flops 6469713920 | bytes 16793792 | tf_op jit(solution)/shard_map/kia,kab->kib/dot_general | solution.py:43
  21.3 0.0 copy-start.2
  21.3 0.0 copy-start.3
  21.3 10.8 %fusion.warped_ref = f32[8,512,512]{2,1,0:T(8,128)S(1)} fusion(f32[8,512,512]{2,1,0:T(8,128)S(1)} %fusion.13, f32[8]{0:T(128)S(1)} %get-tuple-element.4, f32[8]{0:T(128)S(1)} %get-tuple-element.5, f32[8]{0:T(128)S(1)} %get-tuple-element.6, f32[8]{0:T(128)S(1)} %get-tuple-element.7, f32[8]{0:T(128)S(1)} %get-tuple-element.8, f32[8]{0:T(128)S(1)} %get-tuple-element.3, ...), kind=kOutput, calls=%fused_computation.1 | convolution fusion | flops 6469713920 | bytes 16793792 | tf_op jit(solution)/shard_map/kib,kjb->kij/dot_general | solution.py:45
  32.2 0.0 copy-start
  32.2 0.0 copy-done.2
  32.2 0.2 sqrt_atan2_fusion
  32.4 2.6 %multiply_cosine_fusion.1 = (f32[8,17,512]{2,1,0:T(8,128)S(1)}, f32[8,17,512]{2,1,0:T(8,128)S(1)}) fusion(f32[8,512]{1,0:T(8,128)S(1)} %get-tuple-element.33, f32[17]{0:T(128)S(1)} %iota_convert_fusion, f32[8,512]{1,0:T(8,128)S(1)} %get-tuple-element.34), kind=kLoop, calls=%fused_computation.61 | loop fusion | flops 139264 | bytes 589892 | tf_op jit(solution)/shard_map/vmap()/cos | solution.py:52
  35.1 0.8 copy.14.row_ref
  35.9 0.8 pad.18.col_ref
  36.6 0.0 copy-done.3
  36.7 6.7 %multiply_cosine_fusion = f32[8,512,17]{2,1,0:T(8,128)S(1)} fusion(f32[8,512]{1,0:T(8,128)S(1)} %get-tuple-element.34, f32[17]{0:T(128)S(1)} %iota_convert_fusion), kind=kLoop, calls=%fused_computation.57 | loop fusion | flops 69632 | bytes 294980 | tf_op jit(solution)/shard_map/vmap()/cos | solution.py:52
  43.4 0.0 copy-done
  43.4 3.9 %fusion.68 = f32[8,17,512]{2,1,0:T(8,128)S(1)} fusion(f32[8,512,512]{2,1,0:T(8,128)S(1)} %fusion.warped_ref, f32[8,512]{1,0:T(8,128)S(1)} %get-tuple-element.34, f32[17]{0:T(128)S(1)} %iota_convert_fusion), kind=kOutput, calls=%fused_computation.68 | convolution fusion | flops 213979136 | bytes 8683588 | tf_op jit(solution)/shard_map/mtp,mpq->mtq/dot_general | solution.py:66
  47.3 46.3 %all-gather.2.cloned.1.call-done = f32[128,64,512]{2,1,0:T(8,128)} async-done(((f32[1,64,512]{2,1,0:T(8,128)}), f32[128,64,512]{2,1,0:T(8,128)}) %all-gather.2.cloned.1.call-update) | async-done | bytes 16777232 | tf_op jit(solution)/shard_map/all_gather | solution.py:180
  93.6 9.4 %shard_map.86 = f32[8,24,24]{2,1,0:T(8,128)} custom-call(s32[8]{0:T(128)} %patch_of.3, f32[16,512,512]{2,1,0:T(8,128)} %bitcast.59, bf16[8,2,24,512]{3,2,1,0:T(8,128)(2,1)} %copy.14.row_ref, f32[8,24,512]{2,1,0:T(8,128)} %pad.18.col_ref), custom_call_target="tpu_custom_call" | custom-call | flops 105381888 | bytes 9175040 | tf_op jit(solution)/shard_map/pallas_call | solution.py:96
  103.0 2.8 %convolution_subtract_fusion = f32[8,17,17]{2,1,0:T(8,128)S(1)} fusion(f32[8,17,512]{2,1,0:T(8,128)S(1)} %fusion.68, f32[8,512]{1,0:T(8,128)S(1)} %get-tuple-element.33, f32[17]{0:T(128)S(1)} %iota_convert_fusion, f32[8,24,24]{2,1,0:T(8,128)} %shard_map.86), kind=kOutput, calls=%fused_computation.58 | convolution fusion | flops 14276872 | bytes 313476 | tf_op jit(solution)/shard_map/mtq,muq->mtu/dot_general | solution.py:67
  105.7 0.2 fusion.69
  105.9 1.3 collective-permute-start
  107.2 2.7 %collective-permute-start.1 = (f32[4,17,17]{2,0,1:T(4,128)S(1)}, f32[4,17,17]{2,0,1:T(4,128)S(1)}, u32[]{:S(2)}, u32[]{:S(2)}) collective-permute-start(f32[4,17,17]{2,0,1:T(4,128)S(1)} %fusion.69), channel_id=1, source_target_pairs={{0,2},{1,3},{2,0},{3,1},{4,6},{5,7},{6,4},{7,5},{8,10},{9,11},{10,... | collective-permute-start | bytes 13880 | tf_op jit(solution)/shard_map/ppermute | solution.py:167
  109.9 1.4 collective-permute-start.2
  111.3 1.5 %pad.16.rows_ref = f32[8,512,24]{2,1,0:T(8,128)} pad(f32[8,512,17]{2,1,0:T(8,128)S(1)} %multiply_cosine_fusion, f32[]{:T(128)} %constant.137.clone.1), padding=0_0x0_0x0_7 | pad | bytes 671748 | tf_op jit(solution)/shard_map/jit(_pad)/pad | solution.py:134
  112.8 0.0 collective-permute-done
  112.8 0.0 collective-permute-done.1
  112.8 1.0 collective-permute-done.2
  113.9 1.0 collective-permute-start.3
  114.9 2.1 %collective-permute-start.4 = (f32[4,17,17]{2,0,1:T(4,128)S(1)}, f32[4,17,17]{2,0,1:T(4,128)S(1)}, u32[]{:S(2)}, u32[]{:S(2)}) collective-permute-start(f32[4,17,17]{2,0,1:T(4,128)S(1)} %fusion.182), channel_id=1, source_target_pairs={{0,8},{4,12},{8,0},{12,4},{1,9},{5,13},{9,1},{13,5},{2,10},{6,14},... | collective-permute-start | bytes 13880 | tf_op jit(solution)/shard_map/ppermute | solution.py:167
  117.0 1.9 %collective-permute-start.5 = (f32[4,17,17]{2,0,1:T(4,128)S(1)}, f32[4,17,17]{2,0,1:T(4,128)S(1)}, u32[]{:S(2)}, u32[]{:S(2)}) collective-permute-start(f32[4,17,17]{2,0,1:T(4,128)S(1)} %fusion.182), channel_id=1, source_target_pairs={{0,12},{4,0},{8,4},{12,8},{1,13},{5,1},{9,5},{13,9},{2,14},{6,2},{... | collective-permute-start | bytes 13880 | tf_op jit(solution)/shard_map/ppermute | solution.py:167
  119.0 0.1 collective-permute-done.3
  119.1 1.2 collective-permute-done.4
  120.3 0.6 collective-permute-done.5
  121.1 0.0 copy-start.1
  121.1 0.6 gather_fusion
  121.6 0.1 broadcast_select_fusion
  121.7 0.6 pad.19.coef_ref
  122.4 15.6 %shard_map.87 = f32[8,512,512]{2,1,0:T(8,128)} custom-call(s32[8]{0:T(128)} %patch_of.3, f32[8,512,512]{2,1,0:T(8,128)} %copy-done, f32[16,512,512]{2,1,0:T(8,128)} %bitcast.60, f32[8,512,24]{2,1,0:T(8,128)} %pad.16.rows_ref, f32[8,24,24]{2,1,0:T(8,128)} %pad.19.coef_ref, f32[8,24,512]{2,1,0:T(8,128)} %pad.18.col_ref), custom_call_target="tpu_custom_call" | custom-call | flops 105381888 | bytes 25165824 | tf_op jit(solution)/shard_map/pallas_call | solution.py:138
  138.0 0.0 copy-done.1
  (16 shorter events, 0.3 us)
Async XLA Ops:
  7.2 86.4 %all-gather.2.cloned.1.call-start = ((), (), s32[]{:S(2)}) async-start(), calls=%async_computation | async-start | bytes 16908288 | tf_op jit(solution)/shard_map/all_gather | solution.py:180
  21.3 10.9 %copy-start.2 = (s32[8,2]{0,1:T(2,128)S(1)}, s32[8,2]{0,1:T(2,128)}, u32[]{:S(2)}) copy-start(s32[8,2]{0,1:T(2,128)} %param.12) | copy-start | bytes 196
  21.3 15.3 %copy-start.3 = (s32[8]{0:T(128)S(1)}, s32[8]{0:T(128)}, u32[]{:S(2)}) copy-start(s32[8]{0:T(128)} %param.11) | copy-start | bytes 100
  32.2 11.2 %copy-start = (f32[8,512,512]{2,1,0:T(8,128)}, f32[8,512,512]{2,1,0:T(8,128)S(1)}, u32[]{:S(2)}) copy-start(f32[8,512,512]{2,1,0:T(8,128)S(1)} %fusion.warped_ref) | copy-start | bytes 25165828
  105.9 6.9 %collective-permute-start = (f32[4,17,17]{2,0,1:T(4,128)S(1)}, f32[4,17,17]{2,0,1:T(4,128)S(1)}, u32[]{:S(2)}, u32[]{:S(2)}) collective-permute-start(f32[4,17,17]{2,0,1:T(4,128)S(1)} %fusion.69), channel_id=1, source_target_pairs={{0,1},{1,2},{2,3},{3,0},{4,5},{5,6},{6,7},{7,4},{8,9},{9,10},{10,1... | collective-permute-start | bytes 13880 | tf_op jit(solution)/shard_map/ppermute | solution.py:167
  107.2 5.6 %collective-permute-start.1 = (f32[4,17,17]{2,0,1:T(4,128)S(1)}, f32[4,17,17]{2,0,1:T(4,128)S(1)}, u32[]{:S(2)}, u32[]{:S(2)}) collective-permute-start(f32[4,17,17]{2,0,1:T(4,128)S(1)} %fusion.69), channel_id=1, source_target_pairs={{0,2},{1,3},{2,0},{3,1},{4,6},{5,7},{6,4},{7,5},{8,10},{9,11},{10,... | collective-permute-start | bytes 13880 | tf_op jit(solution)/shard_map/ppermute | solution.py:167
  109.9 3.9 %collective-permute-start.2 = (f32[4,17,17]{2,0,1:T(4,128)S(1)}, f32[4,17,17]{2,0,1:T(4,128)S(1)}, u32[]{:S(2)}, u32[]{:S(2)}) collective-permute-start(f32[4,17,17]{2,0,1:T(4,128)S(1)} %fusion.69), channel_id=1, source_target_pairs={{0,3},{1,0},{2,1},{3,2},{4,7},{5,4},{6,5},{7,6},{8,11},{9,8},{10,9... | collective-permute-start | bytes 13880 | tf_op jit(solution)/shard_map/ppermute | solution.py:167
  113.9 5.2 %collective-permute-start.3 = (f32[4,17,17]{2,0,1:T(4,128)S(1)}, f32[4,17,17]{2,0,1:T(4,128)S(1)}, u32[]{:S(2)}, u32[]{:S(2)}) collective-permute-start(f32[4,17,17]{2,0,1:T(4,128)S(1)} %fusion.182), channel_id=1, source_target_pairs={{0,4},{4,8},{8,12},{12,0},{1,5},{5,9},{9,13},{13,1},{2,6},{6,10},{... | collective-permute-start | bytes 13880 | tf_op jit(solution)/shard_map/ppermute | solution.py:167
  114.9 5.4 %collective-permute-start.4 = (f32[4,17,17]{2,0,1:T(4,128)S(1)}, f32[4,17,17]{2,0,1:T(4,128)S(1)}, u32[]{:S(2)}, u32[]{:S(2)}) collective-permute-start(f32[4,17,17]{2,0,1:T(4,128)S(1)} %fusion.182), channel_id=1, source_target_pairs={{0,8},{4,12},{8,0},{12,4},{1,9},{5,13},{9,1},{13,5},{2,10},{6,14},... | collective-permute-start | bytes 13880 | tf_op jit(solution)/shard_map/ppermute | solution.py:167
  117.0 3.9 %collective-permute-start.5 = (f32[4,17,17]{2,0,1:T(4,128)S(1)}, f32[4,17,17]{2,0,1:T(4,128)S(1)}, u32[]{:S(2)}, u32[]{:S(2)}) collective-permute-start(f32[4,17,17]{2,0,1:T(4,128)S(1)} %fusion.182), channel_id=1, source_target_pairs={{0,12},{4,0},{8,4},{12,8},{1,13},{5,1},{9,5},{13,9},{2,14},{6,2},{... | collective-permute-start | bytes 13880 | tf_op jit(solution)/shard_map/ppermute | solution.py:167
  121.1 17.0 %copy-start.1 = (f32[4,17,17]{2,0,1:T(4,128)}, f32[4,17,17]{2,0,1:T(4,128)S(1)}, u32[]{:S(2)}) copy-start(f32[4,17,17]{2,0,1:T(4,128)S(1)} %multiply_bitcast_fusion) | copy-start | bytes 13876
Sparse Core Ops, SparseCore 0:
  11.1 82.4 all-gather.1
